TPU v7x, 128 devices: a whole 4x4x4 slice. The times are simulated.
128 devices in a mesh: dp: 16 (over y, x_lo, core), ctx: 8 (over z, x_hi).
Axes of the slice: x: 4 (x_hi: 2, x_lo: 2; x = x_hi * 2 + x_lo), y: 4, z: 4, core: 2. Of those that a mesh axis runs over, the one named last changes fastest.
Arguments:
- query_in: bfloat16 [32768, 2048], P(('dp', 'ctx')), may hold values from -16 to 16
- key_in: bfloat16 [32768, 512], P(('dp', 'ctx')), may hold values from -16 to 16
- value_in: bfloat16 [32768, 512], P(('dp', 'ctx')), may hold values from -6 to 6
- grad_out: bfloat16 [32768, 2048], P(('dp', 'ctx')), may hold values from -6 to 6
- target: int32 [32768], P(('dp', 'ctx')), may hold values from 0 to 32767, as said below
- span_order: int32 [16, 16], P('dp'), may hold values from 0 to 15, each once within a row
- doc_ids: int32 [16, 2048], P('dp', 'ctx'), may hold values from 0 to 7, never falling along the last dimension, each value on 1 to 1024 neighbouring positions
Outputs:
- grad_query: float32 [32768, 2048], P(('dp', 'ctx'))
- grad_key: float32 [32768, 512], P(('dp', 'ctx'))
- grad_value: float32 [32768, 512], P(('dp', 'ctx'))
Inputs may be any that keep to these rules, and one draw needn't show every extreme that they name: target is a permutation of the 32768 packed rows; of the 256 rows of one device at most 4 go to any one block of 256 packed rows, and exactly 4 go to some block. `span_order`: each row names every span once. `doc_ids`: each document is one run of 1 to 1024 positions; numbers never fall along a pack.
All inputs are finite; a program needn't handle non-finite values.
Results may differ from a plain program's by a relative error of at most 0.035.
Values may be sent and summed in bfloat16 or wider, within the bound.
No kernel may reach another device: no remote copies, remote signals or barrier semaphores. Data moves between devices by JAX's collectives and lax.ppermute only.
A program may use at most 128 MiB of HBM per device.

v0:
```python
import jax
import jax.numpy as jnp
from jax import lax
from jax.sharding import PartitionSpec as P
from jax.experimental import pallas as pl
from jax.experimental.pallas import tpu as pltpu

HQ = 16
HK = 4
DH = 128


CHUNK = 256


def attention_kernel(
    list_ref, count_ref, q_ref, g_ref, k_ref, v_ref, qpos_ref, qdoc_ref, kpos_ref, kdoc_ref, dq_ref, dk_ref, dv_ref
):
    scale = DH ** (-0.5)
    rows = q_ref.shape[0]
    count = count_ref[0]
    dk_ref[...] = jnp.zeros(dk_ref.shape, jnp.float32)
    dv_ref[...] = jnp.zeros(dv_ref.shape, jnp.float32)
    qpos = qpos_ref[...]
    qdoc = qdoc_ref[...]

    def chunk(i):
        start = pl.multiple_of(list_ref[i] * CHUNK, CHUNK)
        kp = kpos_ref[:, pl.ds(start, CHUNK)]
        kd = kdoc_ref[:, pl.ds(start, CHUNK)]
        allowed = (kp <= qpos) & (kd == qdoc)
        return start, k_ref[pl.ds(start, CHUNK), :], v_ref[pl.ds(start, CHUNK), :], allowed

    def scores(q, kb, allowed):
        s = lax.dot_general(q, kb, (((1,), (1,)), ((), ())), preferred_element_type=jnp.float32) * scale
        return jnp.where(allowed, s, -jnp.inf)

    for g in range(q_ref.shape[1] // DH):
        cols = slice(g * DH, (g + 1) * DH)
        q = q_ref[:, cols]
        gr = g_ref[:, cols]

        def stats(i, carry):
            m, l = carry
            _, kb, _, allowed = chunk(i)
            s = scores(q, kb, allowed)
            m_new = jnp.maximum(m, jnp.max(s, axis=1, keepdims=True))
            l = l * jnp.exp(m - m_new) + jnp.sum(jnp.exp(s - m_new), axis=1, keepdims=True)
            return m_new, l

        m, l = lax.fori_loop(
            0, count, stats, (jnp.full((rows, 1), -1e30, jnp.float32), jnp.zeros((rows, 1), jnp.float32))
        )
        lse = m + jnp.log(l)

        def forward(i, o):
            _, kb, vb, allowed = chunk(i)
            p = jnp.exp(scores(q, kb, allowed) - lse).astype(jnp.bfloat16)
            return o + jnp.dot(p, vb, preferred_element_type=jnp.float32)

        o = lax.fori_loop(0, count, forward, jnp.zeros((rows, DH), jnp.float32))
        delta = jnp.sum(
            gr.astype(jnp.float32) * o.astype(jnp.bfloat16).astype(jnp.float32), axis=1, keepdims=True
        )

        def backward(i, dq):
            start, kb, vb, allowed = chunk(i)
            p = jnp.exp(scores(q, kb, allowed) - lse)
            dp = lax.dot_general(gr, vb, (((1,), (1,)), ((), ())), preferred_element_type=jnp.float32)
            ds = (p * (dp - delta)).astype(jnp.bfloat16)
            dk_ref[pl.ds(start, CHUNK), :] += lax.dot_general(
                ds, q, (((0,), (0,)), ((), ())), preferred_element_type=jnp.float32
            )
            dv_ref[pl.ds(start, CHUNK), :] += lax.dot_general(
                p.astype(jnp.bfloat16), gr, (((0,), (0,)), ((), ())), preferred_element_type=jnp.float32
            )
            return dq + jnp.dot(ds, kb, preferred_element_type=jnp.float32)

        dq = lax.fori_loop(0, count, backward, jnp.zeros((rows, DH), jnp.float32))
        dq_ref[:, cols] = dq * scale
    dk_ref[...] = dk_ref[...] * scale


def attention(chunk_list, chunk_count, query, grad, keys, values, qpos, qdoc, kpos, kdoc, interpret=False):
    rows, width = query.shape
    keys_len, kv_width = keys.shape
    groups = width // kv_width
    heads = kv_width // DH
    q_spec = pl.BlockSpec((rows, groups * DH), lambda c, *_: (0, c))
    k_spec = pl.BlockSpec((keys_len, DH), lambda c, *_: (0, c))
    col_spec = pl.BlockSpec((rows, 1), lambda c, *_: (0, 0))
    row_spec = pl.BlockSpec((1, keys_len), lambda c, *_: (0, 0))
    return pl.pallas_call(
        attention_kernel,
        grid_spec=pltpu.PrefetchScalarGridSpec(
            num_scalar_prefetch=2,
            grid=(heads,),
            in_specs=[q_spec, q_spec, k_spec, k_spec, col_spec, col_spec, row_spec, row_spec],
            out_specs=[q_spec, k_spec, k_spec],
        ),
        out_shape=[
            jax.ShapeDtypeStruct((rows, width), jnp.float32),
            jax.ShapeDtypeStruct((keys_len, kv_width), jnp.float32),
            jax.ShapeDtypeStruct((keys_len, kv_width), jnp.float32),
        ],
        compiler_params=pltpu.CompilerParams(dimension_semantics=("arbitrary",)),
        interpret=interpret,
    )(chunk_list, chunk_count, query, grad, keys, values, qpos, qdoc, kpos, kdoc)


def visible(query_pos, query_doc, key_pos, key_doc):
    return (key_pos[None, :] <= query_pos[:, None]) & (key_doc[None, :] == query_doc[:, None])


def local(query_in, key_in, value_in, grad_out, target, span_order, doc_ids):
    local_rows = query_in.shape[0]
    devices = lax.axis_size(("dp", "ctx"))
    ctx_size = lax.axis_size("ctx")
    capacity = local_rows // devices + 2
    groups = HQ // HK
    score_scale = DH ** (-0.5)
    q_cols = query_in.shape[1]
    k_cols = key_in.shape[1]
    owners = target // local_rows
    onehot = (owners[:, None] == jnp.arange(devices, dtype=jnp.int32)[None, :]).astype(jnp.int32)
    earlier = jnp.cumsum(onehot, axis=0) - onehot
    slot_ids = owners * capacity + jnp.sum(earlier * onehot, axis=1)

    place_col = jnp.zeros((local_rows, 128), jnp.bfloat16).at[:, 0].set(
        (target % local_rows + 1).astype(jnp.bfloat16)
    )

    def exchange(payload):
        width = payload.shape[1]
        holder = jnp.zeros((devices * capacity, width), payload.dtype).at[slot_ids].set(payload)
        return lax.all_to_all(
            holder.reshape(devices, capacity, width), ("dp", "ctx"), split_axis=0, concat_axis=0, tiled=True
        ).reshape(devices * capacity, width)

    got_kv = exchange(jnp.concatenate([key_in, value_in, place_col], axis=1))
    got_qg = exchange(jnp.concatenate([query_in, grad_out], axis=1))
    arrived = got_kv[:, 2 * k_cols].astype(jnp.int32) - 1
    landing = jnp.where(arrived >= 0, arrived, local_rows)

    def unpack(values):
        return jnp.zeros((local_rows, values.shape[1]), values.dtype).at[landing].set(values, mode="drop")

    kv_rows = unpack(got_kv[:, : 2 * k_cols])
    qg_rows = unpack(got_qg)
    query = qg_rows[:, :q_cols]
    grad_rows = qg_rows[:, q_cols:]

    span_rows = local_rows // 2
    span_seq = span_order[0]
    pack_len = local_rows * ctx_size
    positions = (
        span_seq[:, None] * span_rows + jnp.arange(span_rows, dtype=jnp.int32)[None, :]
    ).reshape(-1)
    ctx_index = lax.axis_index("ctx")
    own_pos = lax.dynamic_slice_in_dim(positions, ctx_index * local_rows, local_rows)
    doc_col = jnp.zeros((local_rows, 128), jnp.bfloat16).at[:, 0].set(doc_ids[0].astype(jnp.bfloat16))
    gathered = lax.all_gather(
        jnp.concatenate([kv_rows, doc_col], axis=1), "ctx", axis=0, tiled=True
    )
    seq_docs = gathered[:, 2 * k_cols].astype(jnp.int32)
    doc_all = seq_docs.reshape(2 * ctx_size, span_rows)[span_seq].reshape(-1)
    own_docs = lax.dynamic_slice_in_dim(doc_all, ctx_index * local_rows, local_rows)
    keys_all = gathered[:, :k_cols]
    values_all = gathered[:, k_cols : 2 * k_cols]
    num_chunks = pack_len // CHUNK
    allowed_all = visible(own_pos, own_docs, positions, doc_all)
    active = jnp.any(allowed_all.reshape(local_rows, num_chunks, CHUNK), axis=(0, 2))
    chunk_count = jnp.sum(active.astype(jnp.int32)).reshape(1)
    rank = jnp.cumsum(active.astype(jnp.int32)) - 1
    chunk_list = (
        jnp.zeros((num_chunks,), jnp.int32)
        .at[jnp.where(active, rank, num_chunks)]
        .set(jnp.arange(num_chunks, dtype=jnp.int32), mode="drop")
    )
    dquery_full, dkey_all, dvalue_all = attention(
        chunk_list,
        chunk_count,
        query,
        grad_rows,
        keys_all,
        values_all,
        own_pos.reshape(local_rows, 1),
        own_docs.reshape(local_rows, 1),
        positions.reshape(1, pack_len),
        doc_all.reshape(1, pack_len),
    )
    partial = jnp.concatenate([dkey_all, dvalue_all], axis=1).astype(jnp.bfloat16)
    summed_kv = jnp.sum(
        lax.all_to_all(
            partial.reshape(ctx_size, local_rows, 2 * k_cols), "ctx", split_axis=0, concat_axis=0, tiled=True
        ).astype(jnp.float32),
        axis=0,
    )
    source_rows = jnp.where(arrived >= 0, arrived, 0)
    result = jnp.concatenate([dquery_full.astype(jnp.bfloat16), summed_kv.astype(jnp.bfloat16)], axis=1)
    back = lax.all_to_all(
        result[source_rows].reshape(devices, capacity, q_cols + 2 * k_cols),
        ("dp", "ctx"),
        split_axis=0,
        concat_axis=0,
        tiled=True,
    ).reshape(devices * capacity, q_cols + 2 * k_cols)[slot_ids].astype(jnp.float32)
    return (back[:, :q_cols], back[:, q_cols : q_cols + k_cols], back[:, q_cols + k_cols :])


def solution(mesh):
    placed = (
        P(("dp", "ctx"), None),
        P(("dp", "ctx"), None),
        P(("dp", "ctx"), None),
        P(("dp", "ctx"), None),
        P(("dp", "ctx")),
        P("dp", None),
        P("dp", "ctx"),
    )
    return jax.shard_map(
        local,
        mesh=mesh,
        in_specs=placed,
        out_specs=(P(("dp", "ctx"), None), P(("dp", "ctx"), None), P(("dp", "ctx"), None)),
        check_vma=False,
    )
```

profile of v0, /device:TPU:1, one launch (start us, length us, event | category | flops | bytes accessed | tf_op | source)
XLA Modules:
  0.0 471.2 jit_solution(2825704551105068590)
XLA Ops:
  15.6 11.5 %all-to-all-start = ((bf16[128,4,1152]{2,1,0:T(4,128)(2,1)}), bf16[128,4,1152]{2,1,0:T(4,128)(2,1)S(1)}, u32[]{:S(2)}, u32[]{:S(2)}) async-start(bf16[128,4,1152]{2,1,0:T(4,128)(2,1)} %reshape.250), calls=%async_computation | async-start | bytes 2359296 | tf_op jit(solution)/shard_map/all_to_all | solution.py:136
  28.0 20.0 %all-to-all-done = bf16[128,4,1152]{2,1,0:T(4,128)(2,1)S(1)} async-done(((bf16[128,4,1152]{2,1,0:T(4,128)(2,1)}), bf16[128,4,1152]{2,1,0:T(4,128)(2,1)S(1)}, u32[]{:S(2)}, u32[]{:S(2)}) %all-to-all-start) | async-done | bytes 1179680 | tf_op jit(solution)/shard_map/all_to_all | solution.py:136
  48.5 2.8 scatter_custom_fusion.1
  52.8 6.1 %scatter_custom_fusion.3 = bf16[512,4096]{1,0:T(8,128)(2,1)} fusion(s32[256]{0:T(256)S(1)} %compare_select_fusion.4, bf16[256,2048]{1,0:T(8,128)(2,1)S(1)} %copy-done.2, bf16[]{:T(256)} %constant.130, bf16[256,2048]{1,0:T(8,128)(2,1)S(1)} %copy-done.3, bf16[]{:T(256)} %constant.108.clone.1), kind=kCustom, calls=%fused_computation.9 | custom fusion | flops 4194304 | bytes 6291460 | tf_op jit(solution)/shard_map/scatter | solution.py:135
  58.8 7.2 %reshape.255 = bf16[128,4,4096]{2,1,0:T(4,128)(2,1)} reshape(bf16[512,4096]{1,0:T(8,128)(2,1)} %scatter_custom_fusion.3) | data formatting | bytes 8388608 | tf_op jit(solution)/shard_map/reshape | solution.py:137
  66.1 5.1 %all-to-all-start.1 = ((bf16[128,4,4096]{2,1,0:T(4,128)(2,1)}), bf16[128,4,4096]{2,1,0:T(4,128)(2,1)}, u32[]{:S(2)}, u32[]{:S(2)}) async-start(bf16[128,4,4096]{2,1,0:T(4,128)(2,1)} %reshape.255), calls=%async_computation.1 | async-start | bytes 8388608 | tf_op jit(solution)/shard_map/all_to_all | solution.py:136
  73.1 50.1 %all-to-all-done.1 = bf16[128,4,4096]{2,1,0:T(4,128)(2,1)} async-done(((bf16[128,4,4096]{2,1,0:T(4,128)(2,1)}), bf16[128,4,4096]{2,1,0:T(4,128)(2,1)}, u32[]{:S(2)}, u32[]{:S(2)}) %all-to-all-start.1) | async-done | bytes 4194336 | tf_op jit(solution)/shard_map/all_to_all | solution.py:136
  123.2 7.1 %reshape.320 = bf16[512,4096]{1,0:T(8,128)(2,1)} reshape(bf16[128,4,4096]{2,1,0:T(4,128)(2,1)} %all-to-all-done.1) | data formatting | bytes 8388608 | tf_op jit(solution)/shard_map/reshape | solution.py:138
  130.3 8.2 %scatter_custom_fusion.4 = bf16[256,4096]{1,0:T(8,128)(2,1)S(1)} fusion(s32[512]{0:T(512)S(1)} %get-tuple-element.34, bf16[512,4096]{1,0:T(8,128)(2,1)} %reshape.320, bf16[]{:T(256)} %constant.108.clone.1), kind=kCustom, calls=%fused_computation.22 | custom fusion | bytes 2097664 | tf_op jit(solution)/shard_map/scatter | solution.py:146
  140.0 25.3 %all-gather.2.cloned.1.call-done = bf16[2048,1152]{1,0:T(8,128)(2,1)} async-done(((bf16[256,1152]{1,0:T(8,128)(2,1)}), bf16[2048,1152]{1,0:T(8,128)(2,1)}) %all-gather.2.cloned.1.call-update) | async-done | bytes 4718608 | tf_op jit(solution)/shard_map/all_gather | solution.py:162
  171.4 4.5 fusion.38
  175.9 71.6 %shard_map.94 = (f32[256,2048]{1,0:T(8,128)}, f32[2048,512]{1,0:T(8,128)}, f32[2048,512]{1,0:T(8,128)}) custom-call(s32[8]{0:T(128)} %scatter_custom_fusion.2.list_ref, s32[1]{0:T(128)} %bitcast.13.count_ref, bf16[256,2048]{1,0:T(8,128)(2,1)} %get-tuple-element.38.q_ref, bf16[256,2048]{1,0:T(8,128)(2,1)} %get-tuple-element.37.g_ref, ...), custom_call_target="tpu_custom_call" | custom-call | tf_op jit(solution)/shard_map/pallas_call | solution.py:93
  247.5 2.6 convert.10
  251.2 2.6 pad_maximum_fusion
  253.8 65.2 %all-to-all-start.2 = ((bf16[8,256,1024]{2,1,0:T(8,128)(2,1)}), bf16[8,256,1024]{2,1,0:T(8,128)(2,1)}, u32[]{:S(2)}, u32[]{:S(2)}) async-start(bf16[8,256,1024]{2,1,0:T(8,128)(2,1)} %pad_maximum_fusion), calls=%async_computation.2 | async-start | bytes 8388608 | tf_op jit(solution)/shard_map/all_to_all | solution.py:194
  320.8 27.2 %all-to-all-done.2 = bf16[8,256,1024]{2,1,0:T(8,128)(2,1)} async-done(((bf16[8,256,1024]{2,1,0:T(8,128)(2,1)}), bf16[8,256,1024]{2,1,0:T(8,128)(2,1)}, u32[]{:S(2)}, u32[]{:S(2)}) %all-to-all-start.2) | async-done | bytes 4194336 | tf_op jit(solution)/shard_map/all_to_all | solution.py:194
  348.0 3.1 reduce_sum.32
  351.2 3.9 gather_fusion.1
  355.0 6.1 %reshape.257 = bf16[128,4,3072]{2,1,0:T(4,128)(2,1)} reshape(bf16[512,3072]{1,0:T(8,128)(2,1)} %gather_fusion.1) | data formatting | bytes 6291456 | tf_op jit(solution)/shard_map/reshape | solution.py:202
  361.2 51.1 %all-to-all-start.3 = ((bf16[128,4,3072]{2,1,0:T(4,128)(2,1)}), bf16[128,4,3072]{2,1,0:T(4,128)(2,1)}, u32[]{:S(2)}, u32[]{:S(2)}) async-start(bf16[128,4,3072]{2,1,0:T(4,128)(2,1)} %reshape.257), calls=%async_computation.3 | async-start | bytes 6291456 | tf_op jit(solution)/shard_map/all_to_all | solution.py:201
  412.2 40.9 %all-to-all-done.3 = bf16[128,4,3072]{2,1,0:T(4,128)(2,1)} async-done(((bf16[128,4,3072]{2,1,0:T(4,128)(2,1)}), bf16[128,4,3072]{2,1,0:T(4,128)(2,1)}, u32[]{:S(2)}, u32[]{:S(2)}) %all-to-all-start.3) | async-done | bytes 3145760 | tf_op jit(solution)/shard_map/all_to_all | solution.py:201
  453.1 4.5 reshape.258
  457.6 2.7 gather_fusion.2
  460.4 2.9 slice.90
  (68 shorter events, 24.6 us)
Async XLA Ops:
  14.4 12.7 %copy-start.5 = (s32[1,256]{1,0:T(1,128)S(1)}, s32[1,256]{1,0:T(1,128)}, u32[]{:S(2)}) copy-start(s32[1,256]{1,0:T(1,128)} %param.17) | copy-start | bytes 3076
  15.6 32.4 %all-to-all-start = ((bf16[128,4,1152]{2,1,0:T(4,128)(2,1)}), bf16[128,4,1152]{2,1,0:T(4,128)(2,1)S(1)}, u32[]{:S(2)}, u32[]{:S(2)}) async-start(bf16[128,4,1152]{2,1,0:T(4,128)(2,1)} %reshape.250), calls=%async_computation | async-start | bytes 2359296 | tf_op jit(solution)/shard_map/all_to_all | solution.py:136
  27.1 138.3 %all-gather.2.cloned.1.call-start = ((), (), s32[]{:S(2)}) async-start(), calls=%async_computation.4 | async-start | bytes 5308416 | tf_op jit(solution)/shard_map/all_gather | solution.py:162
  48.3 4.0 copy-start.2
  51.3 1.4 copy-start.3
  66.1 5.1 %copy-start.6 = (s32[1,16]{1,0:T(1,128)S(1)}, s32[1,16]{1,0:T(1,128)}, u32[]{:S(2)}) copy-start(s32[1,16]{1,0:T(1,128)} %param.16) | copy-start | bytes 196
  66.1 57.1 %all-to-all-start.1 = ((bf16[128,4,4096]{2,1,0:T(4,128)(2,1)}), bf16[128,4,4096]{2,1,0:T(4,128)(2,1)}, u32[]{:S(2)}, u32[]{:S(2)}) async-start(bf16[128,4,4096]{2,1,0:T(4,128)(2,1)} %reshape.255), calls=%async_computation.1 | async-start | bytes 8388608 | tf_op jit(solution)/shard_map/all_to_all | solution.py:136
  167.3 8.6 %copy-start.4 = (s32[16,128]{1,0:T(8,128)}, s32[16,128]{1,0:T(8,128)S(1)}, u32[]{:S(2)}) copy-start(s32[16,128]{1,0:T(8,128)S(1)} %gather_fusion) | copy-start | bytes 24580
  247.5 3.4 copy-start.1
  253.8 94.2 %all-to-all-start.2 = ((bf16[8,256,1024]{2,1,0:T(8,128)(2,1)}), bf16[8,256,1024]{2,1,0:T(8,128)(2,1)}, u32[]{:S(2)}, u32[]{:S(2)}) async-start(bf16[8,256,1024]{2,1,0:T(8,128)(2,1)} %pad_maximum_fusion), calls=%async_computation.2 | async-start | bytes 8388608 | tf_op jit(solution)/shard_map/all_to_all | solution.py:194
  361.2 92.0 %all-to-all-start.3 = ((bf16[128,4,3072]{2,1,0:T(4,128)(2,1)}), bf16[128,4,3072]{2,1,0:T(4,128)(2,1)}, u32[]{:S(2)}, u32[]{:S(2)}) async-start(bf16[128,4,3072]{2,1,0:T(4,128)(2,1)} %reshape.257), calls=%async_computation.3 | async-start | bytes 6291456 | tf_op jit(solution)/shard_map/all_to_all | solution.py:201
  460.4 2.9 copy-start
Sparse Core Ops, SparseCore 0:
  52.3 112.9 all-gather.1
where the time goes:
time: 473 us; the launch traced here: 471 us
  waiting for transfers between devices  164 us (35%)
  starting transfers between devices  133 us (28%)
  Pallas kernels  71.6 us (15%)
  local copies, waits for them, and re-layouts  59.4 us (13%)
  other arithmetic  29.4 us (6%)
  between operations  14.3 us (3%)
    pallas_call x1, Pallas kernels, attention(): pl.pallas_call(attention_kernel, grid_spec=pltpu.PrefetchScalarGridSpec(n...  71.6 us
    all_to_all x2, waiting for transfers between devices, exchange(): lax.all_to_all(holder.reshape(devices, capacity, width), ('dp', 'ctx'), s...  70.1 us
    all_to_all x1, starting transfers between devices, local(): lax.all_to_all(partial.reshape(ctx_size, local_rows, 2 * k_cols), 'ctx',...  65.2 us
    all_to_all x1, starting transfers between devices, local(): lax.all_to_all(result[source_rows].reshape(devices, capacity, q_cols + 2...  51.1 us
    all_to_all x1, waiting for transfers between devices, local(): lax.all_to_all(result[source_rows].reshape(devices, capacity, q_cols + 2...  40.9 us
    all_to_all x1, waiting for transfers between devices, local(): lax.all_to_all(partial.reshape(ctx_size, local_rows, 2 * k_cols), 'ctx',...  27.2 us
    all_gather x1, waiting for transfers between devices, local(): lax.all_gather(jnp.concatenate([kv_rows, doc_col], axis=1), 'ctx', axis=0...  25.3 us
    all_to_all x2, starting transfers between devices, exchange(): lax.all_to_all(holder.reshape(devices, capacity, width), ('dp', 'ctx'), s...  16.6 us
  transfers between devices with their start and end apart: 5, of which 5 were waited for; matrix products, arithmetic and copies ran while one was open for 7% of the time, Pallas kernels for 0%

commit v1 on v0

--- a/solution.py
+++ b/solution.py
@@ -10,30 +10,29 @@
 DH = 128
 
 
-CHUNK = 256
+SPAN_ROWS = 128
 
 
 def attention_kernel(
-    list_ref, count_ref, q_ref, g_ref, k_ref, v_ref, qpos_ref, qdoc_ref, kpos_ref, kdoc_ref, dq_ref, dk_ref, dv_ref
+    list_ref, count_ref, q_ref, g_ref, k_ref, v_ref, qpos_ref, qdoc_ref, kpos_ref, kdoc_ref,
+    dq_ref, dk_ref, dv_ref, tiles_ref,
 ):
     scale = DH ** (-0.5)
     rows = q_ref.shape[0]
-    count = count_ref[0]
-    dk_ref[...] = jnp.zeros(dk_ref.shape, jnp.float32)
-    dv_ref[...] = jnp.zeros(dv_ref.shape, jnp.float32)
+    span = pl.program_id(1)
+    spans = list_ref.shape[0] // pl.num_programs(1)
+    count = count_ref[span]
+
+    @pl.when(span == 0)
+    def _():
+        dk_ref[...] = jnp.zeros(dk_ref.shape, jnp.float32)
+        dv_ref[...] = jnp.zeros(dv_ref.shape, jnp.float32)
+
     qpos = qpos_ref[...]
     qdoc = qdoc_ref[...]
 
-    def chunk(i):
-        start = pl.multiple_of(list_ref[i] * CHUNK, CHUNK)
-        kp = kpos_ref[:, pl.ds(start, CHUNK)]
-        kd = kdoc_ref[:, pl.ds(start, CHUNK)]
-        allowed = (kp <= qpos) & (kd == qdoc)
-        return start, k_ref[pl.ds(start, CHUNK), :], v_ref[pl.ds(start, CHUNK), :], allowed
-
-    def scores(q, kb, allowed):
-        s = lax.dot_general(q, kb, (((1,), (1,)), ((), ())), preferred_element_type=jnp.float32) * scale
-        return jnp.where(allowed, s, -jnp.inf)
+    def first_key(i):
+        return pl.multiple_of(list_ref[span * spans + i] * SPAN_ROWS, SPAN_ROWS)
 
     for g in range(q_ref.shape[1] // DH):
         cols = slice(g * DH, (g + 1) * DH)
@@ -42,8 +41,16 @@
 
         def stats(i, carry):
             m, l = carry
-            _, kb, _, allowed = chunk(i)
-            s = scores(q, kb, allowed)
+            start = first_key(i)
+            kp = kpos_ref[:, pl.ds(start, SPAN_ROWS)]
+            kd = kdoc_ref[:, pl.ds(start, SPAN_ROWS)]
+            allowed = (kp <= qpos) & (kd == qdoc)
+            s = lax.dot_general(
+                q, k_ref[pl.ds(start, SPAN_ROWS), :], (((1,), (1,)), ((), ())),
+                preferred_element_type=jnp.float32,
+            ) * scale
+            s = jnp.where(allowed, s, -jnp.inf)
+            tiles_ref[i] = s
             m_new = jnp.maximum(m, jnp.max(s, axis=1, keepdims=True))
             l = l * jnp.exp(m - m_new) + jnp.sum(jnp.exp(s - m_new), axis=1, keepdims=True)
             return m_new, l
@@ -54,9 +61,12 @@
         lse = m + jnp.log(l)
 
         def forward(i, o):
-            _, kb, vb, allowed = chunk(i)
-            p = jnp.exp(scores(q, kb, allowed) - lse).astype(jnp.bfloat16)
-            return o + jnp.dot(p, vb, preferred_element_type=jnp.float32)
+            start = first_key(i)
+            p = jnp.exp(tiles_ref[i] - lse)
+            tiles_ref[i] = p
+            return o + jnp.dot(
+                p.astype(jnp.bfloat16), v_ref[pl.ds(start, SPAN_ROWS), :], preferred_element_type=jnp.float32
+            )
 
         o = lax.fori_loop(0, count, forward, jnp.zeros((rows, DH), jnp.float32))
         delta = jnp.sum(
@@ -64,48 +74,54 @@
         )
 
         def backward(i, dq):
-            start, kb, vb, allowed = chunk(i)
-            p = jnp.exp(scores(q, kb, allowed) - lse)
+            start = first_key(i)
+            kb = k_ref[pl.ds(start, SPAN_ROWS), :]
+            vb = v_ref[pl.ds(start, SPAN_ROWS), :]
+            p = tiles_ref[i]
             dp = lax.dot_general(gr, vb, (((1,), (1,)), ((), ())), preferred_element_type=jnp.float32)
             ds = (p * (dp - delta)).astype(jnp.bfloat16)
-            dk_ref[pl.ds(start, CHUNK), :] += lax.dot_general(
+            dk_ref[pl.ds(start, SPAN_ROWS), :] += lax.dot_general(
                 ds, q, (((0,), (0,)), ((), ())), preferred_element_type=jnp.float32
             )
-            dv_ref[pl.ds(start, CHUNK), :] += lax.dot_general(
+            dv_ref[pl.ds(start, SPAN_ROWS), :] += lax.dot_general(
                 p.astype(jnp.bfloat16), gr, (((0,), (0,)), ((), ())), preferred_element_type=jnp.float32
             )
             return dq + jnp.dot(ds, kb, preferred_element_type=jnp.float32)
 
         dq = lax.fori_loop(0, count, backward, jnp.zeros((rows, DH), jnp.float32))
         dq_ref[:, cols] = dq * scale
-    dk_ref[...] = dk_ref[...] * scale
-
-
-def attention(chunk_list, chunk_count, query, grad, keys, values, qpos, qdoc, kpos, kdoc, interpret=False):
+
+    @pl.when(span == pl.num_programs(1) - 1)
+    def _():
+        dk_ref[...] = dk_ref[...] * scale
+
+
+def attention(span_list, span_count, query, grad, keys, values, qpos, qdoc, kpos, kdoc, interpret=False):
     rows, width = query.shape
     keys_len, kv_width = keys.shape
     groups = width // kv_width
     heads = kv_width // DH
-    q_spec = pl.BlockSpec((rows, groups * DH), lambda c, *_: (0, c))
-    k_spec = pl.BlockSpec((keys_len, DH), lambda c, *_: (0, c))
-    col_spec = pl.BlockSpec((rows, 1), lambda c, *_: (0, 0))
-    row_spec = pl.BlockSpec((1, keys_len), lambda c, *_: (0, 0))
+    q_spec = pl.BlockSpec((SPAN_ROWS, groups * DH), lambda c, s, *_: (s, c))
+    k_spec = pl.BlockSpec((keys_len, DH), lambda c, s, *_: (0, c))
+    col_spec = pl.BlockSpec((SPAN_ROWS, 1), lambda c, s, *_: (s, 0))
+    row_spec = pl.BlockSpec((1, keys_len), lambda c, s, *_: (0, 0))
     return pl.pallas_call(
         attention_kernel,
         grid_spec=pltpu.PrefetchScalarGridSpec(
             num_scalar_prefetch=2,
-            grid=(heads,),
+            grid=(heads, rows // SPAN_ROWS),
             in_specs=[q_spec, q_spec, k_spec, k_spec, col_spec, col_spec, row_spec, row_spec],
             out_specs=[q_spec, k_spec, k_spec],
+            scratch_shapes=[pltpu.VMEM((keys_len // SPAN_ROWS, SPAN_ROWS, SPAN_ROWS), jnp.float32)],
         ),
         out_shape=[
             jax.ShapeDtypeStruct((rows, width), jnp.float32),
             jax.ShapeDtypeStruct((keys_len, kv_width), jnp.float32),
             jax.ShapeDtypeStruct((keys_len, kv_width), jnp.float32),
         ],
-        compiler_params=pltpu.CompilerParams(dimension_semantics=("arbitrary",)),
+        compiler_params=pltpu.CompilerParams(dimension_semantics=("arbitrary", "arbitrary")),
         interpret=interpret,
-    )(chunk_list, chunk_count, query, grad, keys, values, qpos, qdoc, kpos, kdoc)
+    )(span_list, span_count, query, grad, keys, values, qpos, qdoc, kpos, kdoc)
 
 
 def visible(query_pos, query_doc, key_pos, key_doc):
@@ -167,19 +183,21 @@
     own_docs = lax.dynamic_slice_in_dim(doc_all, ctx_index * local_rows, local_rows)
     keys_all = gathered[:, :k_cols]
     values_all = gathered[:, k_cols : 2 * k_cols]
-    num_chunks = pack_len // CHUNK
+    query_spans = local_rows // SPAN_ROWS
+    key_spans = pack_len // SPAN_ROWS
     allowed_all = visible(own_pos, own_docs, positions, doc_all)
-    active = jnp.any(allowed_all.reshape(local_rows, num_chunks, CHUNK), axis=(0, 2))
-    chunk_count = jnp.sum(active.astype(jnp.int32)).reshape(1)
-    rank = jnp.cumsum(active.astype(jnp.int32)) - 1
-    chunk_list = (
-        jnp.zeros((num_chunks,), jnp.int32)
-        .at[jnp.where(active, rank, num_chunks)]
-        .set(jnp.arange(num_chunks, dtype=jnp.int32), mode="drop")
+    active = jnp.any(allowed_all.reshape(query_spans, SPAN_ROWS, key_spans, SPAN_ROWS), axis=(1, 3))
+    span_count = jnp.sum(active.astype(jnp.int32), axis=1)
+    rank = jnp.cumsum(active.astype(jnp.int32), axis=1) - 1
+    slot = jnp.where(active, rank + key_spans * jnp.arange(query_spans)[:, None], query_spans * key_spans)
+    span_list = (
+        jnp.zeros((query_spans * key_spans,), jnp.int32)
+        .at[slot.reshape(-1)]
+        .set(jnp.tile(jnp.arange(key_spans, dtype=jnp.int32), query_spans), mode="drop")
     )
     dquery_full, dkey_all, dvalue_all = attention(
-        chunk_list,
-        chunk_count,
+        span_list,
+        span_count,
         query,
         grad_rows,
         keys_all,

time: 473 us -> 528 us (1.12)
  starting transfers between devices: 133 us -> 165 us
  waiting for transfers between devices: 164 us -> 175 us
  Pallas kernels: 71.6 us -> 78 us
    all_to_all x1, starting transfers between devices: 65.2 us -> 139 us  [local(): lax.all_to_all(partial.reshape(ctx_size, local_rows, 2 * k_cols), 'ctx',...]
    all_to_all x1, starting transfers between devices: 51.1 us -> 10.2 us  [local(): lax.all_to_all(result[source_rows].reshape(devices, capacity, q_cols + 2...]
    all_to_all x1, waiting for transfers between devices: 27.2 us -> 38 us  [local(): lax.all_to_all(partial.reshape(ctx_size, local_rows, 2 * k_cols), 'ctx',...]
    pallas_call x1, Pallas kernels: 71.6 us -> 78 us  [attention(): pl.pallas_call(attention_kernel, grid_spec=pltpu.PrefetchScalarGridSpec(n...]
  transfers between devices with their start and end apart: 5 -> 5, of which waited for: 5 -> 5; matrix products, arithmetic and copies ran while one was open for 7% -> 6% of each run, Pallas kernels for 0% -> 0%
where the time goes in v1:
time: 528 us; the launch traced here: 521 us
  waiting for transfers between devices  175 us (33%)
  starting transfers between devices  165 us (31%)
  Pallas kernels  78 us (15%)
  local copies, waits for them, and re-layouts  59.6 us (11%)
  other arithmetic  28.6 us (5%)
  between operations  14.3 us (3%)
    all_to_all x1, starting transfers between devices, local(): lax.all_to_all(partial.reshape(ctx_size, local_rows, 2 * k_cols), 'ctx',...  139 us
    pallas_call x1, Pallas kernels, attention(): pl.pallas_call(attention_kernel, grid_spec=pltpu.PrefetchScalarGridSpec(n...  78 us
    all_to_all x2, waiting for transfers between devices, exchange(): lax.all_to_all(holder.reshape(devices, capacity, width), ('dp', 'ctx'), s...  70.8 us
    all_to_all x1, waiting for transfers between devices, local(): lax.all_to_all(result[source_rows].reshape(devices, capacity, q_cols + 2...  40.9 us
    all_to_all x1, waiting for transfers between devices, local(): lax.all_to_all(partial.reshape(ctx_size, local_rows, 2 * k_cols), 'ctx',...  38 us
    all_gather x1, waiting for transfers between devices, local(): lax.all_gather(jnp.concatenate([kv_rows, doc_col], axis=1), 'ctx', axis=0...  25.3 us
    all_to_all x2, starting transfers between devices, exchange(): lax.all_to_all(holder.reshape(devices, capacity, width), ('dp', 'ctx'), s...  16.6 us
    scatter x2, local copies, waits for them, and re-layouts, unpack(): jnp.zeros((local_rows, values.shape[1]), values.dtype).at[landing]  11 us
  transfers between devices with their start and end apart: 5, of which 5 were waited for; matrix products, arithmetic and copies ran while one was open for 6% of the time, Pallas kernels for 0%

profile of v1, /device:TPU:1, one launch (start us, length us, event | category | flops | bytes accessed | tf_op | source)
XLA Modules:
  0.0 521.2 jit_solution(12459534643032629971)
XLA Ops:
  15.6 11.5 %all-to-all-start = ((bf16[128,4,1152]{2,1,0:T(4,128)(2,1)}), bf16[128,4,1152]{2,1,0:T(4,128)(2,1)S(1)}, u32[]{:S(2)}, u32[]{:S(2)}) async-start(bf16[128,4,1152]{2,1,0:T(4,128)(2,1)} %reshape.262), calls=%async_computation | async-start | bytes 2359296 | tf_op jit(solution)/shard_map/all_to_all | solution.py:152
  28.0 20.0 %all-to-all-done = bf16[128,4,1152]{2,1,0:T(4,128)(2,1)S(1)} async-done(((bf16[128,4,1152]{2,1,0:T(4,128)(2,1)}), bf16[128,4,1152]{2,1,0:T(4,128)(2,1)S(1)}, u32[]{:S(2)}, u32[]{:S(2)}) %all-to-all-start) | async-done | bytes 1179680 | tf_op jit(solution)/shard_map/all_to_all | solution.py:152
  48.5 2.8 scatter_custom_fusion.1
  52.8 6.1 %scatter_custom_fusion.3 = bf16[512,4096]{1,0:T(8,128)(2,1)} fusion(s32[256]{0:T(256)S(1)} %compare_select_fusion.4, bf16[256,2048]{1,0:T(8,128)(2,1)S(1)} %copy-done.2, bf16[]{:T(256)} %constant.130, bf16[256,2048]{1,0:T(8,128)(2,1)S(1)} %copy-done.3, bf16[]{:T(256)} %constant.109.clone.1), kind=kCustom, calls=%fused_computation.9 | custom fusion | flops 4194304 | bytes 6291460 | tf_op jit(solution)/shard_map/scatter | solution.py:151
  58.8 7.2 %reshape.266 = bf16[128,4,4096]{2,1,0:T(4,128)(2,1)} reshape(bf16[512,4096]{1,0:T(8,128)(2,1)} %scatter_custom_fusion.3) | data formatting | bytes 8388608 | tf_op jit(solution)/shard_map/reshape | solution.py:153
  66.1 5.1 all-to-all-start.1
  72.4 50.8 %all-to-all-done.1 = bf16[128,4,4096]{2,1,0:T(4,128)(2,1)} async-done(((bf16[128,4,4096]{2,1,0:T(4,128)(2,1)}), bf16[128,4,4096]{2,1,0:T(4,128)(2,1)}, u32[]{:S(2)}, u32[]{:S(2)}) %all-to-all-start.1) | async-done | bytes 4194336 | tf_op jit(solution)/shard_map/all_to_all | solution.py:152
  123.2 7.1 %reshape.331 = bf16[512,4096]{1,0:T(8,128)(2,1)} reshape(bf16[128,4,4096]{2,1,0:T(4,128)(2,1)} %all-to-all-done.1) | data formatting | bytes 8388608 | tf_op jit(solution)/shard_map/reshape | solution.py:154
  130.3 8.2 %scatter_custom_fusion.4 = bf16[256,4096]{1,0:T(8,128)(2,1)S(1)} fusion(s32[512]{0:T(512)S(1)} %get-tuple-element.34, bf16[512,4096]{1,0:T(8,128)(2,1)} %reshape.331, bf16[]{:T(256)} %constant.109.clone.1), kind=kCustom, calls=%fused_computation.22 | custom fusion | bytes 2097664 | tf_op jit(solution)/shard_map/scatter | solution.py:162
  140.0 25.3 %all-gather.2.cloned.1.call-done = bf16[2048,1152]{1,0:T(8,128)(2,1)} async-done(((bf16[256,1152]{1,0:T(8,128)(2,1)}), bf16[2048,1152]{1,0:T(8,128)(2,1)}) %all-gather.2.cloned.1.call-update) | async-done | bytes 4718608 | tf_op jit(solution)/shard_map/all_gather | solution.py:178
  171.6 4.5 fusion.38
  176.1 78.0 %shard_map.94 = (f32[256,2048]{1,0:T(8,128)}, f32[2048,512]{1,0:T(8,128)}, f32[2048,512]{1,0:T(8,128)}) custom-call(s32[32]{0:T(128)} %scatter_custom_fusion.2.list_ref, s32[2]{0:T(128)} %get-tuple-element.41.count_ref, bf16[256,2048]{1,0:T(8,128)(2,1)} %get-tuple-element.38.q_ref, bf16[256,2048]{1,0:T(8,128)(2,1)} %get-tuple-element.37.g_ref, ...), custom_call_target="tpu_custom_call" | custom-call | tf_op jit(solution)/shard_map/pallas_call | solution.py:108
  254.1 2.6 convert.10
  257.8 2.6 pad_maximum_fusion
  260.4 138.7 %all-to-all-start.2 = ((bf16[8,256,1024]{2,1,0:T(8,128)(2,1)}), bf16[8,256,1024]{2,1,0:T(8,128)(2,1)}, u32[]{:S(2)}, u32[]{:S(2)}) async-start(bf16[8,256,1024]{2,1,0:T(8,128)(2,1)} %pad_maximum_fusion), calls=%async_computation.2 | async-start | bytes 8388608 | tf_op jit(solution)/shard_map/all_to_all | solution.py:212
  400.8 38.0 %all-to-all-done.2 = bf16[8,256,1024]{2,1,0:T(8,128)(2,1)} async-done(((bf16[8,256,1024]{2,1,0:T(8,128)(2,1)}), bf16[8,256,1024]{2,1,0:T(8,128)(2,1)}, u32[]{:S(2)}, u32[]{:S(2)}) %all-to-all-start.2) | async-done | bytes 4194336 | tf_op jit(solution)/shard_map/all_to_all | solution.py:212
  438.8 3.1 reduce_sum.32
  442.1 3.9 gather_fusion.1
  445.9 6.1 %reshape.268 = bf16[128,4,3072]{2,1,0:T(4,128)(2,1)} reshape(bf16[512,3072]{1,0:T(8,128)(2,1)} %gather_fusion.1) | data formatting | bytes 6291456 | tf_op jit(solution)/shard_map/reshape | solution.py:220
  452.0 10.2 %all-to-all-start.3 = ((bf16[128,4,3072]{2,1,0:T(4,128)(2,1)}), bf16[128,4,3072]{2,1,0:T(4,128)(2,1)}, u32[]{:S(2)}, u32[]{:S(2)}) async-start(bf16[128,4,3072]{2,1,0:T(4,128)(2,1)} %reshape.268), calls=%async_computation.3 | async-start | bytes 6291456 | tf_op jit(solution)/shard_map/all_to_all | solution.py:219
  462.2 40.9 %all-to-all-done.3 = bf16[128,4,3072]{2,1,0:T(4,128)(2,1)} async-done(((bf16[128,4,3072]{2,1,0:T(4,128)(2,1)}), bf16[128,4,3072]{2,1,0:T(4,128)(2,1)}, u32[]{:S(2)}, u32[]{:S(2)}) %all-to-all-start.3) | async-done | bytes 3145760 | tf_op jit(solution)/shard_map/all_to_all | solution.py:219
  503.1 4.5 reshape.269
  507.6 2.7 gather_fusion.2
  510.3 2.9 slice.90
  (69 shorter events, 24.0 us)
Async XLA Ops:
  14.4 12.7 %copy-start.6 = (s32[1,256]{1,0:T(1,128)S(1)}, s32[1,256]{1,0:T(1,128)}, u32[]{:S(2)}) copy-start(s32[1,256]{1,0:T(1,128)} %param.17) | copy-start | bytes 3076
  15.6 32.4 %all-to-all-start = ((bf16[128,4,1152]{2,1,0:T(4,128)(2,1)}), bf16[128,4,1152]{2,1,0:T(4,128)(2,1)S(1)}, u32[]{:S(2)}, u32[]{:S(2)}) async-start(bf16[128,4,1152]{2,1,0:T(4,128)(2,1)} %reshape.262), calls=%async_computation | async-start | bytes 2359296 | tf_op jit(solution)/shard_map/all_to_all | solution.py:152
  27.1 138.3 %all-gather.2.cloned.1.call-start = ((), (), s32[]{:S(2)}) async-start(), calls=%async_computation.4 | async-start | bytes 5308416 | tf_op jit(solution)/shard_map/all_gather | solution.py:178
  48.3 4.0 copy-start.2
  51.3 1.4 copy-start.3
  66.1 5.2 %copy-start.7 = (s32[1,16]{1,0:T(1,128)S(1)}, s32[1,16]{1,0:T(1,128)}, u32[]{:S(2)}) copy-start(s32[1,16]{1,0:T(1,128)} %param.16) | copy-start | bytes 196
  66.1 57.1 %all-to-all-start.1 = ((bf16[128,4,4096]{2,1,0:T(4,128)(2,1)}), bf16[128,4,4096]{2,1,0:T(4,128)(2,1)}, u32[]{:S(2)}, u32[]{:S(2)}) async-start(bf16[128,4,4096]{2,1,0:T(4,128)(2,1)} %reshape.266), calls=%async_computation.1 | async-start | bytes 8388608 | tf_op jit(solution)/shard_map/all_to_all | solution.py:152
  71.4 96.1 %copy-start.5 = (s32[16,128]{1,0:T(8,128)}, s32[16,128]{1,0:T(8,128)S(1)}, u32[]{:S(2)}) copy-start(s32[16,128]{1,0:T(8,128)S(1)} %get-tuple-element.43) | copy-start | bytes 24580
  167.3 8.7 %copy-start.4 = (s32[16,128]{1,0:T(8,128)}, s32[16,128]{1,0:T(8,128)S(1)}, u32[]{:S(2)}) copy-start(s32[16,128]{1,0:T(8,128)S(1)} %gather_fusion) | copy-start | bytes 24580
  254.1 3.5 copy-start.1
  260.4 178.4 %all-to-all-start.2 = ((bf16[8,256,1024]{2,1,0:T(8,128)(2,1)}), bf16[8,256,1024]{2,1,0:T(8,128)(2,1)}, u32[]{:S(2)}, u32[]{:S(2)}) async-start(bf16[8,256,1024]{2,1,0:T(8,128)(2,1)} %pad_maximum_fusion), calls=%async_computation.2 | async-start | bytes 8388608 | tf_op jit(solution)/shard_map/all_to_all | solution.py:212
  452.0 51.1 %all-to-all-start.3 = ((bf16[128,4,3072]{2,1,0:T(4,128)(2,1)}), bf16[128,4,3072]{2,1,0:T(4,128)(2,1)}, u32[]{:S(2)}, u32[]{:S(2)}) async-start(bf16[128,4,3072]{2,1,0:T(4,128)(2,1)} %reshape.268), calls=%async_computation.3 | async-start | bytes 6291456 | tf_op jit(solution)/shard_map/all_to_all | solution.py:219
  510.3 2.9 copy-start
Sparse Core Ops, SparseCore 0:
  52.3 112.9 all-gather.1

commit v2 on v1

--- a/solution.py
+++ b/solution.py
@@ -19,6 +19,8 @@
 ):
     scale = DH ** (-0.5)
     rows = q_ref.shape[0]
+    heads = q_ref.shape[1] // DH
+    stacked = heads * rows
     span = pl.program_id(1)
     spans = list_ref.shape[0] // pl.num_programs(1)
     count = count_ref[span]
@@ -30,66 +32,62 @@
 
     qpos = qpos_ref[...]
     qdoc = qdoc_ref[...]
+    q = jnp.concatenate([q_ref[:, g * DH : (g + 1) * DH] for g in range(heads)], axis=0)
+    gr = jnp.concatenate([g_ref[:, g * DH : (g + 1) * DH] for g in range(heads)], axis=0)
 
     def first_key(i):
         return pl.multiple_of(list_ref[span * spans + i] * SPAN_ROWS, SPAN_ROWS)
 
-    for g in range(q_ref.shape[1] // DH):
-        cols = slice(g * DH, (g + 1) * DH)
-        q = q_ref[:, cols]
-        gr = g_ref[:, cols]
-
-        def stats(i, carry):
-            m, l = carry
-            start = first_key(i)
-            kp = kpos_ref[:, pl.ds(start, SPAN_ROWS)]
-            kd = kdoc_ref[:, pl.ds(start, SPAN_ROWS)]
-            allowed = (kp <= qpos) & (kd == qdoc)
-            s = lax.dot_general(
-                q, k_ref[pl.ds(start, SPAN_ROWS), :], (((1,), (1,)), ((), ())),
-                preferred_element_type=jnp.float32,
-            ) * scale
-            s = jnp.where(allowed, s, -jnp.inf)
-            tiles_ref[i] = s
-            m_new = jnp.maximum(m, jnp.max(s, axis=1, keepdims=True))
-            l = l * jnp.exp(m - m_new) + jnp.sum(jnp.exp(s - m_new), axis=1, keepdims=True)
-            return m_new, l
-
-        m, l = lax.fori_loop(
-            0, count, stats, (jnp.full((rows, 1), -1e30, jnp.float32), jnp.zeros((rows, 1), jnp.float32))
+    def stats(i, carry):
+        m, l = carry
+        start = first_key(i)
+        kp = kpos_ref[:, pl.ds(start, SPAN_ROWS)]
+        kd = kdoc_ref[:, pl.ds(start, SPAN_ROWS)]
+        allowed = (kp <= qpos) & (kd == qdoc)
+        s = lax.dot_general(
+            q, k_ref[pl.ds(start, SPAN_ROWS), :], (((1,), (1,)), ((), ())),
+            preferred_element_type=jnp.float32,
+        ) * scale
+        s = jnp.where(allowed[None], s.reshape(heads, rows, SPAN_ROWS), -jnp.inf).reshape(stacked, SPAN_ROWS)
+        tiles_ref[i] = s
+        m_new = jnp.maximum(m, jnp.max(s, axis=1, keepdims=True))
+        l = l * jnp.exp(m - m_new) + jnp.sum(jnp.exp(s - m_new), axis=1, keepdims=True)
+        return m_new, l
+
+    m, l = lax.fori_loop(
+        0, count, stats, (jnp.full((stacked, 1), -1e30, jnp.float32), jnp.zeros((stacked, 1), jnp.float32))
+    )
+    lse = m + jnp.log(l)
+
+    def forward(i, o):
+        start = first_key(i)
+        p = jnp.exp(tiles_ref[i] - lse)
+        tiles_ref[i] = p
+        return o + jnp.dot(
+            p.astype(jnp.bfloat16), v_ref[pl.ds(start, SPAN_ROWS), :], preferred_element_type=jnp.float32
         )
-        lse = m + jnp.log(l)
-
-        def forward(i, o):
-            start = first_key(i)
-            p = jnp.exp(tiles_ref[i] - lse)
-            tiles_ref[i] = p
-            return o + jnp.dot(
-                p.astype(jnp.bfloat16), v_ref[pl.ds(start, SPAN_ROWS), :], preferred_element_type=jnp.float32
-            )
-
-        o = lax.fori_loop(0, count, forward, jnp.zeros((rows, DH), jnp.float32))
-        delta = jnp.sum(
-            gr.astype(jnp.float32) * o.astype(jnp.bfloat16).astype(jnp.float32), axis=1, keepdims=True
+
+    o = lax.fori_loop(0, count, forward, jnp.zeros((stacked, DH), jnp.float32))
+    delta = jnp.sum(gr.astype(jnp.float32) * o.astype(jnp.bfloat16).astype(jnp.float32), axis=1, keepdims=True)
+
+    def backward(i, dq):
+        start = first_key(i)
+        kb = k_ref[pl.ds(start, SPAN_ROWS), :]
+        vb = v_ref[pl.ds(start, SPAN_ROWS), :]
+        p = tiles_ref[i]
+        dp = lax.dot_general(gr, vb, (((1,), (1,)), ((), ())), preferred_element_type=jnp.float32)
+        ds = (p * (dp - delta)).astype(jnp.bfloat16)
+        dk_ref[pl.ds(start, SPAN_ROWS), :] += lax.dot_general(
+            ds, q, (((0,), (0,)), ((), ())), preferred_element_type=jnp.float32
         )
-
-        def backward(i, dq):
-            start = first_key(i)
-            kb = k_ref[pl.ds(start, SPAN_ROWS), :]
-            vb = v_ref[pl.ds(start, SPAN_ROWS), :]
-            p = tiles_ref[i]
-            dp = lax.dot_general(gr, vb, (((1,), (1,)), ((), ())), preferred_element_type=jnp.float32)
-            ds = (p * (dp - delta)).astype(jnp.bfloat16)
-            dk_ref[pl.ds(start, SPAN_ROWS), :] += lax.dot_general(
-                ds, q, (((0,), (0,)), ((), ())), preferred_element_type=jnp.float32
-            )
-            dv_ref[pl.ds(start, SPAN_ROWS), :] += lax.dot_general(
-                p.astype(jnp.bfloat16), gr, (((0,), (0,)), ((), ())), preferred_element_type=jnp.float32
-            )
-            return dq + jnp.dot(ds, kb, preferred_element_type=jnp.float32)
-
-        dq = lax.fori_loop(0, count, backward, jnp.zeros((rows, DH), jnp.float32))
-        dq_ref[:, cols] = dq * scale
+        dv_ref[pl.ds(start, SPAN_ROWS), :] += lax.dot_general(
+            p.astype(jnp.bfloat16), gr, (((0,), (0,)), ((), ())), preferred_element_type=jnp.float32
+        )
+        return dq + jnp.dot(ds, kb, preferred_element_type=jnp.float32)
+
+    dq = lax.fori_loop(0, count, backward, jnp.zeros((stacked, DH), jnp.float32)) * scale
+    for g in range(heads):
+        dq_ref[:, g * DH : (g + 1) * DH] = dq[g * rows : (g + 1) * rows]
 
     @pl.when(span == pl.num_programs(1) - 1)
     def _():
@@ -112,7 +110,7 @@
             grid=(heads, rows // SPAN_ROWS),
             in_specs=[q_spec, q_spec, k_spec, k_spec, col_spec, col_spec, row_spec, row_spec],
             out_specs=[q_spec, k_spec, k_spec],
-            scratch_shapes=[pltpu.VMEM((keys_len // SPAN_ROWS, SPAN_ROWS, SPAN_ROWS), jnp.float32)],
+            scratch_shapes=[pltpu.VMEM((keys_len // SPAN_ROWS, groups * SPAN_ROWS, SPAN_ROWS), jnp.float32)],
         ),
         out_shape=[
             jax.ShapeDtypeStruct((rows, width), jnp.float32),

time: 528 us -> 387 us (0.73); the launches traced: 521 us -> 389 us
  starting transfers between devices: 165 us -> 65.1 us
  Pallas kernels: 78 us -> 52.9 us
  waiting for transfers between devices: 175 us -> 169 us
    all_to_all x1, starting transfers between devices: 139 us -> 4.76 us  [local(): lax.all_to_all(partial.reshape(ctx_size, local_rows, 2 * k_cols), 'ctx',...]
    all_to_all x1, starting transfers between devices: 10.2 us -> 43.6 us  [local(): lax.all_to_all(result[source_rows].reshape(devices, capacity, q_cols + 2...]
    pallas_call x1, Pallas kernels: 78 us -> 52.9 us  [attention(): pl.pallas_call(attention_kernel, grid_spec=pltpu.PrefetchScalarGridSpec(n...]
    all_to_all x1, waiting for transfers between devices: 38 us -> 31.9 us  [local(): lax.all_to_all(partial.reshape(ctx_size, local_rows, 2 * k_cols), 'ctx',...]
  transfers between devices with their start and end apart: 5 -> 5, of which waited for: 5 -> 5; matrix products, arithmetic and copies ran while one was open for 6% -> 9% of each run, Pallas kernels for 0% -> 0%
where the time goes in v2:
time: 387 us; the launch traced here: 389 us
  waiting for transfers between devices  169 us (44%)
  starting transfers between devices  65.1 us (17%)
  local copies, waits for them, and re-layouts  59.6 us (15%)
  Pallas kernels  52.9 us (14%)
  other arithmetic  28.6 us (7%)
  between operations  14.3 us (4%)
    all_to_all x2, waiting for transfers between devices, exchange(): lax.all_to_all(holder.reshape(devices, capacity, width), ('dp', 'ctx'), s...  70.8 us
    pallas_call x1, Pallas kernels, attention(): pl.pallas_call(attention_kernel, grid_spec=pltpu.PrefetchScalarGridSpec(n...  52.9 us
    all_to_all x1, starting transfers between devices, local(): lax.all_to_all(result[source_rows].reshape(devices, capacity, q_cols + 2...  43.6 us
    all_to_all x1, waiting for transfers between devices, local(): lax.all_to_all(result[source_rows].reshape(devices, capacity, q_cols + 2...  40.9 us
    all_to_all x1, waiting for transfers between devices, local(): lax.all_to_all(partial.reshape(ctx_size, local_rows, 2 * k_cols), 'ctx',...  31.9 us
    all_gather x1, waiting for transfers between devices, local(): lax.all_gather(jnp.concatenate([kv_rows, doc_col], axis=1), 'ctx', axis=0...  25.3 us
    all_to_all x2, starting transfers between devices, exchange(): lax.all_to_all(holder.reshape(devices, capacity, width), ('dp', 'ctx'), s...  16.6 us
    scatter x2, local copies, waits for them, and re-layouts, unpack(): jnp.zeros((local_rows, values.shape[1]), values.dtype).at[landing]  11 us
  transfers between devices with their start and end apart: 5, of which 5 were waited for; matrix products, arithmetic and copies ran while one was open for 9% of the time, Pallas kernels for 0%

profile of v2, /device:TPU:1, one launch (start us, length us, event | category | flops | bytes accessed | tf_op | source)
XLA Modules:
  0.0 389.5 jit_solution(9518821261368636118)
XLA Ops:
  15.6 11.5 %all-to-all-start = ((bf16[128,4,1152]{2,1,0:T(4,128)(2,1)}), bf16[128,4,1152]{2,1,0:T(4,128)(2,1)S(1)}, u32[]{:S(2)}, u32[]{:S(2)}) async-start(bf16[128,4,1152]{2,1,0:T(4,128)(2,1)} %reshape.262), calls=%async_computation | async-start | bytes 2359296 | tf_op jit(solution)/shard_map/all_to_all | solution.py:150
  28.0 20.0 %all-to-all-done = bf16[128,4,1152]{2,1,0:T(4,128)(2,1)S(1)} async-done(((bf16[128,4,1152]{2,1,0:T(4,128)(2,1)}), bf16[128,4,1152]{2,1,0:T(4,128)(2,1)S(1)}, u32[]{:S(2)}, u32[]{:S(2)}) %all-to-all-start) | async-done | bytes 1179680 | tf_op jit(solution)/shard_map/all_to_all | solution.py:150
  48.5 2.8 scatter_custom_fusion.1
  52.8 6.1 %scatter_custom_fusion.3 = bf16[512,4096]{1,0:T(8,128)(2,1)} fusion(s32[256]{0:T(256)S(1)} %compare_select_fusion.4, bf16[256,2048]{1,0:T(8,128)(2,1)S(1)} %copy-done.2, bf16[]{:T(256)} %constant.130, bf16[256,2048]{1,0:T(8,128)(2,1)S(1)} %copy-done.3, bf16[]{:T(256)} %constant.109.clone.1), kind=kCustom, calls=%fused_computation.9 | custom fusion | flops 4194304 | bytes 6291460 | tf_op jit(solution)/shard_map/scatter | solution.py:149
  58.8 7.2 %reshape.266 = bf16[128,4,4096]{2,1,0:T(4,128)(2,1)} reshape(bf16[512,4096]{1,0:T(8,128)(2,1)} %scatter_custom_fusion.3) | data formatting | bytes 8388608 | tf_op jit(solution)/shard_map/reshape | solution.py:151
  66.1 5.1 %all-to-all-start.1 = ((bf16[128,4,4096]{2,1,0:T(4,128)(2,1)}), bf16[128,4,4096]{2,1,0:T(4,128)(2,1)}, u32[]{:S(2)}, u32[]{:S(2)}) async-start(bf16[128,4,4096]{2,1,0:T(4,128)(2,1)} %reshape.266), calls=%async_computation.1 | async-start | bytes 8388608 | tf_op jit(solution)/shard_map/all_to_all | solution.py:150
  72.4 50.8 %all-to-all-done.1 = bf16[128,4,4096]{2,1,0:T(4,128)(2,1)} async-done(((bf16[128,4,4096]{2,1,0:T(4,128)(2,1)}), bf16[128,4,4096]{2,1,0:T(4,128)(2,1)}, u32[]{:S(2)}, u32[]{:S(2)}) %all-to-all-start.1) | async-done | bytes 4194336 | tf_op jit(solution)/shard_map/all_to_all | solution.py:150
  123.2 7.1 %reshape.331 = bf16[512,4096]{1,0:T(8,128)(2,1)} reshape(bf16[128,4,4096]{2,1,0:T(4,128)(2,1)} %all-to-all-done.1) | data formatting | bytes 8388608 | tf_op jit(solution)/shard_map/reshape | solution.py:152
  130.3 8.2 %scatter_custom_fusion.4 = bf16[256,4096]{1,0:T(8,128)(2,1)S(1)} fusion(s32[512]{0:T(512)S(1)} %get-tuple-element.34, bf16[512,4096]{1,0:T(8,128)(2,1)} %reshape.331, bf16[]{:T(256)} %constant.109.clone.1), kind=kCustom, calls=%fused_computation.22 | custom fusion | bytes 2097664 | tf_op jit(solution)/shard_map/scatter | solution.py:160
  140.0 25.3 %all-gather.2.cloned.1.call-done = bf16[2048,1152]{1,0:T(8,128)(2,1)} async-done(((bf16[256,1152]{1,0:T(8,128)(2,1)}), bf16[2048,1152]{1,0:T(8,128)(2,1)}) %all-gather.2.cloned.1.call-update) | async-done | bytes 4718608 | tf_op jit(solution)/shard_map/all_gather | solution.py:176
  171.6 4.5 %fusion.38 = (bf16[2048,512]{1,0:T(8,128)(2,1)}, bf16[2048,512]{1,0:T(8,128)(2,1)}) fusion(bf16[2048,1152]{1,0:T(8,128)(2,1)} %all-gather.2.cloned.1.call-done), kind=kLoop, calls=%fused_computation.81 | loop fusion | bytes 8388608 | tf_op jit(solution)/shard_map/slice | solution.py:183
  176.1 52.9 %shard_map.94 = (f32[256,2048]{1,0:T(8,128)}, f32[2048,512]{1,0:T(8,128)}, f32[2048,512]{1,0:T(8,128)}) custom-call(s32[32]{0:T(128)} %scatter_custom_fusion.2.list_ref, s32[2]{0:T(128)} %get-tuple-element.41.count_ref, bf16[256,2048]{1,0:T(8,128)(2,1)} %get-tuple-element.38.q_ref, bf16[256,2048]{1,0:T(8,128)(2,1)} %get-tuple-element.37.g_ref, ...), custom_call_target="tpu_custom_call" | custom-call | tf_op jit(solution)/shard_map/pallas_call | solution.py:106
  229.0 2.6 convert.10
  232.7 2.6 pad_maximum_fusion
  235.2 4.8 %all-to-all-start.2 = ((bf16[8,256,1024]{2,1,0:T(8,128)(2,1)}), bf16[8,256,1024]{2,1,0:T(8,128)(2,1)}, u32[]{:S(2)}, u32[]{:S(2)}) async-start(bf16[8,256,1024]{2,1,0:T(8,128)(2,1)} %pad_maximum_fusion), calls=%async_computation.2 | async-start | bytes 8388608 | tf_op jit(solution)/shard_map/all_to_all | solution.py:210
  241.7 31.9 %all-to-all-done.2 = bf16[8,256,1024]{2,1,0:T(8,128)(2,1)} async-done(((bf16[8,256,1024]{2,1,0:T(8,128)(2,1)}), bf16[8,256,1024]{2,1,0:T(8,128)(2,1)}, u32[]{:S(2)}, u32[]{:S(2)}) %all-to-all-start.2) | async-done | bytes 4194336 | tf_op jit(solution)/shard_map/all_to_all | solution.py:210
  273.6 3.1 reduce_sum.32
  276.9 3.9 gather_fusion.1
  280.7 6.1 %reshape.268 = bf16[128,4,3072]{2,1,0:T(4,128)(2,1)} reshape(bf16[512,3072]{1,0:T(8,128)(2,1)} %gather_fusion.1) | data formatting | bytes 6291456 | tf_op jit(solution)/shard_map/reshape | solution.py:218
  286.8 43.6 %all-to-all-start.3 = ((bf16[128,4,3072]{2,1,0:T(4,128)(2,1)}), bf16[128,4,3072]{2,1,0:T(4,128)(2,1)}, u32[]{:S(2)}, u32[]{:S(2)}) async-start(bf16[128,4,3072]{2,1,0:T(4,128)(2,1)} %reshape.268), calls=%async_computation.3 | async-start | bytes 6291456 | tf_op jit(solution)/shard_map/all_to_all | solution.py:217
  330.5 40.9 %all-to-all-done.3 = bf16[128,4,3072]{2,1,0:T(4,128)(2,1)} async-done(((bf16[128,4,3072]{2,1,0:T(4,128)(2,1)}), bf16[128,4,3072]{2,1,0:T(4,128)(2,1)}, u32[]{:S(2)}, u32[]{:S(2)}) %all-to-all-start.3) | async-done | bytes 3145760 | tf_op jit(solution)/shard_map/all_to_all | solution.py:217
  371.4 4.5 %reshape.269 = bf16[512,3072]{1,0:T(8,128)(2,1)S(1)} reshape(bf16[128,4,3072]{2,1,0:T(4,128)(2,1)} %all-to-all-done.3) | data formatting | bytes 6291456 | tf_op jit(solution)/shard_map/reshape | solution.py:223
  375.9 2.7 gather_fusion.2
  378.6 2.9 slice.90
  (69 shorter events, 24.0 us)
Async XLA Ops:
  14.4 12.7 %copy-start.6 = (s32[1,256]{1,0:T(1,128)S(1)}, s32[1,256]{1,0:T(1,128)}, u32[]{:S(2)}) copy-start(s32[1,256]{1,0:T(1,128)} %param.17) | copy-start | bytes 3076
  15.6 32.4 %all-to-all-start = ((bf16[128,4,1152]{2,1,0:T(4,128)(2,1)}), bf16[128,4,1152]{2,1,0:T(4,128)(2,1)S(1)}, u32[]{:S(2)}, u32[]{:S(2)}) async-start(bf16[128,4,1152]{2,1,0:T(4,128)(2,1)} %reshape.262), calls=%async_computation | async-start | bytes 2359296 | tf_op jit(solution)/shard_map/all_to_all | solution.py:150
  27.1 138.3 %all-gather.2.cloned.1.call-start = ((), (), s32[]{:S(2)}) async-start(), calls=%async_computation.4 | async-start | bytes 5308416 | tf_op jit(solution)/shard_map/all_gather | solution.py:176
  48.3 4.0 %copy-start.2 = (bf16[256,2048]{1,0:T(8,128)(2,1)S(1)}, bf16[256,2048]{1,0:T(8,128)(2,1)}, u32[]{:S(2)}) copy-start(bf16[256,2048]{1,0:T(8,128)(2,1)} %param.14) | copy-start | bytes 3145732
  51.3 1.4 copy-start.3
  66.1 5.2 %copy-start.7 = (s32[1,16]{1,0:T(1,128)S(1)}, s32[1,16]{1,0:T(1,128)}, u32[]{:S(2)}) copy-start(s32[1,16]{1,0:T(1,128)} %param.16) | copy-start | bytes 196
  66.1 57.1 %all-to-all-start.1 = ((bf16[128,4,4096]{2,1,0:T(4,128)(2,1)}), bf16[128,4,4096]{2,1,0:T(4,128)(2,1)}, u32[]{:S(2)}, u32[]{:S(2)}) async-start(bf16[128,4,4096]{2,1,0:T(4,128)(2,1)} %reshape.266), calls=%async_computation.1 | async-start | bytes 8388608 | tf_op jit(solution)/shard_map/all_to_all | solution.py:150
  71.4 96.1 %copy-start.5 = (s32[16,128]{1,0:T(8,128)}, s32[16,128]{1,0:T(8,128)S(1)}, u32[]{:S(2)}) copy-start(s32[16,128]{1,0:T(8,128)S(1)} %get-tuple-element.43) | copy-start | bytes 24580
  167.3 8.7 %copy-start.4 = (s32[16,128]{1,0:T(8,128)}, s32[16,128]{1,0:T(8,128)S(1)}, u32[]{:S(2)}) copy-start(s32[16,128]{1,0:T(8,128)S(1)} %gather_fusion) | copy-start | bytes 24580
  228.9 3.5 copy-start.1
  235.2 38.4 %all-to-all-start.2 = ((bf16[8,256,1024]{2,1,0:T(8,128)(2,1)}), bf16[8,256,1024]{2,1,0:T(8,128)(2,1)}, u32[]{:S(2)}, u32[]{:S(2)}) async-start(bf16[8,256,1024]{2,1,0:T(8,128)(2,1)} %pad_maximum_fusion), calls=%async_computation.2 | async-start | bytes 8388608 | tf_op jit(solution)/shard_map/all_to_all | solution.py:210
  286.8 84.6 %all-to-all-start.3 = ((bf16[128,4,3072]{2,1,0:T(4,128)(2,1)}), bf16[128,4,3072]{2,1,0:T(4,128)(2,1)}, u32[]{:S(2)}, u32[]{:S(2)}) async-start(bf16[128,4,3072]{2,1,0:T(4,128)(2,1)} %reshape.268), calls=%async_computation.3 | async-start | bytes 6291456 | tf_op jit(solution)/shard_map/all_to_all | solution.py:217
  378.6 2.9 copy-start
Sparse Core Ops, SparseCore 0:
  52.3 112.9 all-gather.1

commit v3 on v2

--- a/solution.py
+++ b/solution.py
@@ -1,4 +1,5 @@
 import jax
+import numpy as np
 import jax.numpy as jnp
 from jax import lax
 from jax.sharding import PartitionSpec as P
@@ -130,98 +131,118 @@
     local_rows = query_in.shape[0]
     devices = lax.axis_size(("dp", "ctx"))
     ctx_size = lax.axis_size("ctx")
-    capacity = local_rows // devices + 2
-    groups = HQ // HK
-    score_scale = DH ** (-0.5)
+    packs = devices // ctx_size
+    pack_len = local_rows * ctx_size
+    capacity = (local_rows // devices + 2) * ctx_size
     q_cols = query_in.shape[1]
     k_cols = key_in.shape[1]
-    owners = target // local_rows
-    onehot = (owners[:, None] == jnp.arange(devices, dtype=jnp.int32)[None, :]).astype(jnp.int32)
-    earlier = jnp.cumsum(onehot, axis=0) - onehot
-    slot_ids = owners * capacity + jnp.sum(earlier * onehot, axis=1)
-
-    place_col = jnp.zeros((local_rows, 128), jnp.bfloat16).at[:, 0].set(
-        (target % local_rows + 1).astype(jnp.bfloat16)
-    )
-
-    def exchange(payload):
-        width = payload.shape[1]
-        holder = jnp.zeros((devices * capacity, width), payload.dtype).at[slot_ids].set(payload)
-        return lax.all_to_all(
-            holder.reshape(devices, capacity, width), ("dp", "ctx"), split_axis=0, concat_axis=0, tiled=True
-        ).reshape(devices * capacity, width)
-
-    got_kv = exchange(jnp.concatenate([key_in, value_in, place_col], axis=1))
-    got_qg = exchange(jnp.concatenate([query_in, grad_out], axis=1))
-    arrived = got_kv[:, 2 * k_cols].astype(jnp.int32) - 1
-    landing = jnp.where(arrived >= 0, arrived, local_rows)
-
-    def unpack(values):
-        return jnp.zeros((local_rows, values.shape[1]), values.dtype).at[landing].set(values, mode="drop")
-
-    kv_rows = unpack(got_kv[:, : 2 * k_cols])
-    qg_rows = unpack(got_qg)
-    query = qg_rows[:, :q_cols]
-    grad_rows = qg_rows[:, q_cols:]
-
-    span_rows = local_rows // 2
+    q_width = q_cols // ctx_size
+    k_width = k_cols // ctx_size
+    ctx_ids = np.arange(ctx_size)
+    kv_of = (ctx_ids // 4) * 2 + ctx_ids % 2
+    half_of = (ctx_ids // 2) % 2
+    block_of = 2 * kv_of + half_of
+    ctx_of_block = np.argsort(block_of)
+
+    pack_of = target // pack_len
+    row_in_pack = target % pack_len
+    onehot = (pack_of[:, None] == jnp.arange(packs, dtype=jnp.int32)[None, :]).astype(jnp.int32)
+    slot = jnp.sum((jnp.cumsum(onehot, axis=0) - onehot) * onehot, axis=1)
+    dest_pack = pack_of[:, None]
+    dest_ctx = jnp.asarray(ctx_ids, jnp.int32)[None, :]
+    dest_slot = slot[:, None]
+
+    payload = jnp.concatenate(
+        [
+            query_in.reshape(local_rows, ctx_size, q_width)[:, block_of],
+            grad_out.reshape(local_rows, ctx_size, q_width)[:, block_of],
+            key_in.reshape(local_rows, k_cols // DH, DH)[:, kv_of],
+            value_in.reshape(local_rows, k_cols // DH, DH)[:, kv_of],
+        ],
+        axis=2,
+    )
+    width = payload.shape[2]
+    holder = (
+        jnp.zeros((packs, ctx_size, capacity, width), jnp.bfloat16)
+        .at[dest_pack, dest_ctx, dest_slot]
+        .set(payload)
+        .reshape(devices * capacity, width)
+    )
+    places = (
+        jnp.zeros((packs, ctx_size, capacity), jnp.int32)
+        .at[dest_pack, dest_ctx, dest_slot]
+        .set(jnp.broadcast_to((row_in_pack + 1)[:, None], (local_rows, ctx_size)))
+        .reshape(devices * capacity)
+    )
+    got = lax.all_to_all(holder, ("dp", "ctx"), split_axis=0, concat_axis=0, tiled=True)
+    got_places = lax.all_to_all(places, ("dp", "ctx"), split_axis=0, concat_axis=0, tiled=True)
+    landing = jnp.where(got_places > 0, got_places - 1, pack_len)
+    rows = jnp.zeros((pack_len, width), jnp.bfloat16).at[landing].set(got, mode="drop")
+    query = rows[:, :q_width]
+    grad_rows = rows[:, q_width : 2 * q_width]
+    keys = rows[:, 2 * q_width : 2 * q_width + DH]
+    values = rows[:, 2 * q_width + DH : 2 * q_width + 2 * DH]
+
     span_seq = span_order[0]
-    pack_len = local_rows * ctx_size
+    span_rows = pack_len // span_seq.shape[0]
     positions = (
         span_seq[:, None] * span_rows + jnp.arange(span_rows, dtype=jnp.int32)[None, :]
     ).reshape(-1)
-    ctx_index = lax.axis_index("ctx")
-    own_pos = lax.dynamic_slice_in_dim(positions, ctx_index * local_rows, local_rows)
-    doc_col = jnp.zeros((local_rows, 128), jnp.bfloat16).at[:, 0].set(doc_ids[0].astype(jnp.bfloat16))
-    gathered = lax.all_gather(
-        jnp.concatenate([kv_rows, doc_col], axis=1), "ctx", axis=0, tiled=True
-    )
-    seq_docs = gathered[:, 2 * k_cols].astype(jnp.int32)
-    doc_all = seq_docs.reshape(2 * ctx_size, span_rows)[span_seq].reshape(-1)
-    own_docs = lax.dynamic_slice_in_dim(doc_all, ctx_index * local_rows, local_rows)
-    keys_all = gathered[:, :k_cols]
-    values_all = gathered[:, k_cols : 2 * k_cols]
-    query_spans = local_rows // SPAN_ROWS
-    key_spans = pack_len // SPAN_ROWS
-    allowed_all = visible(own_pos, own_docs, positions, doc_all)
-    active = jnp.any(allowed_all.reshape(query_spans, SPAN_ROWS, key_spans, SPAN_ROWS), axis=(1, 3))
+    seq_docs = lax.all_gather(doc_ids[0], "ctx", axis=0, tiled=True)
+    doc_all = seq_docs[positions]
+
+    spans = pack_len // SPAN_ROWS
+    allowed_all = visible(positions, doc_all, positions, doc_all)
+    active = jnp.any(allowed_all.reshape(spans, SPAN_ROWS, spans, SPAN_ROWS), axis=(1, 3))
     span_count = jnp.sum(active.astype(jnp.int32), axis=1)
     rank = jnp.cumsum(active.astype(jnp.int32), axis=1) - 1
-    slot = jnp.where(active, rank + key_spans * jnp.arange(query_spans)[:, None], query_spans * key_spans)
+    slot_of = jnp.where(active, rank + spans * jnp.arange(spans)[:, None], spans * spans)
     span_list = (
-        jnp.zeros((query_spans * key_spans,), jnp.int32)
-        .at[slot.reshape(-1)]
-        .set(jnp.tile(jnp.arange(key_spans, dtype=jnp.int32), query_spans), mode="drop")
-    )
-    dquery_full, dkey_all, dvalue_all = attention(
+        jnp.zeros((spans * spans,), jnp.int32)
+        .at[slot_of.reshape(-1)]
+        .set(jnp.tile(jnp.arange(spans, dtype=jnp.int32), spans), mode="drop")
+    )
+    dquery, dkey, dvalue = attention(
         span_list,
         span_count,
         query,
         grad_rows,
-        keys_all,
-        values_all,
-        own_pos.reshape(local_rows, 1),
-        own_docs.reshape(local_rows, 1),
+        keys,
+        values,
+        positions.reshape(pack_len, 1),
+        doc_all.reshape(pack_len, 1),
         positions.reshape(1, pack_len),
         doc_all.reshape(1, pack_len),
     )
-    partial = jnp.concatenate([dkey_all, dvalue_all], axis=1).astype(jnp.bfloat16)
-    summed_kv = jnp.sum(
-        lax.all_to_all(
-            partial.reshape(ctx_size, local_rows, 2 * k_cols), "ctx", split_axis=0, concat_axis=0, tiled=True
-        ).astype(jnp.float32),
-        axis=0,
-    )
-    source_rows = jnp.where(arrived >= 0, arrived, 0)
-    result = jnp.concatenate([dquery_full.astype(jnp.bfloat16), summed_kv.astype(jnp.bfloat16)], axis=1)
+
+    half = jnp.asarray(half_of, jnp.int32)[lax.axis_index("ctx")]
+    split_key = dkey.reshape(pack_len, 2, k_width)
+    split_value = dvalue.reshape(pack_len, 2, k_width)
+    mine = jnp.concatenate(
+        [lax.dynamic_index_in_dim(split_key, half, 1, False), lax.dynamic_index_in_dim(split_value, half, 1, False)],
+        axis=1,
+    )
+    other = jnp.concatenate(
+        [
+            lax.dynamic_index_in_dim(split_key, 1 - half, 1, False),
+            lax.dynamic_index_in_dim(split_value, 1 - half, 1, False),
+        ],
+        axis=1,
+    ).astype(jnp.bfloat16)
+    partner = [(int(c), int(c) ^ 2) for c in ctx_ids]
+    key_value = mine + lax.ppermute(other, "ctx", partner).astype(jnp.float32)
+
+    result = jnp.concatenate([dquery.astype(jnp.bfloat16), key_value.astype(jnp.bfloat16)], axis=1)
+    source_rows = jnp.where(landing < pack_len, landing, 0)
     back = lax.all_to_all(
-        result[source_rows].reshape(devices, capacity, q_cols + 2 * k_cols),
-        ("dp", "ctx"),
-        split_axis=0,
-        concat_axis=0,
-        tiled=True,
-    ).reshape(devices * capacity, q_cols + 2 * k_cols)[slot_ids].astype(jnp.float32)
-    return (back[:, :q_cols], back[:, q_cols : q_cols + k_cols], back[:, q_cols + k_cols :])
+        result[source_rows], ("dp", "ctx"), split_axis=0, concat_axis=0, tiled=True
+    ).reshape(packs, ctx_size, capacity, result.shape[1])
+    pieces = back[dest_pack, jnp.asarray(ctx_of_block, jnp.int32)[None, :], dest_slot].astype(jnp.float32)
+    return (
+        pieces[:, :, :q_width].reshape(local_rows, q_cols),
+        pieces[:, :, q_width : q_width + k_width].reshape(local_rows, k_cols),
+        pieces[:, :, q_width + k_width :].reshape(local_rows, k_cols),
+    )
 
 
 def solution(mesh):

time: 387 us -> 383 us (0.990)
  waiting for transfers between devices: 169 us -> 46.8 us
  blocking collectives: 0 us -> 81.5 us
  local copies, waits for them, and re-layouts: 59.6 us -> 128 us
  starting transfers between devices: 65.1 us -> 36.2 us
  Pallas kernels: 52.9 us -> 67.1 us
  between operations: 14.3 us -> 4.35 us
  other arithmetic: 28.6 us -> 19.1 us
    all_to_all x4 -> x3, waiting for transfers between devices: 144 us -> 41 us  [the longest x1 40.9 us: local(): lax.all_to_all(result[source_rows], ('dp', 'ctx'), split_axis=0, concat_a...]
    all_gather x0 -> x1, blocking collectives: none -> 81.5 us  [local(): seq_docs = lax.all_gather(doc_ids[0], 'ctx', axis=0, tiled=True)]
    gather x3 -> x7, local copies, waits for them, and re-layouts: 7.13 us -> 59.5 us  [the longest x1 24.6 us: local(): back[dest_pack, jnp.asarray(ctx_of_block, jnp.int32)[None, :], dest_slot]]
    unnamed x17 -> x33, local copies, waits for them, and re-layouts: 1.39 us -> 33.7 us
    all_to_all x4 -> x3, starting transfers between devices: 65 us -> 36.2 us  [the longest x1 14.5 us: local(): lax.all_to_all(result[source_rows], ('dp', 'ctx'), split_axis=0, concat_a...]
    all_gather x1 -> x0, waiting for transfers between devices: 25.3 us -> none  [local(): lax.all_gather(jnp.concatenate([kv_rows, doc_col], axis=1), 'ctx', axis=0...]
    reshape x6 -> x4, local copies, waits for them, and re-layouts: 26.4 us -> 1.39 us  [the longest x1 0.52 us: local(): query_in.reshape(local_rows, ctx_size, q_width)[:, block_of]]
    pallas_call x1, Pallas kernels: 52.9 us -> 67.1 us  [attention(): pl.pallas_call(attention_kernel, grid_spec=pltpu.PrefetchScalarGridSpec(n...]
  transfers between devices with their start and end apart: 5 -> 4, of which waited for: 5 -> 2; matrix products, arithmetic and copies ran while one was open for 9% -> 15% of each run, Pallas kernels for 0% -> 0%
where the time goes in v3:
time: 383 us
  local copies, waits for them, and re-layouts  128 us (33%)
  blocking collectives  81.5 us (21%)
  Pallas kernels  67.1 us (18%)
  waiting for transfers between devices  46.8 us (12%)
  starting transfers between devices  36.2 us (9%)
  other arithmetic  19.1 us (5%)
  between operations  4.35 us (1%)
    all_gather x1, blocking collectives, local(): seq_docs = lax.all_gather(doc_ids[0], 'ctx', axis=0, tiled=True)  81.5 us
    pallas_call x1, Pallas kernels, attention(): pl.pallas_call(attention_kernel, grid_spec=pltpu.PrefetchScalarGridSpec(n...  67.1 us
    all_to_all x1, waiting for transfers between devices, local(): lax.all_to_all(result[source_rows], ('dp', 'ctx'), split_axis=0, concat_a...  40.9 us
    unnamed x33, local copies, waits for them, and re-layouts  33.7 us
    gather x1, local copies, waits for them, and re-layouts, local(): back[dest_pack, jnp.asarray(ctx_of_block, jnp.int32)[None, :], dest_slot]  24.6 us
    scatter x1, local copies, waits for them, and re-layouts, local(): jnp.zeros((pack_len, width), jnp.bfloat16).at[landing].set(got, mode='drop')  20 us
    gather x1, local copies, waits for them, and re-layouts, local(): result[source_rows]  17 us
    all_to_all x1, starting transfers between devices, local(): lax.all_to_all(result[source_rows], ('dp', 'ctx'), split_axis=0, concat_a...  14.5 us
  transfers between devices with their start and end apart: 4, of which 2 were waited for; matrix products, arithmetic and copies ran while one was open for 15% of the time, Pallas kernels for 0%

profile of v3, /device:TPU:1, one launch (start us, length us, event | category | flops | bytes accessed | tf_op | source)
XLA Modules:
  0.0 383.1 jit_solution(15369072524188352274)
XLA Ops:
  4.2 8.1 %scatter_custom_fusion.2 = s32[4096]{0:T(1024)S(1)} fusion(s32[2048]{0:T(1024)S(1)} %reshape.395, s32[2048]{0:T(1024)S(1)} %reshape.397, s32[]{:T(128)} %constant.40.clone.1), kind=kCustom, calls=%fused_computation.50 | custom fusion | bytes 16388
  13.0 11.5 %all-to-all-start = ((s32[128,32,1]{1,2,0:T(1,128)}), s32[128,32,1]{1,2,0:T(1,128)S(1)}, u32[]{:S(2)}, u32[]{:S(2)}) async-start(s32[128,32,1]{1,2,0:T(1,128)} %bitcast.8), calls=%async_computation | async-start | bytes 131072 | tf_op jit(solution)/shard_map/all_to_all | solution.py:178
  29.2 1.6 gather_fusion.1
  30.8 1.6 gather_fusion.2
  35.9 2.0 pad_maximum_fusion
  37.9 16.7 %scatter_custom_fusion.3 = bf16[4096,768]{1,0:T(8,128)(2,1)} fusion(s32[2048]{0:T(1024)S(1)} %reshape.395, bf16[256,8,768]{2,0,1:T(8,128)(2,1)S(1)} %pad_maximum_fusion, bf16[]{:T(256)} %constant.88.clone.1), kind=kCustom, calls=%fused_computation.13 | custom fusion | bytes 9437186
  54.5 10.2 %all-to-all-start.1 = ((bf16[128,32,768]{2,1,0:T(8,128)(2,1)}), bf16[128,32,768]{2,1,0:T(8,128)(2,1)}, u32[]{:S(2)}, u32[]{:S(2)}) async-start(bf16[128,32,768]{2,1,0:T(8,128)(2,1)} %bitcast.70), calls=%async_computation.1 | async-start | bytes 12582912 | tf_op jit(solution)/shard_map/all_to_all | solution.py:177
  66.2 81.5 %all-gather = s32[1,2048]{1,0:T(1,128)S(1)} all-gather(s32[1,256]{1,0:T(1,128)S(1)} %copy-done.4), channel_id=2, replica_groups=mesh['dp'=16,'ctx'=8] {'ctx'}, dimensions={1}, use_global_device_ids=true | all-gather | bytes 9216 | tf_op jit(solution)/shard_map/all_gather | solution.py:191
  147.8 11.8 %gather_fusion = s32[2048]{0:T(1024)S(1)} fusion(s32[2048]{0:T(1024)S(1)} %bitcast.68, s32[2048]{0:T(1024)S(1)} %broadcast_clamp_fusion.1), kind=kCustom, calls=%fused_computation | custom fusion | bytes 24576 | tf_op jit(solution)/shard_map/gather | solution.py:192
  159.6 7.2 %and_reduce_fusion = pred[16,16]{1,0:T(8,128)(4,1)S(1)} fusion(s32[16,128]{1,0:T(8,128)S(1)} %bitcast.95, s32[16,128]{1,0:T(8,128)S(1)} %iota_add_fusion), kind=kLoop, calls=%fused_computation.11 | loop fusion | flops 16776960 | bytes 16640 | tf_op jit(solution)/shard_map/reduce_or | solution.py:196
  172.4 1.9 scatter_custom_fusion.list_ref
  175.4 20.0 %scatter_custom_fusion.1 = bf16[2048,768]{1,0:T(8,128)(2,1)S(1)} fusion(s32[4096]{0:T(1024)S(1)} %bitcast.100, bf16[4096,768]{1,0:T(8,128)(2,1)} %bitcast.20, bf16[]{:T(256)} %constant.88.clone.1), kind=kCustom, calls=%fused_computation.19 | custom fusion | bytes 3146240 | tf_op jit(solution)/shard_map/scatter | solution.py:180
  195.4 1.5 fusion.25
  197.9 67.1 %shard_map.175 = (f32[2048,256]{1,0:T(8,128)}, f32[2048,128]{1,0:T(8,128)}, f32[2048,128]{1,0:T(8,128)}) custom-call(s32[256]{0:T(256)} %scatter_custom_fusion.list_ref, s32[16]{0:T(128)} %get-tuple-element.34.count_ref, bf16[2048,256]{1,0:T(8,128)(2,1)} %get-tuple-element.31.q_ref, bf16[2048,256]{1,0:T(8,128)(2,1)} %get-tuple-element.30.g_ref, ...), custom_call_target="tpu_custom_call" | custom-call | tf_op jit(solution)/shard_map/pallas_call | solution.py:107
  265.0 1.6 copy.119
  266.9 1.6 copy.117
  270.6 1.7 convert_element_type.27
  272.3 5.8 %collective-permute-done = bf16[2048,128]{1,0:T(8,128)(2,1)S(1)} collective-permute-done((bf16[2048,128]{1,0:T(8,128)(2,1)}, bf16[2048,128]{1,0:T(8,128)(2,1)S(1)}, u32[]{:S(2)}, u32[]{:S(2)}) %collective-permute-start) | collective-permute-done | bytes 524320 | tf_op jit(solution)/shard_map/ppermute | solution.py:233
  278.7 17.0 %gather_fusion.5 = bf16[4096,384]{1,0:T(8,128)(2,1)} fusion(bf16[2048,384]{1,0:T(8,128)(2,1)S(1)} %pad_maximum_fusion.1, s32[4096]{0:T(1024)S(1)} %broadcast_clamp_fusion), kind=kCustom, calls=%fused_computation.5 | custom fusion | bytes 6307840 | tf_op jit(solution)/shard_map/gather | solution.py:238
  295.7 14.5 %all-to-all-start.2 = ((bf16[128,32,384]{2,1,0:T(8,128)(2,1)}), bf16[128,32,384]{2,1,0:T(8,128)(2,1)S(1)}, u32[]{:S(2)}, u32[]{:S(2)}) async-start(bf16[128,32,384]{2,1,0:T(8,128)(2,1)} %bitcast.71), calls=%async_computation.2 | async-start | bytes 6291456 | tf_op jit(solution)/shard_map/all_to_all | solution.py:237
  310.5 40.9 %all-to-all-done.2 = bf16[128,32,384]{2,1,0:T(8,128)(2,1)S(1)} async-done(((bf16[128,32,384]{2,1,0:T(8,128)(2,1)}), bf16[128,32,384]{2,1,0:T(8,128)(2,1)S(1)}, u32[]{:S(2)}, u32[]{:S(2)}) %all-to-all-start.2) | async-done | bytes 3145760 | tf_op jit(solution)/shard_map/all_to_all | solution.py:237
  351.4 24.6 %gather_fusion.6 = bf16[2048,384]{1,0:T(8,128)(2,1)} fusion(bf16[16,8,32,384]{3,2,1,0:T(8,128)(2,1)S(1)} %bitcast.69, s32[2048]{0:T(1024)S(1)} %reshape.373), kind=kCustom, calls=%fused_computation.6 | custom fusion | bytes 3170304 | tf_op jit(solution)/shard_map/gather | solution.py:240
  376.1 1.6 bitcast_convert_fusion
  378.2 2.2 copy.132
  (91 shorter events, 24.7 us)
Async XLA Ops:
  13.0 41.6 %all-to-all-start = ((s32[128,32,1]{1,2,0:T(1,128)}), s32[128,32,1]{1,2,0:T(1,128)S(1)}, u32[]{:S(2)}, u32[]{:S(2)}) async-start(s32[128,32,1]{1,2,0:T(1,128)} %bitcast.8), calls=%async_computation | async-start | bytes 131072 | tf_op jit(solution)/shard_map/all_to_all | solution.py:178
  28.6 3.8 copy-start.6
  28.7 3.8 copy-start
  29.2 3.5 copy-start.1
  54.5 10.2 %copy-start.7 = (s32[1,16]{1,0:T(1,128)S(1)}, s32[1,16]{1,0:T(1,128)}, u32[]{:S(2)}) copy-start(s32[1,16]{1,0:T(1,128)} %param.21) | copy-start | bytes 196
  54.5 11.7 %copy-start.4 = (s32[1,256]{1,0:T(1,128)S(1)}, s32[1,256]{1,0:T(1,128)}, u32[]{:S(2)}) copy-start(s32[1,256]{1,0:T(1,128)} %param.22) | copy-start | bytes 3076
  54.5 120.8 %all-to-all-start.1 = ((bf16[128,32,768]{2,1,0:T(8,128)(2,1)}), bf16[128,32,768]{2,1,0:T(8,128)(2,1)}, u32[]{:S(2)}, u32[]{:S(2)}) async-start(bf16[128,32,768]{2,1,0:T(8,128)(2,1)} %bitcast.70), calls=%async_computation.1 | async-start | bytes 12582912 | tf_op jit(solution)/shard_map/all_to_all | solution.py:177
  64.8 94.8 %copy-start.2 = (s32[16,128]{1,0:T(8,128)}, s32[16,128]{1,0:T(8,128)S(1)}, u32[]{:S(2)}) copy-start(s32[16,128]{1,0:T(8,128)S(1)} %iota_add_fusion) | copy-start | bytes 24580
  147.8 21.5 %copy-start.8 = (s32[8]{0:T(128)S(1)}, s32[8]{0:T(128)}, u32[]{:S(2)}) copy-start(s32[8]{0:T(128)} %constant.101.clone) | copy-start | bytes 100
  159.6 37.3 %copy-start.3 = (s32[2048]{0:T(1024)}, s32[2048]{0:T(1024)S(1)}, u32[]{:S(2)}) copy-start(s32[2048]{0:T(1024)S(1)} %gather_fusion) | copy-start | bytes 24580
  269.9 8.3 %collective-permute-start = (bf16[2048,128]{1,0:T(8,128)(2,1)}, bf16[2048,128]{1,0:T(8,128)(2,1)S(1)}, u32[]{:S(2)}, u32[]{:S(2)}) collective-permute-start(bf16[2048,128]{1,0:T(8,128)(2,1)} %pad_maximum_fusion.2), channel_id=1, source_target_pairs={{0,2},{1,3},{2,0},{3,1},{4,6},{5,7},{6,4},{7,5},{8,10},{9,11},{10,... | collective-permute-start | bytes 1572872 | tf_op jit(solution)/shard_map/ppermute | solution.py:233
  295.7 14.5 %copy-start.5 = (s32[8]{0:T(128)S(1)}, s32[8]{0:T(128)}, u32[]{:S(2)}) copy-start(s32[8]{0:T(128)} %constant.149) | copy-start | bytes 100
  295.7 55.7 %all-to-all-start.2 = ((bf16[128,32,384]{2,1,0:T(8,128)(2,1)}), bf16[128,32,384]{2,1,0:T(8,128)(2,1)S(1)}, u32[]{:S(2)}, u32[]{:S(2)}) async-start(bf16[128,32,384]{2,1,0:T(8,128)(2,1)} %bitcast.71), calls=%async_computation.2 | async-start | bytes 6291456 | tf_op jit(solution)/shard_map/all_to_all | solution.py:237

commit v4 on v3

--- a/solution.py
+++ b/solution.py
@@ -162,18 +162,21 @@
         axis=2,
     )
     width = payload.shape[2]
+    flat_slot = pack_of * capacity + slot
     holder = (
-        jnp.zeros((packs, ctx_size, capacity, width), jnp.bfloat16)
-        .at[dest_pack, dest_ctx, dest_slot]
-        .set(payload)
+        jnp.zeros((packs * capacity, ctx_size * width), jnp.bfloat16)
+        .at[flat_slot]
+        .set(payload.reshape(local_rows, ctx_size * width))
+        .reshape(packs, capacity, ctx_size, width)
+        .transpose(0, 2, 1, 3)
         .reshape(devices * capacity, width)
     )
-    places = (
-        jnp.zeros((packs, ctx_size, capacity), jnp.int32)
-        .at[dest_pack, dest_ctx, dest_slot]
-        .set(jnp.broadcast_to((row_in_pack + 1)[:, None], (local_rows, ctx_size)))
-        .reshape(devices * capacity)
-    )
+    places = jnp.broadcast_to(
+        jnp.zeros((packs, 1, capacity), jnp.int32)
+        .at[pack_of, 0, slot]
+        .set(row_in_pack + 1),
+        (packs, ctx_size, capacity),
+    ).reshape(devices * capacity)
     got = lax.all_to_all(holder, ("dp", "ctx"), split_axis=0, concat_axis=0, tiled=True)
     got_places = lax.all_to_all(places, ("dp", "ctx"), split_axis=0, concat_axis=0, tiled=True)
     landing = jnp.where(got_places > 0, got_places - 1, pack_len)
@@ -189,11 +192,17 @@
         span_seq[:, None] * span_rows + jnp.arange(span_rows, dtype=jnp.int32)[None, :]
     ).reshape(-1)
     seq_docs = lax.all_gather(doc_ids[0], "ctx", axis=0, tiled=True)
-    doc_all = seq_docs[positions]
+    span_docs = seq_docs.reshape(span_seq.shape[0], span_rows)[span_seq]
+    doc_all = span_docs.reshape(-1)
 
     spans = pack_len // SPAN_ROWS
-    allowed_all = visible(positions, doc_all, positions, doc_all)
-    active = jnp.any(allowed_all.reshape(spans, SPAN_ROWS, spans, SPAN_ROWS), axis=(1, 3))
+    first_doc = span_docs[:, 0]
+    last_doc = span_docs[:, -1]
+    active = (
+        (span_seq[None, :] <= span_seq[:, None])
+        & (first_doc[None, :] <= last_doc[:, None])
+        & (first_doc[:, None] <= last_doc[None, :])
+    )
     span_count = jnp.sum(active.astype(jnp.int32), axis=1)
     rank = jnp.cumsum(active.astype(jnp.int32), axis=1) - 1
     slot_of = jnp.where(active, rank + spans * jnp.arange(spans)[:, None], spans * spans)
@@ -234,10 +243,13 @@
 
     result = jnp.concatenate([dquery.astype(jnp.bfloat16), key_value.astype(jnp.bfloat16)], axis=1)
     source_rows = jnp.where(landing < pack_len, landing, 0)
-    back = lax.all_to_all(
-        result[source_rows], ("dp", "ctx"), split_axis=0, concat_axis=0, tiled=True
-    ).reshape(packs, ctx_size, capacity, result.shape[1])
-    pieces = back[dest_pack, jnp.asarray(ctx_of_block, jnp.int32)[None, :], dest_slot].astype(jnp.float32)
+    back = (
+        lax.all_to_all(result[source_rows], ("dp", "ctx"), split_axis=0, concat_axis=0, tiled=True)
+        .reshape(packs, ctx_size, capacity, result.shape[1])
+        .transpose(0, 2, 1, 3)
+        .reshape(packs * capacity, ctx_size, result.shape[1])
+    )
+    pieces = back[flat_slot][:, ctx_of_block].astype(jnp.float32)
     return (
         pieces[:, :, :q_width].reshape(local_rows, q_cols),
         pieces[:, :, q_width : q_width + k_width].reshape(local_rows, k_cols),

time: 383 us -> 362 us (0.945)
  waiting for transfers between devices: 46.8 us -> 115 us
  blocking collectives: 81.5 us -> 22.1 us
  local copies, waits for them, and re-layouts: 128 us -> 115 us
  starting transfers between devices: 36.2 us -> 27.3 us
  other arithmetic: 19.1 us -> 10.4 us
    all_to_all x1, waiting for transfers between devices: 0.01 us -> 65.4 us  [local(): lax.all_to_all(holder, ('dp', 'ctx'), split_axis=0, concat_axis=0, tiled=...]
    all_gather x1, blocking collectives: 81.5 us -> 22.1 us  [local(): seq_docs = lax.all_gather(doc_ids[0], 'ctx', axis=0, tiled=True)]
    gather x2 -> x4, local copies, waits for them, and re-layouts: 36.4 us -> 4.53 us  [the longest x3 3.97 us: local(): pieces = back[flat_slot][:, ctx_of_block].astype(jnp.float32)]
    scatter x0 -> x2, local copies, waits for them, and re-layouts: none -> 21.2 us  [the longest x1 12.8 us: local(): places = jnp.broadcast_to(jnp.zeros((packs, 1, capacity), jnp.int32).at[p...]
    unnamed x33 -> x28, local copies, waits for them, and re-layouts: 33.7 us -> 13.5 us
    transpose x0 -> x3, local copies, waits for them, and re-layouts: none -> 8.05 us  [the longest x2 5.07 us: local(): holder = jnp.zeros((packs * capacity, ctx_size * width), jnp.bfloat16).at...]
    reduce_or x1 -> x0, other arithmetic: 7.23 us -> none  [local(): jnp.any(allowed_all.reshape(spans, SPAN_ROWS, spans, SPAN_ROWS), axis=(1,...]
    all_to_all x1, starting transfers between devices: 14.5 us -> 7.31 us  [local(): lax.all_to_all(result[source_rows], ('dp', 'ctx'), split_axis=0, concat_a...]
  transfers between devices with their start and end apart: 4 -> 4, of which waited for: 2 -> 3; matrix products, arithmetic and copies ran while one was open for 15% -> 12% of each run, Pallas kernels for 0% -> 0%
where the time goes in v4:
time: 362 us; the launch traced here: 361 us
  local copies, waits for them, and re-layouts  115 us (32%)
  waiting for transfers between devices  115 us (32%)
  Pallas kernels  67.1 us (19%)
  starting transfers between devices  27.3 us (8%)
  blocking collectives  22.1 us (6%)
  other arithmetic  10.4 us (3%)
  between operations  4.34 us (1%)
    pallas_call x1, Pallas kernels, attention(): pl.pallas_call(attention_kernel, grid_spec=pltpu.PrefetchScalarGridSpec(n...  67.1 us
    all_to_all x1, waiting for transfers between devices, local(): lax.all_to_all(holder, ('dp', 'ctx'), split_axis=0, concat_axis=0, tiled=...  65.4 us
    all_to_all x1, waiting for transfers between devices, local(): lax.all_to_all(result[source_rows], ('dp', 'ctx'), split_axis=0, concat_a...  41.2 us
    all_gather x1, blocking collectives, local(): seq_docs = lax.all_gather(doc_ids[0], 'ctx', axis=0, tiled=True)  22.1 us
    scatter x1, local copies, waits for them, and re-layouts, local(): jnp.zeros((pack_len, width), jnp.bfloat16).at[landing].set(got, mode='drop')  20.2 us
    gather x1, local copies, waits for them, and re-layouts, local(): result[source_rows]  17 us
    unnamed x28, local copies, waits for them, and re-layouts  13.5 us
    scatter x1, local copies, waits for them, and re-layouts, local(): places = jnp.broadcast_to(jnp.zeros((packs, 1, capacity), jnp.int32).at[p...  12.8 us
  transfers between devices with their start and end apart: 4, of which 3 were waited for; matrix products, arithmetic and copies ran while one was open for 12% of the time, Pallas kernels for 0%

profile of v4, /device:TPU:1, one launch (start us, length us, event | category | flops | bytes accessed | tf_op | source)
XLA Modules:
  0.0 361.5 jit_solution(9596179678619979558)
XLA Ops:
  0.7 22.1 %all-gather = s32[1,2048]{1,0:T(1,128)S(1)} all-gather(s32[1,256]{1,0:T(1,128)} %param.22), channel_id=2, replica_groups=mesh['dp'=16,'ctx'=8] {'ctx'}, dimensions={1}, use_global_device_ids=true | all-gather | bytes 9216 | tf_op jit(solution)/shard_map/all_gather | solution.py:194
  28.4 12.8 %scatter_fusion = s32[16,32]{1,0:T(8,128)S(1)} fusion(s32[16,32]{1,0:T(8,128)S(1)} %broadcast.276, s32[256]{0:T(256)S(1)} %bitcast.80, s32[256]{0:T(256)S(1)} %get-tuple-element.35), kind=kCustom, calls=%fused_computation.9 | custom fusion | bytes 5120 | tf_op jit(solution)/shard_map/scatter | solution.py:177
  41.8 8.5 %all-to-all-start = ((s32[128,32,1]{1,2,0:T(1,128)}), s32[128,32,1]{1,2,0:T(1,128)S(1)}, u32[]{:S(2)}, u32[]{:S(2)}) async-start(s32[128,32,1]{1,2,0:T(1,128)} %bitcast.10), calls=%async_computation | async-start | bytes 131072 | tf_op jit(solution)/shard_map/all_to_all | solution.py:181
  59.4 1.6 gather_fusion.1
  61.0 2.0 pad_maximum_fusion
  63.0 2.8 copy.98
  65.8 3.2 copy.99
  69.0 8.4 %scatter_custom_fusion.2 = bf16[512,6144]{1,0:T(8,128)(2,1)} fusion(s32[256]{0:T(256)S(1)} %compare_select_fusion.6, bf16[256,6144]{1,0:T(8,128)(2,1)S(1)} %copy.99, bf16[]{:T(256)} %constant.81.clone.1), kind=kCustom, calls=%fused_computation.15 | custom fusion | bytes 6291458 | tf_op jit(solution)/shard_map/scatter | solution.py:169
  77.4 4.8 %copy.120 = bf16[64,8,8,768]{3,2,1,0:T(8,128)(2,1)S(1)} copy(bf16[64,8,8,768]{3,1,2,0:T(8,128)(2,1)} %bitcast.78) | data formatting | bytes 12582912
  82.8 4.5 %copy.100 = bf16[16,8,32,768]{3,2,1,0:T(8,128)(2,1)} copy(bf16[16,8,32,768]{3,1,2,0:T(8,128)(2,1)S(1)} %bitcast_bitcast_fusion) | data formatting | bytes 12582912 | tf_op jit(solution)/shard_map/transpose | solution.py:171
  87.3 10.2 %all-to-all-start.1 = ((bf16[128,32,768]{2,1,0:T(8,128)(2,1)}), bf16[128,32,768]{2,1,0:T(8,128)(2,1)}, u32[]{:S(2)}, u32[]{:S(2)}) async-start(bf16[128,32,768]{2,1,0:T(8,128)(2,1)} %bitcast.77), calls=%async_computation.1 | async-start | bytes 12582912 | tf_op jit(solution)/shard_map/all_to_all | solution.py:180
  103.6 1.9 scatter_custom_fusion.list_ref
  106.5 65.4 %all-to-all-done.1 = bf16[128,32,768]{2,1,0:T(8,128)(2,1)} async-done(((bf16[128,32,768]{2,1,0:T(8,128)(2,1)}), bf16[128,32,768]{2,1,0:T(8,128)(2,1)}, u32[]{:S(2)}, u32[]{:S(2)}) %all-to-all-start.1) | async-done | bytes 6291488 | tf_op jit(solution)/shard_map/all_to_all | solution.py:180
  171.9 20.2 %scatter_custom_fusion.3 = bf16[2048,768]{1,0:T(8,128)(2,1)S(1)} fusion(s32[4096]{0:T(1024)S(1)} %bitcast.110, bf16[4096,768]{1,0:T(8,128)(2,1)} %bitcast.23, bf16[]{:T(256)} %constant.81.clone.1), kind=kCustom, calls=%fused_computation.18 | custom fusion | bytes 3146240 | tf_op jit(solution)/shard_map/scatter | solution.py:183
  194.7 67.1 %shard_map.175 = (f32[2048,256]{1,0:T(8,128)}, f32[2048,128]{1,0:T(8,128)}, f32[2048,128]{1,0:T(8,128)}) custom-call(s32[256]{0:T(256)} %scatter_custom_fusion.list_ref, s32[16]{0:T(128)} %get-tuple-element.33.count_ref, bf16[2048,256]{1,0:T(8,128)(2,1)} %get-tuple-element.30.q_ref, bf16[2048,256]{1,0:T(8,128)(2,1)} %get-tuple-element.29.g_ref, ...), custom_call_target="tpu_custom_call" | custom-call | tf_op jit(solution)/shard_map/pallas_call | solution.py:107
  268.7 1.7 convert_element_type.27
  270.4 8.9 %collective-permute-done = bf16[2048,128]{1,0:T(8,128)(2,1)S(1)} collective-permute-done((bf16[2048,128]{1,0:T(8,128)(2,1)}, bf16[2048,128]{1,0:T(8,128)(2,1)S(1)}, u32[]{:S(2)}, u32[]{:S(2)}) %collective-permute-start) | collective-permute-done | bytes 524320 | tf_op jit(solution)/shard_map/ppermute | solution.py:242
  279.7 17.0 %gather_fusion.5 = bf16[4096,384]{1,0:T(8,128)(2,1)} fusion(bf16[2048,384]{1,0:T(8,128)(2,1)S(1)} %pad_maximum_fusion.1, s32[4096]{0:T(1024)S(1)} %broadcast_clamp_fusion), kind=kCustom, calls=%fused_computation.5 | custom fusion | bytes 6307840 | tf_op jit(solution)/shard_map/gather | solution.py:247
  296.8 7.3 %all-to-all-start.2 = ((bf16[128,32,384]{2,1,0:T(8,128)(2,1)}), bf16[128,32,384]{2,1,0:T(8,128)(2,1)S(1)}, u32[]{:S(2)}, u32[]{:S(2)}) async-start(bf16[128,32,384]{2,1,0:T(8,128)(2,1)} %bitcast.81), calls=%async_computation.2 | async-start | bytes 6291456 | tf_op jit(solution)/shard_map/all_to_all | solution.py:247
  304.1 41.2 %all-to-all-done.2 = bf16[128,32,384]{2,1,0:T(8,128)(2,1)S(1)} async-done(((bf16[128,32,384]{2,1,0:T(8,128)(2,1)}), bf16[128,32,384]{2,1,0:T(8,128)(2,1)S(1)}, u32[]{:S(2)}, u32[]{:S(2)}) %all-to-all-start.2) | async-done | bytes 3145760 | tf_op jit(solution)/shard_map/all_to_all | solution.py:247
  345.3 3.0 copy.109
  348.3 2.9 gather_fusion.6
  354.0 1.9 copy.111
  355.9 3.0 copy.114
  (90 shorter events, 35.0 us)
Async XLA Ops:
  0.6 50.9 %copy-start.7 = (s32[8]{0:T(128)S(1)}, s32[8]{0:T(128)}, u32[]{:S(2)}) copy-start(s32[8]{0:T(128)} %constant.124) | copy-start | bytes 100
  0.6 51.0 %copy-start.2 = (bf16[256,512]{1,0:T(8,128)(2,1)S(1)}, bf16[256,512]{1,0:T(8,128)(2,1)}, u32[]{:S(2)}) copy-start(bf16[256,512]{1,0:T(8,128)(2,1)} %param.17) | copy-start | bytes 786436
  24.0 75.1 %copy-start.3 = (s32[16,128]{1,0:T(8,128)}, s32[16,128]{1,0:T(8,128)S(1)}, u32[]{:S(2)}) copy-start(s32[16,128]{1,0:T(8,128)S(1)} %gather_fusion) | copy-start | bytes 24580
  28.4 26.4 %copy-start.1 = (bf16[256,2048]{1,0:T(8,128)(2,1)S(1)}, bf16[256,2048]{1,0:T(8,128)(2,1)}, u32[]{:S(2)}) copy-start(bf16[256,2048]{1,0:T(8,128)(2,1)} %param.19) | copy-start | bytes 3145732
  41.8 45.5 %all-to-all-start = ((s32[128,32,1]{1,2,0:T(1,128)}), s32[128,32,1]{1,2,0:T(1,128)S(1)}, u32[]{:S(2)}, u32[]{:S(2)}) async-start(s32[128,32,1]{1,2,0:T(1,128)} %bitcast.10), calls=%async_computation | async-start | bytes 131072 | tf_op jit(solution)/shard_map/all_to_all | solution.py:181
  51.9 3.9 %copy-start.6 = (s32[8]{0:T(128)S(1)}, s32[8]{0:T(128)}, u32[]{:S(2)}) copy-start(s32[8]{0:T(128)} %constant.122) | copy-start | bytes 100
  87.3 10.3 %copy-start.5 = (s32[1,16]{1,0:T(1,128)S(1)}, s32[1,16]{1,0:T(1,128)}, u32[]{:S(2)}) copy-start(s32[1,16]{1,0:T(1,128)} %param.21) | copy-start | bytes 196
  87.3 13.1 %copy-start.8 = (s32[8]{0:T(128)S(1)}, s32[8]{0:T(128)}, u32[]{:S(2)}) copy-start(s32[8]{0:T(128)} %constant.97.clone) | copy-start | bytes 100
  87.3 84.6 %all-to-all-start.1 = ((bf16[128,32,768]{2,1,0:T(8,128)(2,1)}), bf16[128,32,768]{2,1,0:T(8,128)(2,1)}, u32[]{:S(2)}, u32[]{:S(2)}) async-start(bf16[128,32,768]{2,1,0:T(8,128)(2,1)} %bitcast.77), calls=%async_computation.1 | async-start | bytes 12582912 | tf_op jit(solution)/shard_map/all_to_all | solution.py:180
  97.6 96.0 %copy-start.4 = (s32[16,128]{1,0:T(8,128)}, s32[16,128]{1,0:T(8,128)S(1)}, u32[]{:S(2)}) copy-start(s32[16,128]{1,0:T(8,128)S(1)} %iota_add_fusion) | copy-start | bytes 24580
  266.6 12.6 %collective-permute-start = (bf16[2048,128]{1,0:T(8,128)(2,1)}, bf16[2048,128]{1,0:T(8,128)(2,1)S(1)}, u32[]{:S(2)}, u32[]{:S(2)}) collective-permute-start(bf16[2048,128]{1,0:T(8,128)(2,1)} %pad_maximum_fusion.2), channel_id=1, source_target_pairs={{0,2},{1,3},{2,0},{3,1},{4,6},{5,7},{6,4},{7,5},{8,10},{9,11},{10,... | collective-permute-start | bytes 1572872 | tf_op jit(solution)/shard_map/ppermute | solution.py:242
  296.8 48.5 %all-to-all-start.2 = ((bf16[128,32,384]{2,1,0:T(8,128)(2,1)}), bf16[128,32,384]{2,1,0:T(8,128)(2,1)S(1)}, u32[]{:S(2)}, u32[]{:S(2)}) async-start(bf16[128,32,384]{2,1,0:T(8,128)(2,1)} %bitcast.81), calls=%async_computation.2 | async-start | bytes 6291456 | tf_op jit(solution)/shard_map/all_to_all | solution.py:247
  355.9 3.0 copy-start

commit v5 on v4

--- a/solution.py
+++ b/solution.py
@@ -11,7 +11,7 @@
 DH = 128
 
 
-SPAN_ROWS = 128
+SPAN_ROWS = 256
 
 
 def attention_kernel(
@@ -179,27 +179,32 @@
     ).reshape(devices * capacity)
     got = lax.all_to_all(holder, ("dp", "ctx"), split_axis=0, concat_axis=0, tiled=True)
     got_places = lax.all_to_all(places, ("dp", "ctx"), split_axis=0, concat_axis=0, tiled=True)
-    landing = jnp.where(got_places > 0, got_places - 1, pack_len)
+    span_seq = span_order[0]
+    span_rows = pack_len // span_seq.shape[0]
+    slot_pos = jnp.concatenate(
+        [
+            (span_seq[:, None] * span_rows + jnp.arange(span_rows, dtype=jnp.int32)[None, :]).reshape(-1),
+            jnp.full((1,), pack_len, jnp.int32),
+        ]
+    )
+    landing = slot_pos[jnp.where(got_places > 0, got_places - 1, pack_len)]
     rows = jnp.zeros((pack_len, width), jnp.bfloat16).at[landing].set(got, mode="drop")
     query = rows[:, :q_width]
     grad_rows = rows[:, q_width : 2 * q_width]
     keys = rows[:, 2 * q_width : 2 * q_width + DH]
     values = rows[:, 2 * q_width + DH : 2 * q_width + 2 * DH]
 
-    span_seq = span_order[0]
-    span_rows = pack_len // span_seq.shape[0]
-    positions = (
-        span_seq[:, None] * span_rows + jnp.arange(span_rows, dtype=jnp.int32)[None, :]
-    ).reshape(-1)
-    seq_docs = lax.all_gather(doc_ids[0], "ctx", axis=0, tiled=True)
-    span_docs = seq_docs.reshape(span_seq.shape[0], span_rows)[span_seq]
-    doc_all = span_docs.reshape(-1)
+    doc_block = jnp.broadcast_to(doc_ids[0].astype(jnp.bfloat16)[:, None], (local_rows, 128))
+    doc_all = lax.all_gather(doc_block, "ctx", axis=0, tiled=True)[:, 0].astype(jnp.int32)
+    positions = jnp.arange(pack_len, dtype=jnp.int32)
 
     spans = pack_len // SPAN_ROWS
-    first_doc = span_docs[:, 0]
-    last_doc = span_docs[:, -1]
+    tile_docs = doc_all.reshape(spans, SPAN_ROWS)
+    first_doc = tile_docs[:, 0]
+    last_doc = tile_docs[:, -1]
+    tile_ids = jnp.arange(spans)
     active = (
-        (span_seq[None, :] <= span_seq[:, None])
+        (tile_ids[None, :] <= tile_ids[:, None])
         & (first_doc[None, :] <= last_doc[:, None])
         & (first_doc[:, None] <= last_doc[None, :])
     )

time: 362 us -> 352 us (0.972)
  waiting for transfers between devices: 115 us -> 45.9 us
  blocking collectives: 22.1 us -> 83 us
  Pallas kernels: 67.1 us -> 36.2 us
  local copies, waits for them, and re-layouts: 115 us -> 136 us
  starting transfers between devices: 27.3 us -> 35.1 us
    all_to_all x1, waiting for transfers between devices: 65.4 us -> 0.01 us  [local(): lax.all_to_all(holder, ('dp', 'ctx'), split_axis=0, concat_axis=0, tiled=...]
    all_gather x1, blocking collectives: 22.1 us -> 83 us  [local(): lax.all_gather(doc_block, 'ctx', axis=0, tiled=True)[:, 0].astype(jnp.int32)]
    pallas_call x1, Pallas kernels: 67.1 us -> 36.2 us  [attention(): pl.pallas_call(attention_kernel, grid_spec=pltpu.PrefetchScalarGridSpec(n...]
    gather x1, local copies, waits for them, and re-layouts: 0.56 us -> 23 us  [local(): landing = slot_pos[jnp.where(got_places > 0, got_places - 1, pack_len)]]
    all_to_all x1, starting transfers between devices: 7.31 us -> 13.4 us  [local(): lax.all_to_all(result[source_rows], ('dp', 'ctx'), split_axis=0, concat_a...]
    ppermute x1, waiting for transfers between devices: 8.85 us -> 4.67 us  [local(): key_value = mine + lax.ppermute(other, 'ctx', partner).astype(jnp.float32)]
  transfers between devices with their start and end apart: 4 -> 4, of which waited for: 3 -> 2; matrix products, arithmetic and copies ran while one was open for 12% -> 19% of each run, Pallas kernels for 0% -> 0%
where the time goes in v5:
time: 352 us; the launch traced here: 351 us
  local copies, waits for them, and re-layouts  136 us (39%)
  blocking collectives  83 us (24%)
  waiting for transfers between devices  45.9 us (13%)
  Pallas kernels  36.2 us (10%)
  starting transfers between devices  35.1 us (10%)
  other arithmetic  10.7 us (3%)
  between operations  3.97 us (1%)
    all_gather x1, blocking collectives, local(): lax.all_gather(doc_block, 'ctx', axis=0, tiled=True)[:, 0].astype(jnp.int32)  83 us
    all_to_all x1, waiting for transfers between devices, local(): lax.all_to_all(result[source_rows], ('dp', 'ctx'), split_axis=0, concat_a...  41.2 us
    pallas_call x1, Pallas kernels, attention(): pl.pallas_call(attention_kernel, grid_spec=pltpu.PrefetchScalarGridSpec(n...  36.2 us
    gather x1, local copies, waits for them, and re-layouts, local(): landing = slot_pos[jnp.where(got_places > 0, got_places - 1, pack_len)]  23 us
    scatter x1, local copies, waits for them, and re-layouts, local(): jnp.zeros((pack_len, width), jnp.bfloat16).at[landing].set(got, mode='drop')  20.3 us
    gather x1, local copies, waits for them, and re-layouts, local(): result[source_rows]  17 us
    all_to_all x1, starting transfers between devices, local(): lax.all_to_all(result[source_rows], ('dp', 'ctx'), split_axis=0, concat_a...  13.4 us
    scatter x1, local copies, waits for them, and re-layouts, local(): places = jnp.broadcast_to(jnp.zeros((packs, 1, capacity), jnp.int32).at[p...  12.8 us
  transfers between devices with their start and end apart: 4, of which 2 were waited for; matrix products, arithmetic and copies ran while one was open for 19% of the time, Pallas kernels for 0%

profile of v5, /device:TPU:1, one launch (start us, length us, event | category | flops | bytes accessed | tf_op | source)
XLA Modules:
  0.0 350.9 jit_solution(16409657192687713060)
XLA Ops:
  2.4 12.8 %scatter_fusion = s32[16,32]{1,0:T(8,128)S(1)} fusion(s32[16,32]{1,0:T(8,128)S(1)} %broadcast.254, s32[256]{0:T(256)S(1)} %bitcast.80, s32[256]{0:T(256)S(1)} %get-tuple-element.35), kind=kCustom, calls=%fused_computation.9 | custom fusion | bytes 5120 | tf_op jit(solution)/shard_map/scatter | solution.py:177
  15.8 11.5 %all-to-all-start = ((s32[128,32,1]{1,2,0:T(1,128)}), s32[128,32,1]{1,2,0:T(1,128)S(1)}, u32[]{:S(2)}, u32[]{:S(2)}) async-start(s32[128,32,1]{1,2,0:T(1,128)} %bitcast.10), calls=%async_computation | async-start | bytes 131072 | tf_op jit(solution)/shard_map/all_to_all | solution.py:181
  31.0 1.6 gather_fusion.1
  32.6 1.6 gather_fusion.2
  37.7 2.0 pad_maximum_fusion
  39.7 2.8 copy.105
  42.5 3.2 copy.106
  45.7 8.4 %scatter_custom_fusion.2 = bf16[512,6144]{1,0:T(8,128)(2,1)} fusion(s32[256]{0:T(256)S(1)} %compare_select_fusion.6, bf16[256,6144]{1,0:T(8,128)(2,1)S(1)} %copy.106, bf16[]{:T(256)} %constant.82.clone.1), kind=kCustom, calls=%fused_computation.15 | custom fusion | bytes 6291458 | tf_op jit(solution)/shard_map/scatter | solution.py:169
  54.1 4.8 %copy.128 = bf16[64,8,8,768]{3,2,1,0:T(8,128)(2,1)S(1)} copy(bf16[64,8,8,768]{3,1,2,0:T(8,128)(2,1)} %bitcast.78) | data formatting | bytes 12582912
  59.5 4.5 %copy.107 = bf16[16,8,32,768]{3,2,1,0:T(8,128)(2,1)} copy(bf16[16,8,32,768]{3,1,2,0:T(8,128)(2,1)S(1)} %bitcast_bitcast_fusion) | data formatting | bytes 12582912 | tf_op jit(solution)/shard_map/transpose | solution.py:171
  64.0 10.2 %all-to-all-start.1 = ((bf16[128,32,768]{2,1,0:T(8,128)(2,1)}), bf16[128,32,768]{2,1,0:T(8,128)(2,1)}, u32[]{:S(2)}, u32[]{:S(2)}) async-start(bf16[128,32,768]{2,1,0:T(8,128)(2,1)} %bitcast.77), calls=%async_computation.1 | async-start | bytes 12582912 | tf_op jit(solution)/shard_map/all_to_all | solution.py:180
  74.2 83.0 %all-gather = bf16[1,2048]{1,0:T(2,128)(2,1)S(1)} all-gather(bf16[1,256]{1,0:T(2,128)(2,1)S(1)} %convert_element_type.56), channel_id=3, replica_groups=mesh['dp'=16,'ctx'=8] {'ctx'}, dimensions={1}, use_global_device_ids=true | all-gather | bytes 4608 | tf_op jit(solution)/shard_map/all_gather | solution.py:198
  164.1 23.0 %gather_fusion = s32[4096]{0:T(1024)S(1)} fusion(s32[2049]{0:T(1024)S(1)} %pad_add_fusion, s32[4096]{0:T(1024)S(1)} %broadcast_clamp_fusion.1), kind=kCustom, calls=%fused_computation | custom fusion | bytes 49152 | tf_op jit(solution)/shard_map/gather | solution.py:190
  187.2 20.3 %scatter_custom_fusion.3 = bf16[2048,768]{1,0:T(8,128)(2,1)S(1)} fusion(s32[4096]{0:T(1024)S(1)} %bitcast.107, bf16[4096,768]{1,0:T(8,128)(2,1)} %bitcast.25, bf16[]{:T(256)} %constant.82.clone.1), kind=kCustom, calls=%fused_computation.18 | custom fusion | bytes 3146240 | tf_op jit(solution)/shard_map/scatter | solution.py:191
  211.6 36.2 %shard_map.175 = (f32[2048,256]{1,0:T(8,128)}, f32[2048,128]{1,0:T(8,128)}, f32[2048,128]{1,0:T(8,128)}) custom-call(s32[64]{0:T(128)} %scatter_custom_fusion.list_ref, s32[8]{0:T(128)} %get-tuple-element.36.count_ref, bf16[2048,256]{1,0:T(8,128)(2,1)} %get-tuple-element.28.q_ref, bf16[2048,256]{1,0:T(8,128)(2,1)} %get-tuple-element.27.g_ref, ...), custom_call_target="tpu_custom_call" | custom-call | tf_op jit(solution)/shard_map/pallas_call | solution.py:107
  255.2 1.7 convert_element_type.66
  256.9 4.7 %collective-permute-done = bf16[2048,128]{1,0:T(8,128)(2,1)} collective-permute-done((bf16[2048,128]{1,0:T(8,128)(2,1)}, bf16[2048,128]{1,0:T(8,128)(2,1)}, u32[]{:S(2)}, u32[]{:S(2)}) %collective-permute-start) | collective-permute-done | bytes 524320 | tf_op jit(solution)/shard_map/ppermute | solution.py:247
  263.1 17.0 %gather_fusion.5 = bf16[4096,384]{1,0:T(8,128)(2,1)} fusion(bf16[2048,384]{1,0:T(8,128)(2,1)S(1)} %pad_maximum_fusion.1, s32[4096]{0:T(1024)S(1)} %broadcast_clamp_fusion), kind=kCustom, calls=%fused_computation.5 | custom fusion | bytes 6307840 | tf_op jit(solution)/shard_map/gather | solution.py:252
  280.1 13.4 %all-to-all-start.2 = ((bf16[128,32,384]{2,1,0:T(8,128)(2,1)}), bf16[128,32,384]{2,1,0:T(8,128)(2,1)S(1)}, u32[]{:S(2)}, u32[]{:S(2)}) async-start(bf16[128,32,384]{2,1,0:T(8,128)(2,1)} %bitcast.81), calls=%async_computation.2 | async-start | bytes 6291456 | tf_op jit(solution)/shard_map/all_to_all | solution.py:252
  293.5 41.2 %all-to-all-done.2 = bf16[128,32,384]{2,1,0:T(8,128)(2,1)S(1)} async-done(((bf16[128,32,384]{2,1,0:T(8,128)(2,1)}), bf16[128,32,384]{2,1,0:T(8,128)(2,1)S(1)}, u32[]{:S(2)}, u32[]{:S(2)}) %all-to-all-start.2) | async-done | bytes 3145760 | tf_op jit(solution)/shard_map/all_to_all | solution.py:252
  334.7 3.0 copy.115
  337.7 2.9 gather_fusion.6
  343.4 1.9 copy.117
  345.3 3.0 copy.120
  (95 shorter events, 32.5 us)
Async XLA Ops:
  0.6 27.3 %copy-start.1 = (bf16[256,2048]{1,0:T(8,128)(2,1)S(1)}, bf16[256,2048]{1,0:T(8,128)(2,1)}, u32[]{:S(2)}) copy-start(bf16[256,2048]{1,0:T(8,128)(2,1)} %param.16) | copy-start | bytes 3145732
  15.8 48.2 %all-to-all-start = ((s32[128,32,1]{1,2,0:T(1,128)}), s32[128,32,1]{1,2,0:T(1,128)S(1)}, u32[]{:S(2)}, u32[]{:S(2)}) async-start(s32[128,32,1]{1,2,0:T(1,128)} %bitcast.10), calls=%async_computation | async-start | bytes 131072 | tf_op jit(solution)/shard_map/all_to_all | solution.py:181
  30.5 3.8 %copy-start.5 = (s32[8]{0:T(128)S(1)}, s32[8]{0:T(128)}, u32[]{:S(2)}) copy-start(s32[8]{0:T(128)} %constant.127) | copy-start | bytes 100
  30.5 3.8 %copy-start.2 = (bf16[256,512]{1,0:T(8,128)(2,1)S(1)}, bf16[256,512]{1,0:T(8,128)(2,1)}, u32[]{:S(2)}) copy-start(bf16[256,512]{1,0:T(8,128)(2,1)} %param.17) | copy-start | bytes 786436
  31.0 3.5 %copy-start.3 = (bf16[256,512]{1,0:T(8,128)(2,1)S(1)}, bf16[256,512]{1,0:T(8,128)(2,1)}, u32[]{:S(2)}) copy-start(bf16[256,512]{1,0:T(8,128)(2,1)} %param.18) | copy-start | bytes 786436
  64.0 10.2 %copy-start.4 = (s32[1,256]{1,0:T(1,128)S(1)}, s32[1,256]{1,0:T(1,128)}, u32[]{:S(2)}) copy-start(s32[1,256]{1,0:T(1,128)} %param.22) | copy-start | bytes 3076
  64.0 96.6 %copy-start.7 = (s32[8]{0:T(128)S(1)}, s32[8]{0:T(128)}, u32[]{:S(2)}) copy-start(s32[8]{0:T(128)} %constant.100.clone) | copy-start | bytes 100
  64.0 99.6 %copy-start.6 = (s32[1,16]{1,0:T(1,128)S(1)}, s32[1,16]{1,0:T(1,128)}, u32[]{:S(2)}) copy-start(s32[1,16]{1,0:T(1,128)} %param.21) | copy-start | bytes 196
  64.0 123.2 %all-to-all-start.1 = ((bf16[128,32,768]{2,1,0:T(8,128)(2,1)}), bf16[128,32,768]{2,1,0:T(8,128)(2,1)}, u32[]{:S(2)}, u32[]{:S(2)}) async-start(bf16[128,32,768]{2,1,0:T(8,128)(2,1)} %bitcast.77), calls=%async_computation.1 | async-start | bytes 12582912 | tf_op jit(solution)/shard_map/all_to_all | solution.py:180
  252.6 8.9 %collective-permute-start = (bf16[2048,128]{1,0:T(8,128)(2,1)}, bf16[2048,128]{1,0:T(8,128)(2,1)}, u32[]{:S(2)}, u32[]{:S(2)}) collective-permute-start(bf16[2048,128]{1,0:T(8,128)(2,1)} %pad_maximum_fusion.2), channel_id=1, source_target_pairs={{0,2},{1,3},{2,0},{3,1},{4,6},{5,7},{6,4},{7,5},{8,10},{9,11},{10,... | collective-permute-start | bytes 1572872 | tf_op jit(solution)/shard_map/ppermute | solution.py:247
  280.1 54.6 %all-to-all-start.2 = ((bf16[128,32,384]{2,1,0:T(8,128)(2,1)}), bf16[128,32,384]{2,1,0:T(8,128)(2,1)S(1)}, u32[]{:S(2)}, u32[]{:S(2)}) async-start(bf16[128,32,384]{2,1,0:T(8,128)(2,1)} %bitcast.81), calls=%async_computation.2 | async-start | bytes 6291456 | tf_op jit(solution)/shard_map/all_to_all | solution.py:252
  345.3 3.0 copy-start

commit v6 on v5

--- a/solution.py
+++ b/solution.py
@@ -163,31 +163,36 @@
     )
     width = payload.shape[2]
     flat_slot = pack_of * capacity + slot
+    picks = jnp.arange(packs * capacity, dtype=jnp.int32)[:, None] == flat_slot[None, :]
     holder = (
-        jnp.zeros((packs * capacity, ctx_size * width), jnp.bfloat16)
-        .at[flat_slot]
-        .set(payload.reshape(local_rows, ctx_size * width))
+        jnp.dot(
+            picks.astype(jnp.bfloat16),
+            payload.reshape(local_rows, ctx_size * width),
+            preferred_element_type=jnp.float32,
+        )
+        .astype(jnp.bfloat16)
         .reshape(packs, capacity, ctx_size, width)
         .transpose(0, 2, 1, 3)
         .reshape(devices * capacity, width)
     )
     places = jnp.broadcast_to(
-        jnp.zeros((packs, 1, capacity), jnp.int32)
-        .at[pack_of, 0, slot]
-        .set(row_in_pack + 1),
+        jnp.sum(jnp.where(picks, (row_in_pack + 1)[None, :], 0), axis=1).reshape(packs, 1, capacity),
         (packs, ctx_size, capacity),
     ).reshape(devices * capacity)
     got = lax.all_to_all(holder, ("dp", "ctx"), split_axis=0, concat_axis=0, tiled=True)
     got_places = lax.all_to_all(places, ("dp", "ctx"), split_axis=0, concat_axis=0, tiled=True)
     span_seq = span_order[0]
     span_rows = pack_len // span_seq.shape[0]
-    slot_pos = jnp.concatenate(
-        [
-            (span_seq[:, None] * span_rows + jnp.arange(span_rows, dtype=jnp.int32)[None, :]).reshape(-1),
-            jnp.full((1,), pack_len, jnp.int32),
-        ]
-    )
-    landing = slot_pos[jnp.where(got_places > 0, got_places - 1, pack_len)]
+    packed_row = got_places - 1
+    span_pos = jnp.sum(
+        jnp.where(
+            (packed_row // span_rows)[:, None] == jnp.arange(span_seq.shape[0], dtype=jnp.int32)[None, :],
+            span_seq[None, :],
+            0,
+        ),
+        axis=1,
+    )
+    landing = jnp.where(packed_row >= 0, span_pos * span_rows + packed_row % span_rows, pack_len)
     rows = jnp.zeros((pack_len, width), jnp.bfloat16).at[landing].set(got, mode="drop")
     query = rows[:, :q_width]
     grad_rows = rows[:, q_width : 2 * q_width]

time: 352 us -> 303 us (0.86)
  local copies, waits for them, and re-layouts: 136 us -> 85.5 us
    gather x1 -> x0, local copies, waits for them, and re-layouts: 23 us -> none  [local(): landing = slot_pos[jnp.where(got_places > 0, got_places - 1, pack_len)]]
    scatter x2 -> x0, local copies, waits for them, and re-layouts: 21.2 us -> none  [the longest x1 12.8 us: local(): places = jnp.broadcast_to(jnp.zeros((packs, 1, capacity), jnp.int32).at[p...]
    unnamed x28 -> x24, local copies, waits for them, and re-layouts: 12.7 us -> 11.9 us
  transfers between devices with their start and end apart: 4 -> 4, of which waited for: 2 -> 2; matrix products, arithmetic and copies ran while one was open for 19% -> 11% of each run, Pallas kernels for 0% -> 0%
where the time goes in v6:
time: 303 us; the launch traced here: 302 us
  local copies, waits for them, and re-layouts  85.5 us (28%)
  blocking collectives  83 us (27%)
  waiting for transfers between devices  45.9 us (15%)
  Pallas kernels  36.2 us (12%)
  starting transfers between devices  34.1 us (11%)
  other arithmetic  11.6 us (4%)
  between operations  3.95 us (1%)
    all_gather x1, blocking collectives, local(): lax.all_gather(doc_block, 'ctx', axis=0, tiled=True)[:, 0].astype(jnp.int32)  83 us
    all_to_all x1, waiting for transfers between devices, local(): lax.all_to_all(result[source_rows], ('dp', 'ctx'), split_axis=0, concat_a...  41.2 us
    pallas_call x1, Pallas kernels, attention(): pl.pallas_call(attention_kernel, grid_spec=pltpu.PrefetchScalarGridSpec(n...  36.2 us
    scatter x1, local copies, waits for them, and re-layouts, local(): jnp.zeros((pack_len, width), jnp.bfloat16).at[landing].set(got, mode='drop')  20 us
    gather x1, local copies, waits for them, and re-layouts, local(): result[source_rows]  17 us
    all_to_all x1, starting transfers between devices, local(): lax.all_to_all(result[source_rows], ('dp', 'ctx'), split_axis=0, concat_a...  12.4 us
    unnamed x24, local copies, waits for them, and re-layouts  11.9 us
    all_to_all x1, starting transfers between devices, local(): lax.all_to_all(places, ('dp', 'ctx'), split_axis=0, concat_axis=0, tiled=...  11.5 us
  transfers between devices with their start and end apart: 4, of which 2 were waited for; matrix products, arithmetic and copies ran while one was open for 11% of the time, Pallas kernels for 0%

profile of v6, /device:TPU:1, one launch (start us, length us, event | category | flops | bytes accessed | tf_op | source)
XLA Modules:
  0.0 301.9 jit_solution(3308140355560171980)
XLA Ops:
  3.1 11.5 %all-to-all-start = ((s32[128,32,1]{1,2,0:T(1,128)}), s32[128,32,1]{1,2,0:T(1,128)S(1)}, u32[]{:S(2)}, u32[]{:S(2)}) async-start(s32[128,32,1]{1,2,0:T(1,128)} %bitcast.5), calls=%async_computation | async-start | bytes 131072 | tf_op jit(solution)/shard_map/all_to_all | solution.py:183
  15.3 1.5 copy.98
  17.3 1.5 copy.100
  24.3 2.7 pad_maximum_fusion
  27.0 3.2 %copy.106 = bf16[256,8,768]{0,2,1:T(8,128)(2,1)S(1)} copy(bf16[256,8,768]{2,0,1:T(8,128)(2,1)} %pad_maximum_fusion) | data formatting | bytes 6291456 | tf_op jit(solution)/shard_map/concatenate | solution.py:155
  30.2 1.8 convolution_convert_fusion
  32.0 2.0 copy.128
  34.6 4.5 %copy.107 = bf16[16,8,32,768]{3,2,1,0:T(8,128)(2,1)} copy(bf16[16,8,32,768]{3,1,2,0:T(8,128)(2,1)S(1)} %bitcast_bitcast_fusion) | data formatting | bytes 12582912 | tf_op jit(solution)/shard_map/transpose | solution.py:175
  39.1 10.2 %all-to-all-start.1 = ((bf16[128,32,768]{2,1,0:T(8,128)(2,1)}), bf16[128,32,768]{2,1,0:T(8,128)(2,1)}, u32[]{:S(2)}, u32[]{:S(2)}) async-start(bf16[128,32,768]{2,1,0:T(8,128)(2,1)} %bitcast.72), calls=%async_computation.1 | async-start | bytes 12582912 | tf_op jit(solution)/shard_map/all_to_all | solution.py:182
  49.3 83.0 %all-gather = bf16[1,2048]{1,0:T(2,128)(2,1)S(1)} all-gather(bf16[1,256]{1,0:T(2,128)(2,1)S(1)} %convert_element_type.60), channel_id=3, replica_groups=mesh['dp'=16,'ctx'=8] {'ctx'}, dimensions={1}, use_global_device_ids=true | all-gather | bytes 4608 | tf_op jit(solution)/shard_map/all_gather | solution.py:203
  139.4 20.0 %scatter_custom_fusion.1 = bf16[2048,768]{1,0:T(8,128)(2,1)S(1)} fusion(s32[4096]{0:T(1024)S(1)} %bitcast.102, bf16[4096,768]{1,0:T(8,128)(2,1)} %bitcast.20, bf16[]{:T(256)} %constant.98.clone.1), kind=kCustom, calls=%fused_computation.14 | custom fusion | bytes 3146240 | tf_op jit(solution)/shard_map/scatter | solution.py:196
  159.5 1.5 fusion.22
  163.7 36.2 %shard_map.175 = (f32[2048,256]{1,0:T(8,128)}, f32[2048,128]{1,0:T(8,128)}, f32[2048,128]{1,0:T(8,128)}) custom-call(s32[64]{0:T(128)} %scatter_custom_fusion.list_ref, s32[8]{0:T(128)} %get-tuple-element.39.count_ref, bf16[2048,256]{1,0:T(8,128)(2,1)} %get-tuple-element.30.q_ref, bf16[2048,256]{1,0:T(8,128)(2,1)} %get-tuple-element.29.g_ref, ...), custom_call_target="tpu_custom_call" | custom-call | tf_op jit(solution)/shard_map/pallas_call | solution.py:107
  199.8 1.6 copy.109
  201.4 1.6 copy.111
  207.2 1.7 convert_element_type.71
  208.9 4.7 %collective-permute-done = bf16[2048,128]{1,0:T(8,128)(2,1)} collective-permute-done((bf16[2048,128]{1,0:T(8,128)(2,1)}, bf16[2048,128]{1,0:T(8,128)(2,1)}, u32[]{:S(2)}, u32[]{:S(2)}) %collective-permute-start) | collective-permute-done | bytes 524320 | tf_op jit(solution)/shard_map/ppermute | solution.py:252
  215.1 17.0 %gather_fusion.4 = bf16[4096,384]{1,0:T(8,128)(2,1)} fusion(bf16[2048,384]{1,0:T(8,128)(2,1)S(1)} %pad_maximum_fusion.1, s32[4096]{0:T(1024)S(1)} %broadcast_clamp_fusion), kind=kCustom, calls=%fused_computation.4 | custom fusion | bytes 6307840 | tf_op jit(solution)/shard_map/gather | solution.py:257
  232.1 12.4 %all-to-all-start.2 = ((bf16[128,32,384]{2,1,0:T(8,128)(2,1)}), bf16[128,32,384]{2,1,0:T(8,128)(2,1)S(1)}, u32[]{:S(2)}, u32[]{:S(2)}) async-start(bf16[128,32,384]{2,1,0:T(8,128)(2,1)} %bitcast.75), calls=%async_computation.2 | async-start | bytes 6291456 | tf_op jit(solution)/shard_map/all_to_all | solution.py:257
  244.6 41.2 %all-to-all-done.2 = bf16[128,32,384]{2,1,0:T(8,128)(2,1)S(1)} async-done(((bf16[128,32,384]{2,1,0:T(8,128)(2,1)}), bf16[128,32,384]{2,1,0:T(8,128)(2,1)S(1)}, u32[]{:S(2)}, u32[]{:S(2)}) %all-to-all-start.2) | async-done | bytes 3145760 | tf_op jit(solution)/shard_map/all_to_all | solution.py:257
  285.8 3.0 copy.115
  288.8 2.9 gather_fusion.5
  294.5 1.9 copy.117
  296.3 3.0 copy.120
  (88 shorter events, 27.7 us)
Async XLA Ops:
  3.1 36.0 %all-to-all-start = ((s32[128,32,1]{1,2,0:T(1,128)}), s32[128,32,1]{1,2,0:T(1,128)S(1)}, u32[]{:S(2)}, u32[]{:S(2)}) async-start(s32[128,32,1]{1,2,0:T(1,128)} %bitcast.5), calls=%async_computation | async-start | bytes 131072 | tf_op jit(solution)/shard_map/all_to_all | solution.py:183
  18.8 1.8 copy-start.4
  18.8 1.8 copy-start.1
  39.1 10.2 %copy-start.2 = (s32[1,256]{1,0:T(1,128)S(1)}, s32[1,256]{1,0:T(1,128)}, u32[]{:S(2)}) copy-start(s32[1,256]{1,0:T(1,128)} %param.22) | copy-start | bytes 3076
  39.1 96.6 %copy-start.5 = (s32[8]{0:T(128)S(1)}, s32[8]{0:T(128)}, u32[]{:S(2)}) copy-start(s32[8]{0:T(128)} %constant.115.clone) | copy-start | bytes 100
  39.1 100.1 %copy-start.3 = (s32[1,16]{1,0:T(1,128)S(1)}, s32[1,16]{1,0:T(1,128)}, u32[]{:S(2)}) copy-start(s32[1,16]{1,0:T(1,128)} %param.21) | copy-start | bytes 196
  39.1 100.3 %all-to-all-start.1 = ((bf16[128,32,768]{2,1,0:T(8,128)(2,1)}), bf16[128,32,768]{2,1,0:T(8,128)(2,1)}, u32[]{:S(2)}, u32[]{:S(2)}) async-start(bf16[128,32,768]{2,1,0:T(8,128)(2,1)} %bitcast.72), calls=%async_computation.1 | async-start | bytes 12582912 | tf_op jit(solution)/shard_map/all_to_all | solution.py:182
  204.7 8.9 %collective-permute-start = (bf16[2048,128]{1,0:T(8,128)(2,1)}, bf16[2048,128]{1,0:T(8,128)(2,1)}, u32[]{:S(2)}, u32[]{:S(2)}) collective-permute-start(bf16[2048,128]{1,0:T(8,128)(2,1)} %pad_maximum_fusion.2), channel_id=1, source_target_pairs={{0,2},{1,3},{2,0},{3,1},{4,6},{5,7},{6,4},{7,5},{8,10},{9,11},{10,... | collective-permute-start | bytes 1572872 | tf_op jit(solution)/shard_map/ppermute | solution.py:252
  232.1 53.6 %all-to-all-start.2 = ((bf16[128,32,384]{2,1,0:T(8,128)(2,1)}), bf16[128,32,384]{2,1,0:T(8,128)(2,1)S(1)}, u32[]{:S(2)}, u32[]{:S(2)}) async-start(bf16[128,32,384]{2,1,0:T(8,128)(2,1)} %bitcast.75), calls=%async_computation.2 | async-start | bytes 6291456 | tf_op jit(solution)/shard_map/all_to_all | solution.py:257
  296.3 3.0 copy-start

commit v7 on v6

--- a/solution.py
+++ b/solution.py
@@ -193,7 +193,8 @@
         axis=1,
     )
     landing = jnp.where(packed_row >= 0, span_pos * span_rows + packed_row % span_rows, pack_len)
-    rows = jnp.zeros((pack_len, width), jnp.bfloat16).at[landing].set(got, mode="drop")
+    lands = jnp.arange(pack_len, dtype=jnp.int32)[:, None] == landing[None, :]
+    rows = jnp.dot(lands.astype(jnp.bfloat16), got, preferred_element_type=jnp.float32).astype(jnp.bfloat16)
     query = rows[:, :q_width]
     grad_rows = rows[:, q_width : 2 * q_width]
     keys = rows[:, 2 * q_width : 2 * q_width + DH]
@@ -252,9 +253,16 @@
     key_value = mine + lax.ppermute(other, "ctx", partner).astype(jnp.float32)
 
     result = jnp.concatenate([dquery.astype(jnp.bfloat16), key_value.astype(jnp.bfloat16)], axis=1)
-    source_rows = jnp.where(landing < pack_len, landing, 0)
     back = (
-        lax.all_to_all(result[source_rows], ("dp", "ctx"), split_axis=0, concat_axis=0, tiled=True)
+        lax.all_to_all(
+            lax.dot_general(
+                lands.astype(jnp.bfloat16), result, (((0,), (0,)), ((), ())), preferred_element_type=jnp.float32
+            ).astype(jnp.bfloat16),
+            ("dp", "ctx"),
+            split_axis=0,
+            concat_axis=0,
+            tiled=True,
+        )
         .reshape(packs, ctx_size, capacity, result.shape[1])
         .transpose(0, 2, 1, 3)
         .reshape(packs * capacity, ctx_size, result.shape[1])

time: 303 us -> 293 us (0.967)
  local copies, waits for them, and re-layouts: 85.5 us -> 47.7 us
  matrix products: 1.83 us -> 29.7 us
    dot_general x0 -> x2, matrix products: none -> 27.9 us  [the longest x1 17.6 us: local(): jnp.dot(lands.astype(jnp.bfloat16), got, preferred_element_type=jnp.float32)]
    scatter x1 -> x0, local copies, waits for them, and re-layouts: 20 us -> none  [local(): jnp.zeros((pack_len, width), jnp.bfloat16).at[landing].set(got, mode='drop')]
    gather x1 -> x0, local copies, waits for them, and re-layouts: 17 us -> none  [local(): result[source_rows]]
    transpose x3 -> x1, local copies, waits for them, and re-layouts: 8.05 us -> 2.98 us  [local(): back = lax.all_to_all(lax.dot_general(lands.astype(jnp.bfloat16), result,...]
    reshape x0 -> x1, local copies, waits for them, and re-layouts: none -> 4.5 us  [local(): holder = jnp.dot(picks.astype(jnp.bfloat16), payload.reshape(local_rows,...]
where the time goes in v7:
time: 293 us; the launch traced here: 292 us
  blocking collectives  83 us (28%)
  local copies, waits for them, and re-layouts  47.7 us (16%)
  waiting for transfers between devices  45.9 us (16%)
  Pallas kernels  36.2 us (12%)
  starting transfers between devices  33.9 us (12%)
  matrix products  29.7 us (10%)
  other arithmetic  11.3 us (4%)
  between operations  3.9 us (1%)
    all_gather x1, blocking collectives, local(): lax.all_gather(doc_block, 'ctx', axis=0, tiled=True)[:, 0].astype(jnp.int32)  83 us
    all_to_all x1, waiting for transfers between devices, local(): lax.all_to_all(lax.dot_general(lands.astype(jnp.bfloat16), result, (((0,)...  41.2 us
    pallas_call x1, Pallas kernels, attention(): pl.pallas_call(attention_kernel, grid_spec=pltpu.PrefetchScalarGridSpec(n...  36.2 us
    dot_general x1, matrix products, local(): jnp.dot(lands.astype(jnp.bfloat16), got, preferred_element_type=jnp.float32)  17.6 us
    all_to_all x1, starting transfers between devices, local(): lax.all_to_all(lax.dot_general(lands.astype(jnp.bfloat16), result, (((0,)...  12.3 us
    unnamed x24, local copies, waits for them, and re-layouts  11.9 us
    all_to_all x1, starting transfers between devices, local(): lax.all_to_all(places, ('dp', 'ctx'), split_axis=0, concat_axis=0, tiled=...  11.5 us
    dot_general x1, matrix products, local(): lax.dot_general(lands.astype(jnp.bfloat16), result, (((0,), (0,)), ((), (...  10.3 us
  transfers between devices with their start and end apart: 4, of which 2 were waited for; matrix products, arithmetic and copies ran while one was open for 11% of the time, Pallas kernels for 0%

profile of v7, /device:TPU:1, one launch (start us, length us, event | category | flops | bytes accessed | tf_op | source)
XLA Modules:
  0.0 291.7 jit_solution(4014069433260385092)
XLA Ops:
  3.1 11.5 %all-to-all-start = ((s32[128,32,1]{1,2,0:T(1,128)}), s32[128,32,1]{1,2,0:T(1,128)S(1)}, u32[]{:S(2)}, u32[]{:S(2)}) async-start(s32[128,32,1]{1,2,0:T(1,128)} %bitcast.2), calls=%async_computation | async-start | bytes 131072 | tf_op jit(solution)/shard_map/all_to_all | solution.py:183
  15.3 1.5 copy.99
  17.3 1.5 copy.97
  24.3 2.7 pad_maximum_fusion
  27.0 3.2 %copy.105 = bf16[256,8,768]{0,2,1:T(8,128)(2,1)S(1)} copy(bf16[256,8,768]{2,0,1:T(8,128)(2,1)} %pad_maximum_fusion) | data formatting | bytes 6291456 | tf_op jit(solution)/shard_map/concatenate | solution.py:155
  30.2 1.8 convolution_convert_fusion
  32.0 2.0 copy.127
  34.0 4.5 %copy.106 = bf16[16,32,8,768]{3,1,2,0:T(8,128)(2,1)} copy(bf16[16,32,8,768]{3,2,1,0:T(8,128)(2,1)S(1)} %bitcast.69) | data formatting | bytes 12582912 | tf_op jit(solution)/shard_map/reshape | solution.py:174
  38.5 10.2 %all-to-all-start.1 = ((bf16[128,32,768]{2,1,0:T(8,128)(2,1)}), bf16[128,32,768]{2,1,0:T(8,128)(2,1)}, u32[]{:S(2)}, u32[]{:S(2)}) async-start(bf16[128,32,768]{2,1,0:T(8,128)(2,1)} %bitcast.67), calls=%async_computation.1 | async-start | bytes 12582912 | tf_op jit(solution)/shard_map/all_to_all | solution.py:182
  48.7 83.0 %all-gather = bf16[1,2048]{1,0:T(2,128)(2,1)S(1)} all-gather(bf16[1,256]{1,0:T(2,128)(2,1)S(1)} %convert_element_type.70), channel_id=3, replica_groups=mesh['dp'=16,'ctx'=8] {'ctx'}, dimensions={1}, use_global_device_ids=true | all-gather | bytes 4608 | tf_op jit(solution)/shard_map/all_gather | solution.py:204
  138.6 17.6 %fusion.5 = bf16[2048,768]{1,0:T(8,128)(2,1)S(1)} fusion(bf16[4096,768]{1,0:T(8,128)(2,1)} %bitcast.18, s32[4096]{0:T(1024)S(1)} %fusion.12), kind=kOutput, calls=%fused_computation.14 | convolution fusion | flops 12894863360 | bytes 9453568 | tf_op jit(solution)/shard_map/dot_general | solution.py:197
  156.3 1.5 fusion.29
  160.4 36.2 %shard_map.175 = (f32[2048,256]{1,0:T(8,128)}, f32[2048,128]{1,0:T(8,128)}, f32[2048,128]{1,0:T(8,128)}) custom-call(s32[64]{0:T(128)} %scatter_custom_fusion.list_ref, s32[8]{0:T(128)} %get-tuple-element.33.count_ref, bf16[2048,256]{1,0:T(8,128)(2,1)} %get-tuple-element.28.q_ref, bf16[2048,256]{1,0:T(8,128)(2,1)} %get-tuple-element.27.g_ref, ...), custom_call_target="tpu_custom_call" | custom-call | tf_op jit(solution)/shard_map/pallas_call | solution.py:107
  196.6 1.6 copy.108
  198.2 1.6 copy.110
  204.0 1.7 convert_element_type.80
  205.7 4.7 %collective-permute-done = bf16[2048,128]{1,0:T(8,128)(2,1)} collective-permute-done((bf16[2048,128]{1,0:T(8,128)(2,1)}, bf16[2048,128]{1,0:T(8,128)(2,1)}, u32[]{:S(2)}, u32[]{:S(2)}) %collective-permute-start) | collective-permute-done | bytes 524320 | tf_op jit(solution)/shard_map/ppermute | solution.py:253
  211.8 10.3 %fusion.4 = bf16[4096,384]{1,0:T(8,128)(2,1)} fusion(s32[4096]{0:T(1024)S(1)} %fusion.12, bf16[2048,128]{1,0:T(8,128)(2,1)S(1)} %fusion.9, bf16[2048,256]{1,0:T(8,128)(2,1)S(1)} %convert_element_type.80), kind=kOutput, calls=%fused_computation.13 | convolution fusion | flops 6455558144 | bytes 4734976 | tf_op jit(solution)/shard_map/dot_general | solution.py:258
  222.0 12.3 %all-to-all-start.2 = ((bf16[128,32,384]{2,1,0:T(8,128)(2,1)}), bf16[128,32,384]{2,1,0:T(8,128)(2,1)S(1)}, u32[]{:S(2)}, u32[]{:S(2)}) async-start(bf16[128,32,384]{2,1,0:T(8,128)(2,1)} %bitcast.84), calls=%async_computation.2 | async-start | bytes 6291456 | tf_op jit(solution)/shard_map/all_to_all | solution.py:257
  234.3 41.2 %all-to-all-done.2 = bf16[128,32,384]{2,1,0:T(8,128)(2,1)S(1)} async-done(((bf16[128,32,384]{2,1,0:T(8,128)(2,1)}), bf16[128,32,384]{2,1,0:T(8,128)(2,1)S(1)}, u32[]{:S(2)}, u32[]{:S(2)}) %all-to-all-start.2) | async-done | bytes 3145760 | tf_op jit(solution)/shard_map/all_to_all | solution.py:257
  275.5 3.0 %copy.114 = bf16[16,32,8,384]{3,2,1,0:T(8,128)(2,1)} copy(bf16[16,32,8,384]{3,1,2,0:T(8,128)(2,1)S(1)} %bitcast.71) | data formatting | bytes 6291456 | tf_op jit(solution)/shard_map/transpose | solution.py:267
  278.5 2.9 gather_fusion.4
  284.2 1.9 copy.116
  286.1 3.0 %copy.119 = f32[256,2048]{1,0:T(8,128)} copy(f32[256,2048]{0,1:T(8,128)} %bitcast.72) | data formatting | bytes 4194304
  (82 shorter events, 26.7 us)
Async XLA Ops:
  3.1 35.4 %all-to-all-start = ((s32[128,32,1]{1,2,0:T(1,128)}), s32[128,32,1]{1,2,0:T(1,128)S(1)}, u32[]{:S(2)}, u32[]{:S(2)}) async-start(s32[128,32,1]{1,2,0:T(1,128)} %bitcast.2), calls=%async_computation | async-start | bytes 131072 | tf_op jit(solution)/shard_map/all_to_all | solution.py:183
  18.8 1.8 copy-start.4
  18.8 1.8 copy-start.1
  38.5 10.2 %copy-start.2 = (s32[1,256]{1,0:T(1,128)S(1)}, s32[1,256]{1,0:T(1,128)}, u32[]{:S(2)}) copy-start(s32[1,256]{1,0:T(1,128)} %param.22) | copy-start | bytes 3076
  38.5 96.6 %copy-start.5 = (s32[8]{0:T(128)S(1)}, s32[8]{0:T(128)}, u32[]{:S(2)}) copy-start(s32[8]{0:T(128)} %constant.112.clone) | copy-start | bytes 100
  38.5 99.9 %copy-start.3 = (s32[1,16]{1,0:T(1,128)S(1)}, s32[1,16]{1,0:T(1,128)}, u32[]{:S(2)}) copy-start(s32[1,16]{1,0:T(1,128)} %param.21) | copy-start | bytes 196
  38.5 100.1 %all-to-all-start.1 = ((bf16[128,32,768]{2,1,0:T(8,128)(2,1)}), bf16[128,32,768]{2,1,0:T(8,128)(2,1)}, u32[]{:S(2)}, u32[]{:S(2)}) async-start(bf16[128,32,768]{2,1,0:T(8,128)(2,1)} %bitcast.67), calls=%async_computation.1 | async-start | bytes 12582912 | tf_op jit(solution)/shard_map/all_to_all | solution.py:182
  201.5 8.9 %collective-permute-start = (bf16[2048,128]{1,0:T(8,128)(2,1)}, bf16[2048,128]{1,0:T(8,128)(2,1)}, u32[]{:S(2)}, u32[]{:S(2)}) collective-permute-start(bf16[2048,128]{1,0:T(8,128)(2,1)} %pad_maximum_fusion.1), channel_id=1, source_target_pairs={{0,2},{1,3},{2,0},{3,1},{4,6},{5,7},{6,4},{7,5},{8,10},{9,11},{10,... | collective-permute-start | bytes 1572872 | tf_op jit(solution)/shard_map/ppermute | solution.py:253
  222.0 53.5 %all-to-all-start.2 = ((bf16[128,32,384]{2,1,0:T(8,128)(2,1)}), bf16[128,32,384]{2,1,0:T(8,128)(2,1)S(1)}, u32[]{:S(2)}, u32[]{:S(2)}) async-start(bf16[128,32,384]{2,1,0:T(8,128)(2,1)} %bitcast.84), calls=%async_computation.2 | async-start | bytes 6291456 | tf_op jit(solution)/shard_map/all_to_all | solution.py:257
  286.1 3.0 %copy-start = (f32[256,8,64]{2,0,1:T(8,128)S(1)}, f32[256,8,64]{2,0,1:T(8,128)}, u32[]{:S(2)}) copy-start(f32[256,8,64]{2,0,1:T(8,128)} %get-tuple-element.24) | copy-start | bytes 1572868

commit v8 on v7

--- a/solution.py
+++ b/solution.py
@@ -12,6 +12,7 @@
 
 
 SPAN_ROWS = 256
+QUERY_ROWS = 512
 
 
 def attention_kernel(
@@ -100,25 +101,27 @@
     keys_len, kv_width = keys.shape
     groups = width // kv_width
     heads = kv_width // DH
-    q_spec = pl.BlockSpec((SPAN_ROWS, groups * DH), lambda c, s, *_: (s, c))
+    q_spec = pl.BlockSpec((QUERY_ROWS, groups * DH), lambda c, s, *_: (s, c))
     k_spec = pl.BlockSpec((keys_len, DH), lambda c, s, *_: (0, c))
-    col_spec = pl.BlockSpec((SPAN_ROWS, 1), lambda c, s, *_: (s, 0))
+    col_spec = pl.BlockSpec((QUERY_ROWS, 1), lambda c, s, *_: (s, 0))
     row_spec = pl.BlockSpec((1, keys_len), lambda c, s, *_: (0, 0))
     return pl.pallas_call(
         attention_kernel,
         grid_spec=pltpu.PrefetchScalarGridSpec(
             num_scalar_prefetch=2,
-            grid=(heads, rows // SPAN_ROWS),
+            grid=(heads, rows // QUERY_ROWS),
             in_specs=[q_spec, q_spec, k_spec, k_spec, col_spec, col_spec, row_spec, row_spec],
             out_specs=[q_spec, k_spec, k_spec],
-            scratch_shapes=[pltpu.VMEM((keys_len // SPAN_ROWS, groups * SPAN_ROWS, SPAN_ROWS), jnp.float32)],
+            scratch_shapes=[pltpu.VMEM((keys_len // SPAN_ROWS, groups * QUERY_ROWS, SPAN_ROWS), jnp.float32)],
         ),
         out_shape=[
             jax.ShapeDtypeStruct((rows, width), jnp.float32),
             jax.ShapeDtypeStruct((keys_len, kv_width), jnp.float32),
             jax.ShapeDtypeStruct((keys_len, kv_width), jnp.float32),
         ],
-        compiler_params=pltpu.CompilerParams(dimension_semantics=("arbitrary", "arbitrary")),
+        compiler_params=pltpu.CompilerParams(
+            dimension_semantics=("arbitrary", "arbitrary"), vmem_limit_bytes=48 * 1024 * 1024
+        ),
         interpret=interpret,
     )(span_list, span_count, query, grad, keys, values, qpos, qdoc, kpos, kdoc)
 
@@ -205,22 +208,23 @@
     positions = jnp.arange(pack_len, dtype=jnp.int32)
 
     spans = pack_len // SPAN_ROWS
+    query_tiles = pack_len // QUERY_ROWS
     tile_docs = doc_all.reshape(spans, SPAN_ROWS)
-    first_doc = tile_docs[:, 0]
-    last_doc = tile_docs[:, -1]
+    query_docs = doc_all.reshape(query_tiles, QUERY_ROWS)
     tile_ids = jnp.arange(spans)
+    query_ids = jnp.arange(query_tiles)
     active = (
-        (tile_ids[None, :] <= tile_ids[:, None])
-        & (first_doc[None, :] <= last_doc[:, None])
-        & (first_doc[:, None] <= last_doc[None, :])
+        (tile_ids[None, :] * SPAN_ROWS < (query_ids[:, None] + 1) * QUERY_ROWS)
+        & (tile_docs[None, :, 0] <= query_docs[:, None, -1])
+        & (query_docs[:, None, 0] <= tile_docs[None, :, -1])
     )
     span_count = jnp.sum(active.astype(jnp.int32), axis=1)
     rank = jnp.cumsum(active.astype(jnp.int32), axis=1) - 1
-    slot_of = jnp.where(active, rank + spans * jnp.arange(spans)[:, None], spans * spans)
+    slot_of = jnp.where(active, rank + spans * query_ids[:, None], spans * query_tiles)
     span_list = (
-        jnp.zeros((spans * spans,), jnp.int32)
+        jnp.zeros((spans * query_tiles,), jnp.int32)
         .at[slot_of.reshape(-1)]
-        .set(jnp.tile(jnp.arange(spans, dtype=jnp.int32), spans), mode="drop")
+        .set(jnp.tile(jnp.arange(spans, dtype=jnp.int32), query_tiles), mode="drop")
     )
     dquery, dkey, dvalue = attention(
         span_list,

time: 293 us -> 287 us (0.980)
  starting transfers between devices: 33.9 us -> 37.7 us
  Pallas kernels: 36.2 us -> 33.1 us
    all_to_all x1, starting transfers between devices: 12.3 us -> 16.1 us  [local(): lax.all_to_all(lax.dot_general(lands.astype(jnp.bfloat16), result, (((0,)...]
    pallas_call x1, Pallas kernels: 36.2 us -> 33.1 us  [attention(): pl.pallas_call(attention_kernel, grid_spec=pltpu.PrefetchScalarGridSpec(n...]
    unnamed x24 -> x26, local copies, waits for them, and re-layouts: 11.9 us -> 12.1 us
  transfers between devices with their start and end apart: 4 -> 4, of which waited for: 2 -> 2; matrix products, arithmetic and copies ran while one was open for 11% -> 12% of each run, Pallas kernels for 0% -> 0%
where the time goes in v8:
time: 287 us
  blocking collectives  83 us (29%)
  local copies, waits for them, and re-layouts  45.3 us (16%)
  waiting for transfers between devices  44 us (15%)
  starting transfers between devices  37.7 us (13%)
  Pallas kernels  33.1 us (12%)
  matrix products  29.7 us (10%)
  other arithmetic  10.2 us (4%)
  between operations  4.33 us (2%)
    all_gather x1, blocking collectives, local(): lax.all_gather(doc_block, 'ctx', axis=0, tiled=True)[:, 0].astype(jnp.int32)  83 us
    all_to_all x1, waiting for transfers between devices, local(): lax.all_to_all(lax.dot_general(lands.astype(jnp.bfloat16), result, (((0,)...  41.2 us
    pallas_call x1, Pallas kernels, attention(): pl.pallas_call(attention_kernel, grid_spec=pltpu.PrefetchScalarGridSpec(n...  33.1 us
    dot_general x1, matrix products, local(): jnp.dot(lands.astype(jnp.bfloat16), got, preferred_element_type=jnp.float32)  17.6 us
    all_to_all x1, starting transfers between devices, local(): lax.all_to_all(lax.dot_general(lands.astype(jnp.bfloat16), result, (((0,)...  16.1 us
    unnamed x26, local copies, waits for them, and re-layouts  12.1 us
    all_to_all x1, starting transfers between devices, local(): lax.all_to_all(places, ('dp', 'ctx'), split_axis=0, concat_axis=0, tiled=...  11.5 us
    dot_general x1, matrix products, local(): lax.dot_general(lands.astype(jnp.bfloat16), result, (((0,), (0,)), ((), (...  10.3 us
  transfers between devices with their start and end apart: 4, of which 2 were waited for; matrix products, arithmetic and copies ran while one was open for 12% of the time, Pallas kernels for 0%

profile of v8, /device:TPU:1, one launch (start us, length us, event | category | flops | bytes accessed | tf_op | source)
XLA Modules:
  0.0 287.4 jit_solution(10465077921759829028)
XLA Ops:
  3.1 11.5 %all-to-all-start = ((s32[128,32,1]{1,2,0:T(1,128)}), s32[128,32,1]{1,2,0:T(1,128)S(1)}, u32[]{:S(2)}, u32[]{:S(2)}) async-start(s32[128,32,1]{1,2,0:T(1,128)} %bitcast.2), calls=%async_computation | async-start | bytes 131072 | tf_op jit(solution)/shard_map/all_to_all | solution.py:186
  15.3 1.5 copy.107
  17.3 1.5 copy.109
  22.9 1.4 gather_fusion.3
  24.3 2.7 pad_maximum_fusion
  27.0 3.2 %copy.115 = bf16[256,8,768]{0,2,1:T(8,128)(2,1)S(1)} copy(bf16[256,8,768]{2,0,1:T(8,128)(2,1)} %pad_maximum_fusion) | data formatting | bytes 6291456 | tf_op jit(solution)/shard_map/concatenate | solution.py:158
  30.2 1.8 convolution_convert_fusion
  32.0 2.0 copy.139
  34.0 4.5 %copy.116 = bf16[16,32,8,768]{3,1,2,0:T(8,128)(2,1)} copy(bf16[16,32,8,768]{3,2,1,0:T(8,128)(2,1)S(1)} %bitcast.73) | data formatting | bytes 12582912 | tf_op jit(solution)/shard_map/reshape | solution.py:177
  38.5 10.2 %all-to-all-start.1 = ((bf16[128,32,768]{2,1,0:T(8,128)(2,1)}), bf16[128,32,768]{2,1,0:T(8,128)(2,1)}, u32[]{:S(2)}, u32[]{:S(2)}) async-start(bf16[128,32,768]{2,1,0:T(8,128)(2,1)} %bitcast.71), calls=%async_computation.1 | async-start | bytes 12582912 | tf_op jit(solution)/shard_map/all_to_all | solution.py:185
  48.7 83.0 %all-gather = bf16[1,2048]{1,0:T(2,128)(2,1)S(1)} all-gather(bf16[1,256]{1,0:T(2,128)(2,1)S(1)} %convert_element_type.76), channel_id=3, replica_groups=mesh['dp'=16,'ctx'=8] {'ctx'}, dimensions={1}, use_global_device_ids=true | all-gather | bytes 4608 | tf_op jit(solution)/shard_map/all_gather | solution.py:207
  133.0 1.4 copy.117.qdoc_ref
  137.6 17.6 %fusion.5 = bf16[2048,768]{1,0:T(8,128)(2,1)S(1)} fusion(bf16[4096,768]{1,0:T(8,128)(2,1)} %bitcast.20, s32[4096]{0:T(1024)S(1)} %fusion.12), kind=kOutput, calls=%fused_computation.14 | convolution fusion | flops 12894863360 | bytes 9453568 | tf_op jit(solution)/shard_map/dot_general | solution.py:200
  156.5 33.1 %shard_map.175 = (f32[2048,256]{1,0:T(8,128)}, f32[2048,128]{1,0:T(8,128)S(1)}, f32[2048,128]{1,0:T(8,128)S(1)}) custom-call(s32[32]{0:T(128)S(1)} %scatter_custom_fusion.list_ref, s32[4]{0:T(128)S(1)} %get-tuple-element.23.count_ref, bf16[2048,256]{1,0:T(8,128)(2,1)S(1)} %get-tuple-element.30.q_ref, bf16[2048,256]{1,0:T(8,128)(2,1)S(1)} %get-tuple-element.29.g_ref, ...), custom_call_target="tpu_custom_call" | custom-call | tf_op jit(solution)/shard_map/pallas_call | solution.py:108
  197.8 1.7 convert_element_type.88
  199.5 2.8 collective-permute-done
  202.3 1.4 fusion.9
  203.7 10.3 %fusion.4 = bf16[4096,384]{1,0:T(8,128)(2,1)} fusion(s32[4096]{0:T(1024)S(1)} %fusion.12, bf16[2048,128]{1,0:T(8,128)(2,1)S(1)} %fusion.9, bf16[2048,256]{1,0:T(8,128)(2,1)S(1)} %convert_element_type.88), kind=kOutput, calls=%fused_computation.13 | convolution fusion | flops 6455558144 | bytes 4734976 | tf_op jit(solution)/shard_map/dot_general | solution.py:262
  214.0 16.1 %all-to-all-start.2 = ((bf16[128,32,384]{2,1,0:T(8,128)(2,1)}), bf16[128,32,384]{2,1,0:T(8,128)(2,1)S(1)}, u32[]{:S(2)}, u32[]{:S(2)}) async-start(bf16[128,32,384]{2,1,0:T(8,128)(2,1)} %bitcast.88), calls=%async_computation.2 | async-start | bytes 6291456 | tf_op jit(solution)/shard_map/all_to_all | solution.py:261
  230.1 41.2 %all-to-all-done.2 = bf16[128,32,384]{2,1,0:T(8,128)(2,1)S(1)} async-done(((bf16[128,32,384]{2,1,0:T(8,128)(2,1)}), bf16[128,32,384]{2,1,0:T(8,128)(2,1)S(1)}, u32[]{:S(2)}, u32[]{:S(2)}) %all-to-all-start.2) | async-done | bytes 3145760 | tf_op jit(solution)/shard_map/all_to_all | solution.py:261
  271.3 3.0 %copy.124 = bf16[16,32,8,384]{3,2,1,0:T(8,128)(2,1)} copy(bf16[16,32,8,384]{3,1,2,0:T(8,128)(2,1)S(1)} %bitcast.75) | data formatting | bytes 6291456 | tf_op jit(solution)/shard_map/transpose | solution.py:271
  274.2 2.9 %gather_fusion.4 = bf16[256,8,384]{2,1,0:T(8,128)(2,1)S(1)} fusion(bf16[512,8,384]{2,1,0:T(8,128)(2,1)} %bitcast.77, s32[1024]{0:T(1024)S(1)} %pad_clamp_fusion), kind=kCustom, calls=%fused_computation.4 | custom fusion | bytes 3146752 | tf_op jit(solution)/shard_map/gather | solution.py:274
  279.9 1.9 copy.126
  281.8 3.0 %copy.129 = f32[256,2048]{1,0:T(8,128)} copy(f32[256,2048]{0,1:T(8,128)} %bitcast.76) | data formatting | bytes 4194304
  (89 shorter events, 23.6 us)
Async XLA Ops:
  3.1 35.4 %all-to-all-start = ((s32[128,32,1]{1,2,0:T(1,128)}), s32[128,32,1]{1,2,0:T(1,128)S(1)}, u32[]{:S(2)}, u32[]{:S(2)}) async-start(s32[128,32,1]{1,2,0:T(1,128)} %bitcast.2), calls=%async_computation | async-start | bytes 131072 | tf_op jit(solution)/shard_map/all_to_all | solution.py:186
  18.8 1.8 copy-start.4
  18.8 1.8 copy-start.1
  38.5 10.2 %copy-start.2 = (s32[1,256]{1,0:T(1,128)S(1)}, s32[1,256]{1,0:T(1,128)}, u32[]{:S(2)}) copy-start(s32[1,256]{1,0:T(1,128)} %param.22) | copy-start | bytes 3076
  38.5 95.9 %copy-start.5 = (s32[8]{0:T(128)S(1)}, s32[8]{0:T(128)}, u32[]{:S(2)}) copy-start(s32[8]{0:T(128)} %constant.115.clone) | copy-start | bytes 100
  38.5 98.9 %copy-start.3 = (s32[1,16]{1,0:T(1,128)S(1)}, s32[1,16]{1,0:T(1,128)}, u32[]{:S(2)}) copy-start(s32[1,16]{1,0:T(1,128)} %param.21) | copy-start | bytes 196
  38.5 99.1 %all-to-all-start.1 = ((bf16[128,32,768]{2,1,0:T(8,128)(2,1)}), bf16[128,32,768]{2,1,0:T(8,128)(2,1)}, u32[]{:S(2)}, u32[]{:S(2)}) async-start(bf16[128,32,768]{2,1,0:T(8,128)(2,1)} %bitcast.71), calls=%async_computation.1 | async-start | bytes 12582912 | tf_op jit(solution)/shard_map/all_to_all | solution.py:185
  192.0 10.3 %collective-permute-start = (bf16[2048,128]{1,0:T(8,128)(2,1)}, bf16[2048,128]{1,0:T(8,128)(2,1)}, u32[]{:S(2)}, u32[]{:S(2)}) collective-permute-start(bf16[2048,128]{1,0:T(8,128)(2,1)} %pad_maximum_fusion.1), channel_id=1, source_target_pairs={{0,2},{1,3},{2,0},{3,1},{4,6},{5,7},{6,4},{7,5},{8,10},{9,11},{10,... | collective-permute-start | bytes 1572872 | tf_op jit(solution)/shard_map/ppermute | solution.py:257
  214.0 57.3 %all-to-all-start.2 = ((bf16[128,32,384]{2,1,0:T(8,128)(2,1)}), bf16[128,32,384]{2,1,0:T(8,128)(2,1)S(1)}, u32[]{:S(2)}, u32[]{:S(2)}) async-start(bf16[128,32,384]{2,1,0:T(8,128)(2,1)} %bitcast.88), calls=%async_computation.2 | async-start | bytes 6291456 | tf_op jit(solution)/shard_map/all_to_all | solution.py:261
  281.8 3.0 %copy-start = (f32[256,8,64]{2,0,1:T(8,128)S(1)}, f32[256,8,64]{2,0,1:T(8,128)}, u32[]{:S(2)}) copy-start(f32[256,8,64]{2,0,1:T(8,128)} %get-tuple-element.26) | copy-start | bytes 1572868

commit v9 on v8

--- a/solution.py
+++ b/solution.py
@@ -257,21 +257,21 @@
     key_value = mine + lax.ppermute(other, "ctx", partner).astype(jnp.float32)
 
     result = jnp.concatenate([dquery.astype(jnp.bfloat16), key_value.astype(jnp.bfloat16)], axis=1)
-    back = (
-        lax.all_to_all(
-            lax.dot_general(
-                lands.astype(jnp.bfloat16), result, (((0,), (0,)), ((), ())), preferred_element_type=jnp.float32
-            ).astype(jnp.bfloat16),
-            ("dp", "ctx"),
-            split_axis=0,
-            concat_axis=0,
-            tiled=True,
-        )
-        .reshape(packs, ctx_size, capacity, result.shape[1])
-        .transpose(0, 2, 1, 3)
-        .reshape(packs * capacity, ctx_size, result.shape[1])
-    )
-    pieces = back[flat_slot][:, ctx_of_block].astype(jnp.float32)
+    back = lax.all_to_all(
+        lax.dot_general(
+            lands.astype(jnp.bfloat16), result, (((0,), (0,)), ((), ())), preferred_element_type=jnp.float32
+        ).astype(jnp.bfloat16),
+        ("dp", "ctx"),
+        split_axis=0,
+        concat_axis=0,
+        tiled=True,
+    ).reshape(packs, ctx_size, capacity, result.shape[1])[:, ctx_of_block]
+    pieces = lax.dot_general(
+        picks.T.reshape(local_rows, packs, capacity).astype(jnp.bfloat16),
+        back,
+        (((1, 2), (0, 2)), ((), ())),
+        preferred_element_type=jnp.float32,
+    )
     return (
         pieces[:, :, :q_width].reshape(local_rows, q_cols),
         pieces[:, :, q_width : q_width + k_width].reshape(local_rows, k_cols),

time: 287 us -> 284 us (0.990)
  local copies, waits for them, and re-layouts: 45.3 us -> 37 us
  starting transfers between devices: 37.7 us -> 43 us
  Pallas kernels: 33.1 us -> 28.9 us
  matrix products: 29.7 us -> 32.7 us
    all_to_all x1, starting transfers between devices: 16.1 us -> 21.4 us  [local(): lax.all_to_all(lax.dot_general(lands.astype(jnp.bfloat16), result, (((0,)...]
    pallas_call x1, Pallas kernels: 33.1 us -> 28.9 us  [attention(): pl.pallas_call(attention_kernel, grid_spec=pltpu.PrefetchScalarGridSpec(n...]
    dot_general x0 -> x1, matrix products: none -> 3 us  [local(): lax.dot_general(picks.T.reshape(local_rows, packs, capacity).astype(jnp.b...]
    transpose x1 -> x0, local copies, waits for them, and re-layouts: 2.98 us -> none  [local(): back = lax.all_to_all(lax.dot_general(lands.astype(jnp.bfloat16), result,...]
    unnamed x26 -> x28, local copies, waits for them, and re-layouts: 12.1 us -> 11.1 us
  transfers between devices with their start and end apart: 4 -> 4, of which waited for: 2 -> 2; matrix products, arithmetic and copies ran while one was open for 12% -> 10% of each run, Pallas kernels for 0% -> 0%
where the time goes in v9:
time: 284 us
  blocking collectives  83 us (29%)
  waiting for transfers between devices  45.1 us (16%)
  starting transfers between devices  43 us (15%)
  local copies, waits for them, and re-layouts  37 us (13%)
  matrix products  32.7 us (12%)
  Pallas kernels  28.9 us (10%)
  other arithmetic  10.1 us (4%)
  between operations  4.32 us (2%)
    all_gather x1, blocking collectives, local(): lax.all_gather(doc_block, 'ctx', axis=0, tiled=True)[:, 0].astype(jnp.int32)  83 us
    all_to_all x1, waiting for transfers between devices, local(): lax.all_to_all(lax.dot_general(lands.astype(jnp.bfloat16), result, (((0,)...  41.2 us
    pallas_call x1, Pallas kernels, attention(): pl.pallas_call(attention_kernel, grid_spec=pltpu.PrefetchScalarGridSpec(n...  28.9 us
    all_to_all x1, starting transfers between devices, local(): lax.all_to_all(lax.dot_general(lands.astype(jnp.bfloat16), result, (((0,)...  21.4 us
    dot_general x1, matrix products, local(): jnp.dot(lands.astype(jnp.bfloat16), got, preferred_element_type=jnp.float32)  17.6 us
    all_to_all x1, starting transfers between devices, local(): lax.all_to_all(places, ('dp', 'ctx'), split_axis=0, concat_axis=0, tiled=...  11.5 us
    unnamed x28, local copies, waits for them, and re-layouts  11.1 us
    dot_general x1, matrix products, local(): lax.dot_general(lands.astype(jnp.bfloat16), result, (((0,), (0,)), ((), (...  10.3 us
  transfers between devices with their start and end apart: 4, of which 2 were waited for; matrix products, arithmetic and copies ran while one was open for 10% of the time, Pallas kernels for 0%

profile of v9, /device:TPU:1, one launch (start us, length us, event | category | flops | bytes accessed | tf_op | source)
XLA Modules:
  0.0 284.3 jit_solution(9399380043904559173)
XLA Ops:
  3.2 11.5 %all-to-all-start = ((s32[128,32,1]{1,2,0:T(1,128)}), s32[128,32,1]{1,2,0:T(1,128)S(1)}, u32[]{:S(2)}, u32[]{:S(2)}) async-start(s32[128,32,1]{1,2,0:T(1,128)} %bitcast.3), calls=%async_computation | async-start | bytes 131072 | tf_op jit(solution)/shard_map/all_to_all | solution.py:186
  15.4 1.5 copy.105
  22.0 1.4 gather_fusion.3
  23.4 2.7 pad_maximum_fusion
  26.2 3.2 %copy.113 = bf16[256,8,768]{0,2,1:T(8,128)(2,1)S(1)} copy(bf16[256,8,768]{2,0,1:T(8,128)(2,1)} %pad_maximum_fusion) | data formatting | bytes 6291456 | tf_op jit(solution)/shard_map/concatenate | solution.py:158
  29.3 1.8 convolution_convert_fusion
  31.2 2.0 copy.136
  33.2 4.5 %copy.114 = bf16[16,32,8,768]{3,1,2,0:T(8,128)(2,1)} copy(bf16[16,32,8,768]{3,2,1,0:T(8,128)(2,1)S(1)} %bitcast.79) | data formatting | bytes 12582912 | tf_op jit(solution)/shard_map/reshape | solution.py:177
  37.7 10.2 %all-to-all-start.1 = ((bf16[128,32,768]{2,1,0:T(8,128)(2,1)}), bf16[128,32,768]{2,1,0:T(8,128)(2,1)}, u32[]{:S(2)}, u32[]{:S(2)}) async-start(bf16[128,32,768]{2,1,0:T(8,128)(2,1)} %bitcast.77), calls=%async_computation.1 | async-start | bytes 12582912 | tf_op jit(solution)/shard_map/all_to_all | solution.py:185
  47.9 83.0 %all-gather = bf16[1,2048]{1,0:T(2,128)(2,1)S(1)} all-gather(bf16[1,256]{1,0:T(2,128)(2,1)S(1)} %convert_element_type.74), channel_id=3, replica_groups=mesh['dp'=16,'ctx'=8] {'ctx'}, dimensions={1}, use_global_device_ids=true | all-gather | bytes 4608 | tf_op jit(solution)/shard_map/all_gather | solution.py:207
  132.1 1.4 copy.115.qdoc_ref
  136.8 17.6 %fusion.5 = bf16[2048,768]{1,0:T(8,128)(2,1)S(1)} fusion(bf16[4096,768]{1,0:T(8,128)(2,1)} %bitcast.21, s32[4096]{0:T(1024)S(1)} %fusion.21), kind=kOutput, calls=%fused_computation.13 | convolution fusion | flops 12894863360 | bytes 9453568 | tf_op jit(solution)/shard_map/dot_general | solution.py:200
  155.7 28.9 %shard_map.175 = (f32[2048,256]{1,0:T(8,128)}, f32[2048,128]{1,0:T(8,128)S(1)}, f32[2048,128]{1,0:T(8,128)S(1)}) custom-call(s32[32]{0:T(128)S(1)} %scatter_custom_fusion.list_ref, s32[4]{0:T(128)S(1)} %get-tuple-element.21.count_ref, bf16[2048,256]{1,0:T(8,128)(2,1)S(1)} %get-tuple-element.28.q_ref, bf16[2048,256]{1,0:T(8,128)(2,1)S(1)} %get-tuple-element.27.g_ref, ...), custom_call_target="tpu_custom_call" | custom-call | tf_op jit(solution)/shard_map/pallas_call | solution.py:108
  189.7 1.7 convert_element_type.86
  191.4 3.9 %collective-permute-done = bf16[2048,128]{1,0:T(8,128)(2,1)} collective-permute-done((bf16[2048,128]{1,0:T(8,128)(2,1)}, bf16[2048,128]{1,0:T(8,128)(2,1)}, u32[]{:S(2)}, u32[]{:S(2)}) %collective-permute-start) | collective-permute-done | bytes 524320 | tf_op jit(solution)/shard_map/ppermute | solution.py:257
  195.3 1.4 fusion.14
  196.7 10.3 %fusion.4 = bf16[4096,384]{1,0:T(8,128)(2,1)} fusion(s32[4096]{0:T(1024)S(1)} %fusion.21, bf16[2048,128]{1,0:T(8,128)(2,1)S(1)} %fusion.14, bf16[2048,256]{1,0:T(8,128)(2,1)S(1)} %convert_element_type.86), kind=kOutput, calls=%fused_computation.12 | convolution fusion | flops 6455558144 | bytes 4734976 | tf_op jit(solution)/shard_map/dot_general | solution.py:261
  207.0 21.4 %all-to-all-start.2 = ((bf16[128,32,384]{2,1,0:T(8,128)(2,1)}), bf16[128,32,384]{2,1,0:T(8,128)(2,1)S(1)}, u32[]{:S(2)}, u32[]{:S(2)}) async-start(bf16[128,32,384]{2,1,0:T(8,128)(2,1)} %bitcast.93), calls=%async_computation.2 | async-start | bytes 6291456 | tf_op jit(solution)/shard_map/all_to_all | solution.py:260
  228.4 41.2 %all-to-all-done.2 = bf16[128,32,384]{2,1,0:T(8,128)(2,1)S(1)} async-done(((bf16[128,32,384]{2,1,0:T(8,128)(2,1)}), bf16[128,32,384]{2,1,0:T(8,128)(2,1)S(1)}, u32[]{:S(2)}, u32[]{:S(2)}) %all-to-all-start.2) | async-done | bytes 3145760 | tf_op jit(solution)/shard_map/all_to_all | solution.py:260
  269.6 2.7 gather_fusion.4
  272.3 3.0 %fusion.8 = f32[256,8,384]{2,0,1:T(8,128)S(1)} fusion(bf16[8,16,32,384]{3,2,1,0:T(8,128)(2,1)} %gather_fusion.4, s32[256]{0:T(256)S(1)} %multiply_add_fusion.1, s32[16,32]{1,0:T(8,128)S(1)} %multiply_add_fusion), kind=kOutput, calls=%fused_computation.17 | convolution fusion | flops 805437440 | bytes 6294528 | tf_op jit(solution)/shard_map/dot_general | solution.py:269
  275.5 1.3 fusion.33
  276.8 1.9 copy.122
  278.7 3.0 %copy.125 = f32[256,2048]{1,0:T(8,128)} copy(f32[256,2048]{0,1:T(8,128)} %bitcast.82) | data formatting | bytes 4194304
  (88 shorter events, 18.5 us)
Async XLA Ops:
  0.6 16.8 %copy-start.1 = (bf16[256,2048]{1,0:T(8,128)(2,1)S(1)}, bf16[256,2048]{1,0:T(8,128)(2,1)}, u32[]{:S(2)}) copy-start(bf16[256,2048]{1,0:T(8,128)(2,1)} %param.19) | copy-start | bytes 3145732
  3.2 34.5 %all-to-all-start = ((s32[128,32,1]{1,2,0:T(1,128)}), s32[128,32,1]{1,2,0:T(1,128)S(1)}, u32[]{:S(2)}, u32[]{:S(2)}) async-start(s32[128,32,1]{1,2,0:T(1,128)} %bitcast.3), calls=%async_computation | async-start | bytes 131072 | tf_op jit(solution)/shard_map/all_to_all | solution.py:186
  17.9 1.8 copy-start.5
  18.0 1.8 copy-start.2
  37.7 10.2 %copy-start.3 = (s32[1,256]{1,0:T(1,128)S(1)}, s32[1,256]{1,0:T(1,128)}, u32[]{:S(2)}) copy-start(s32[1,256]{1,0:T(1,128)} %param.22) | copy-start | bytes 3076
  37.7 95.8 %copy-start.6 = (s32[8]{0:T(128)S(1)}, s32[8]{0:T(128)}, u32[]{:S(2)}) copy-start(s32[8]{0:T(128)} %constant.114.clone) | copy-start | bytes 100
  37.7 98.9 %copy-start.4 = (s32[1,16]{1,0:T(1,128)S(1)}, s32[1,16]{1,0:T(1,128)}, u32[]{:S(2)}) copy-start(s32[1,16]{1,0:T(1,128)} %param.21) | copy-start | bytes 196
  37.7 99.1 %all-to-all-start.1 = ((bf16[128,32,768]{2,1,0:T(8,128)(2,1)}), bf16[128,32,768]{2,1,0:T(8,128)(2,1)}, u32[]{:S(2)}, u32[]{:S(2)}) async-start(bf16[128,32,768]{2,1,0:T(8,128)(2,1)} %bitcast.77), calls=%async_computation.1 | async-start | bytes 12582912 | tf_op jit(solution)/shard_map/all_to_all | solution.py:185
  187.0 8.3 %collective-permute-start = (bf16[2048,128]{1,0:T(8,128)(2,1)}, bf16[2048,128]{1,0:T(8,128)(2,1)}, u32[]{:S(2)}, u32[]{:S(2)}) collective-permute-start(bf16[2048,128]{1,0:T(8,128)(2,1)} %pad_maximum_fusion.1), channel_id=1, source_target_pairs={{0,2},{1,3},{2,0},{3,1},{4,6},{5,7},{6,4},{7,5},{8,10},{9,11},{10,... | collective-permute-start | bytes 1572872 | tf_op jit(solution)/shard_map/ppermute | solution.py:257
  207.0 62.6 %all-to-all-start.2 = ((bf16[128,32,384]{2,1,0:T(8,128)(2,1)}), bf16[128,32,384]{2,1,0:T(8,128)(2,1)S(1)}, u32[]{:S(2)}, u32[]{:S(2)}) async-start(bf16[128,32,384]{2,1,0:T(8,128)(2,1)} %bitcast.93), calls=%async_computation.2 | async-start | bytes 6291456 | tf_op jit(solution)/shard_map/all_to_all | solution.py:260
  278.7 3.0 %copy-start = (f32[256,8,64]{2,0,1:T(8,128)S(1)}, f32[256,8,64]{2,0,1:T(8,128)}, u32[]{:S(2)}) copy-start(f32[256,8,64]{2,0,1:T(8,128)} %get-tuple-element.24) | copy-start | bytes 1572868

commit v10 on v9

--- a/solution.py
+++ b/solution.py
@@ -142,10 +142,8 @@
     q_width = q_cols // ctx_size
     k_width = k_cols // ctx_size
     ctx_ids = np.arange(ctx_size)
-    kv_of = (ctx_ids // 4) * 2 + ctx_ids % 2
-    half_of = (ctx_ids // 2) % 2
-    block_of = 2 * kv_of + half_of
-    ctx_of_block = np.argsort(block_of)
+    kv_of = ctx_ids // 2
+    half_of = ctx_ids % 2
 
     pack_of = target // pack_len
     row_in_pack = target % pack_len
@@ -157,8 +155,8 @@
 
     payload = jnp.concatenate(
         [
-            query_in.reshape(local_rows, ctx_size, q_width)[:, block_of],
-            grad_out.reshape(local_rows, ctx_size, q_width)[:, block_of],
+            query_in.reshape(local_rows, ctx_size, q_width),
+            grad_out.reshape(local_rows, ctx_size, q_width),
             key_in.reshape(local_rows, k_cols // DH, DH)[:, kv_of],
             value_in.reshape(local_rows, k_cols // DH, DH)[:, kv_of],
         ],
@@ -253,7 +251,7 @@
         ],
         axis=1,
     ).astype(jnp.bfloat16)
-    partner = [(int(c), int(c) ^ 2) for c in ctx_ids]
+    partner = [(int(c), int(c) ^ 1) for c in ctx_ids]
     key_value = mine + lax.ppermute(other, "ctx", partner).astype(jnp.float32)
 
     result = jnp.concatenate([dquery.astype(jnp.bfloat16), key_value.astype(jnp.bfloat16)], axis=1)
@@ -265,7 +263,7 @@
         split_axis=0,
         concat_axis=0,
         tiled=True,
-    ).reshape(packs, ctx_size, capacity, result.shape[1])[:, ctx_of_block]
+    ).reshape(packs, ctx_size, capacity, result.shape[1])
     pieces = lax.dot_general(
         picks.T.reshape(local_rows, packs, capacity).astype(jnp.bfloat16),
         back,

time: 284 us -> 274 us (0.965)
  local copies, waits for them, and re-layouts: 37 us -> 28.4 us
    gather x3 -> x0, local copies, waits for them, and re-layouts: 3.89 us -> none  [the longest x1 2.66 us: local(): lax.all_to_all(lax.dot_general(lands.astype(jnp.bfloat16), result, (((0,)...]
    concatenate x1 -> x0, local copies, waits for them, and re-layouts: 3.17 us -> none  [local(): jnp.concatenate([query_in.reshape(local_rows, ctx_size, q_width)[:, block...]
    unnamed x28 -> x29, local copies, waits for them, and re-layouts: 11.1 us -> 10.7 us
  transfers between devices with their start and end apart: 4 -> 4, of which waited for: 2 -> 2; matrix products, arithmetic and copies ran while one was open for 10% -> 8% of each run, Pallas kernels for 0% -> 0%
where the time goes in v10:
time: 274 us
  blocking collectives  83 us (30%)
  waiting for transfers between devices  47.2 us (17%)
  starting transfers between devices  43.7 us (16%)
  matrix products  30.8 us (11%)
  Pallas kernels  28.9 us (11%)
  local copies, waits for them, and re-layouts  28.4 us (10%)
  other arithmetic  7.61 us (3%)
  between operations  4.31 us (2%)
    all_gather x1, blocking collectives, local(): lax.all_gather(doc_block, 'ctx', axis=0, tiled=True)[:, 0].astype(jnp.int32)  83 us
    all_to_all x1, waiting for transfers between devices, local(): lax.all_to_all(lax.dot_general(lands.astype(jnp.bfloat16), result, (((0,)...  41.2 us
    pallas_call x1, Pallas kernels, attention(): pl.pallas_call(attention_kernel, grid_spec=pltpu.PrefetchScalarGridSpec(n...  28.9 us
    all_to_all x1, starting transfers between devices, local(): lax.all_to_all(lax.dot_general(lands.astype(jnp.bfloat16), result, (((0,)...  20.7 us
    dot_general x1, matrix products, local(): jnp.dot(lands.astype(jnp.bfloat16), got, preferred_element_type=jnp.float32)  17.6 us
    all_to_all x1, starting transfers between devices, local(): lax.all_to_all(places, ('dp', 'ctx'), split_axis=0, concat_axis=0, tiled=...  11.5 us
    unnamed x29, local copies, waits for them, and re-layouts  10.7 us
    dot_general x1, matrix products, local(): lax.dot_general(lands.astype(jnp.bfloat16), result, (((0,), (0,)), ((), (...  10.3 us
  transfers between devices with their start and end apart: 4, of which 2 were waited for; matrix products, arithmetic and copies ran while one was open for 8% of the time, Pallas kernels for 0%

profile of v10, /device:TPU:1, one launch (start us, length us, event | category | flops | bytes accessed | tf_op | source)
XLA Modules:
  0.0 274.0 jit_solution(1731261064253731511)
XLA Ops:
  3.2 11.5 %all-to-all-start = ((s32[128,32,1]{1,2,0:T(1,128)}), s32[128,32,1]{1,2,0:T(1,128)S(1)}, u32[]{:S(2)}, u32[]{:S(2)}) async-start(s32[128,32,1]{1,2,0:T(1,128)} %bitcast.3), calls=%async_computation | async-start | bytes 131072 | tf_op jit(solution)/shard_map/all_to_all | solution.py:184
  15.3 1.2 copy.99
  20.9 1.8 convolution_convert_fusion
  22.7 2.0 copy.131
  24.7 4.5 %copy.105 = bf16[16,32,8,768]{3,1,2,0:T(8,128)(2,1)} copy(bf16[16,32,8,768]{3,2,1,0:T(8,128)(2,1)S(1)} %bitcast.80) | data formatting | bytes 12582912 | tf_op jit(solution)/shard_map/reshape | solution.py:175
  29.2 10.2 %all-to-all-start.1 = ((bf16[128,32,768]{2,1,0:T(8,128)(2,1)}), bf16[128,32,768]{2,1,0:T(8,128)(2,1)}, u32[]{:S(2)}, u32[]{:S(2)}) async-start(bf16[128,32,768]{2,1,0:T(8,128)(2,1)} %bitcast.78), calls=%async_computation.1 | async-start | bytes 12582912 | tf_op jit(solution)/shard_map/all_to_all | solution.py:183
  39.4 83.0 %all-gather = bf16[1,2048]{1,0:T(2,128)(2,1)S(1)} all-gather(bf16[1,256]{1,0:T(2,128)(2,1)S(1)} %convert_element_type.74), channel_id=3, replica_groups=mesh['dp'=16,'ctx'=8] {'ctx'}, dimensions={1}, use_global_device_ids=true | all-gather | bytes 4608 | tf_op jit(solution)/shard_map/all_gather | solution.py:205
  123.7 1.4 copy.106.qdoc_ref
  128.3 17.6 %fusion.5 = bf16[2048,768]{1,0:T(8,128)(2,1)S(1)} fusion(bf16[4096,768]{1,0:T(8,128)(2,1)} %bitcast.16, s32[4096]{0:T(1024)S(1)} %fusion.16), kind=kOutput, calls=%fused_computation.10 | convolution fusion | flops 12894863360 | bytes 9453568 | tf_op jit(solution)/shard_map/dot_general | solution.py:198
  146.2 1.1 iota.53.qpos_ref
  147.2 28.9 %shard_map.130 = (f32[2048,256]{1,0:T(8,128)}, f32[2048,128]{1,0:T(8,128)S(1)}, f32[2048,128]{1,0:T(8,128)S(1)}) custom-call(s32[32]{0:T(128)S(1)} %scatter_custom_fusion.list_ref, s32[4]{0:T(128)S(1)} %get-tuple-element.21.count_ref, bf16[2048,256]{1,0:T(8,128)(2,1)S(1)} %get-tuple-element.28.q_ref, bf16[2048,256]{1,0:T(8,128)(2,1)S(1)} %get-tuple-element.27.g_ref, ...), custom_call_target="tpu_custom_call" | custom-call | tf_op jit(solution)/shard_map/pallas_call | solution.py:108
  177.4 1.1 pad_maximum_fusion.1
  178.5 1.4 collective-permute-start
  182.6 1.7 convert_element_type.86
  184.3 6.0 %collective-permute-done = bf16[2048,128]{1,0:T(8,128)(2,1)} collective-permute-done((bf16[2048,128]{1,0:T(8,128)(2,1)}, bf16[2048,128]{1,0:T(8,128)(2,1)}, u32[]{:S(2)}, u32[]{:S(2)}) %collective-permute-start) | collective-permute-done | bytes 524320 | tf_op jit(solution)/shard_map/ppermute | solution.py:255
  190.3 1.4 fusion.9
  191.7 10.3 %fusion.4 = bf16[4096,384]{1,0:T(8,128)(2,1)} fusion(s32[4096]{0:T(1024)S(1)} %fusion.16, bf16[2048,128]{1,0:T(8,128)(2,1)S(1)} %fusion.9, bf16[2048,256]{1,0:T(8,128)(2,1)S(1)} %convert_element_type.86), kind=kOutput, calls=%fused_computation.9 | convolution fusion | flops 6455558144 | bytes 4734976 | tf_op jit(solution)/shard_map/dot_general | solution.py:259
  202.0 20.7 %all-to-all-start.2 = ((bf16[128,32,384]{2,1,0:T(8,128)(2,1)}), bf16[128,32,384]{2,1,0:T(8,128)(2,1)S(1)}, u32[]{:S(2)}, u32[]{:S(2)}) async-start(bf16[128,32,384]{2,1,0:T(8,128)(2,1)} %bitcast.93), calls=%async_computation.2 | async-start | bytes 6291456 | tf_op jit(solution)/shard_map/all_to_all | solution.py:258
  222.7 41.2 %all-to-all-done.2 = bf16[128,32,384]{2,1,0:T(8,128)(2,1)S(1)} async-done(((bf16[128,32,384]{2,1,0:T(8,128)(2,1)}), bf16[128,32,384]{2,1,0:T(8,128)(2,1)S(1)}, u32[]{:S(2)}, u32[]{:S(2)}) %all-to-all-start.2) | async-done | bytes 3145760 | tf_op jit(solution)/shard_map/all_to_all | solution.py:258
  263.9 1.1 convolution_bitcast_fusion
  265.2 1.3 fusion.28
  266.5 1.9 copy.114
  268.4 3.0 %copy.117 = f32[256,2048]{1,0:T(8,128)} copy(f32[256,2048]{0,1:T(8,128)} %bitcast.83) | data formatting | bytes 4194304
  271.7 1.0 copy.118
  (84 shorter events, 14.6 us)
Async XLA Ops:
  0.6 17.1 %copy-start.3 = (bf16[256,512]{1,0:T(8,128)(2,1)S(1)}, bf16[256,512]{1,0:T(8,128)(2,1)}, u32[]{:S(2)}) copy-start(bf16[256,512]{1,0:T(8,128)(2,1)} %param.13) | copy-start | bytes 786436
  3.2 26.1 %all-to-all-start = ((s32[128,32,1]{1,2,0:T(1,128)}), s32[128,32,1]{1,2,0:T(1,128)S(1)}, u32[]{:S(2)}, u32[]{:S(2)}) async-start(s32[128,32,1]{1,2,0:T(1,128)} %bitcast.3), calls=%async_computation | async-start | bytes 131072 | tf_op jit(solution)/shard_map/all_to_all | solution.py:184
  15.3 3.7 %copy-start.1 = (bf16[256,2048]{1,0:T(8,128)(2,1)S(1)}, bf16[256,2048]{1,0:T(8,128)(2,1)}, u32[]{:S(2)}) copy-start(bf16[256,2048]{1,0:T(8,128)(2,1)} %param.11) | copy-start | bytes 3145732
  17.3 2.0 copy-start.2
  29.2 10.2 %copy-start.4 = (s32[1,256]{1,0:T(1,128)S(1)}, s32[1,256]{1,0:T(1,128)}, u32[]{:S(2)}) copy-start(s32[1,256]{1,0:T(1,128)} %param.17) | copy-start | bytes 3076
  29.2 95.9 %copy-start.6 = (s32[8]{0:T(128)S(1)}, s32[8]{0:T(128)}, u32[]{:S(2)}) copy-start(s32[8]{0:T(128)} %constant.110.clone) | copy-start | bytes 100
  29.2 98.9 %copy-start.5 = (s32[1,16]{1,0:T(1,128)S(1)}, s32[1,16]{1,0:T(1,128)}, u32[]{:S(2)}) copy-start(s32[1,16]{1,0:T(1,128)} %param.16) | copy-start | bytes 196
  29.2 99.1 %all-to-all-start.1 = ((bf16[128,32,768]{2,1,0:T(8,128)(2,1)}), bf16[128,32,768]{2,1,0:T(8,128)(2,1)}, u32[]{:S(2)}, u32[]{:S(2)}) async-start(bf16[128,32,768]{2,1,0:T(8,128)(2,1)} %bitcast.78), calls=%async_computation.1 | async-start | bytes 12582912 | tf_op jit(solution)/shard_map/all_to_all | solution.py:183
  178.5 11.8 %collective-permute-start = (bf16[2048,128]{1,0:T(8,128)(2,1)}, bf16[2048,128]{1,0:T(8,128)(2,1)}, u32[]{:S(2)}, u32[]{:S(2)}) collective-permute-start(bf16[2048,128]{1,0:T(8,128)(2,1)} %pad_maximum_fusion.1), channel_id=1, source_target_pairs={{0,1},{1,0},{2,3},{3,2},{4,5},{5,4},{6,7},{7,6},{8,9},{9,8},{10,11... | collective-permute-start | bytes 1572872 | tf_op jit(solution)/shard_map/ppermute | solution.py:255
  202.0 61.9 %all-to-all-start.2 = ((bf16[128,32,384]{2,1,0:T(8,128)(2,1)}), bf16[128,32,384]{2,1,0:T(8,128)(2,1)S(1)}, u32[]{:S(2)}, u32[]{:S(2)}) async-start(bf16[128,32,384]{2,1,0:T(8,128)(2,1)} %bitcast.93), calls=%async_computation.2 | async-start | bytes 6291456 | tf_op jit(solution)/shard_map/all_to_all | solution.py:258
  268.4 3.0 %copy-start = (f32[256,8,64]{2,0,1:T(8,128)S(1)}, f32[256,8,64]{2,0,1:T(8,128)}, u32[]{:S(2)}) copy-start(f32[256,8,64]{2,0,1:T(8,128)} %get-tuple-element.24) | copy-start | bytes 1572868
